TPU v7x, 256 devices: a whole 4x4x8 slice. The times are simulated.
256 devices in a mesh: req: 32 (over z, x_lo, core), tp: 8 (over x_hi, y).
Axes of the slice: x: 4 (x_hi: 2, x_lo: 2; x = x_hi * 2 + x_lo), y: 4, z: 8, core: 2. Of those that a mesh axis runs over, the one named last changes fastest.
Arguments:
- queries: bfloat16 [12288, 8192], P('req', 'tp'), may hold values from -40 to 40
- suffix_kv: bfloat16 [2, 12288, 1024], P(None, 'req', 'tp'), may hold values from -4 to 4
- prefix_kv: bfloat16 [2, 32, 256, 1024], P(None, 'req', 'tp'), may hold values from -4 to 4
- suffix_length: int32 [31], replicated, may hold values from 16 to 384, as said below
- request_group: int32 [31], replicated, may hold values from 0 to 3
- request_order: int32 [31], replicated, may hold values from 0 to 30, each once
- owner_map: int32 [32], replicated, may hold values from 0 to 31, each once
Outputs:
- attention: bfloat16 [12288, 8192], P('req', 'tp')
Inputs may be any that keep to these rules, and one draw needn't show every extreme that they name: `suffix_length`: every suffix has 16 to 384 tokens; in every draw one suffix has exactly 384 tokens and one exactly 16.
All inputs are finite; a program needn't handle non-finite values.
Results may differ from a plain program's by a relative error of at most 0.007.
Values may be sent and summed in bfloat16 or wider, within the bound.
No kernel may reach another device: no remote copies, remote signals or barrier semaphores. Data moves between devices by JAX's collectives and lax.ppermute only.
A program may use at most 128 MiB of HBM per device.

v0:
```python
import functools
import math

import jax
import jax.numpy as jnp
from jax import lax
from jax.experimental import pallas as pl
from jax.experimental.pallas import tpu as pltpu
from jax.sharding import PartitionSpec as P

QH = 64
KVH = 8
HD = 128
GROUPS = 4

masked_score = -1e30
TILE = 64
CHUNK = 512


def from_behind(block, axis, distance):
    devices = range(lax.axis_size(axis))
    route = [(i - distance, i) for i in devices if i - distance in devices]
    return lax.ppermute(block, axis, route)


def ring_gather(block, wanted):
    n = lax.axis_size("req")
    r = lax.axis_index("req")
    core = r % 2
    pair = (r // 2) % 2
    n_z = n // 4
    reach = n_z // 2

    def route(fn):
        return [(i, fn(i) % n) for i in range(n)]

    other = lax.ppermute(block, "req", route(lambda i: i ^ 1))
    two = jnp.where(core == 0, jnp.concatenate([block, other], 1), jnp.concatenate([other, block], 1))
    other = lax.ppermute(two, "req", route(lambda i: i ^ 2))
    four = jnp.where(pair == 0, jnp.concatenate([two, other], 1), jnp.concatenate([other, two], 1))
    walked = [four]
    for _ in range(reach):
        walked.append(
            lax.ppermute(walked[-1], "req", route(lambda i: i + 4 if i % 2 == 0 else i - 4))
        )
    swapped = lax.ppermute(jnp.concatenate(walked[1:reach], 1), "req", route(lambda i: i ^ 1))
    stored = jnp.concatenate(walked + [swapped], 1)
    z = r // 4
    o = (wanted // 4 - z) % n_z
    p0 = jnp.where(o == 0, 0, jnp.where(o >= reach, n_z - o, reach + o))
    p1 = jnp.where(o <= reach, o, reach + n_z - o)
    return stored, jnp.where(core == 0, p0, p1) * 4 + wanted % 4


def attend_kernel(
    scal_ref, q_ref, stored_ref, s0_ref, s1_ref, o_ref, buf, sems, *, per_kv, half, n_blocks
):
    h = pl.program_id(0)
    i = pl.program_id(1)
    base = scal_ref[0]
    start = jnp.where(h == 0, scal_ref[1], scal_ref[3])
    stop = jnp.where(h == 0, scal_ref[2], scal_ref[4])
    slot0 = base + h * half + i * TILE
    any_live = (start < slot0 + TILE) & (stop > slot0)
    rows = per_kv * TILE
    scale = 1.0 / math.sqrt(HD)
    block_rows = stored_ref.shape[2]

    def block_copy(hh, b):
        src = stored_ref.at[:, scal_ref[8 + hh * n_blocks + b]]
        dst = buf.at[hh, :, pl.ds(b * block_rows, block_rows), :]
        return pltpu.make_async_copy(src, dst, sems.at[hh, b])

    @pl.when((h == 0) & (i == 0))
    def _():
        for hh in range(2):
            for b in range(n_blocks):
                block_copy(hh, b).start()

    @pl.when(jnp.logical_not(any_live))
    def _():
        o_ref[...] = jnp.zeros_like(o_ref)

    def body(hh, s_ref, key_base, n_suffix):
        @pl.when(i == 0)
        def _():
            for b in range(n_blocks):
                block_copy(hh, b).wait()

        @pl.when(any_live)
        def _():
            compute(hh, s_ref, key_base, n_suffix)

    def compute(hh, s_ref, key_base, n_suffix):
        kref = buf.at[hh, 0]
        vref = buf.at[hh, 1]
        q = jnp.concatenate([q_ref[:, j * HD : (j + 1) * HD] for j in range(per_kv)], axis=0)
        row = lax.broadcasted_iota(jnp.int32, (rows, 1), 0)
        slot = slot0 + jnp.bitwise_and(row, TILE - 1)
        live = (slot >= start) & (slot < stop)
        key_slot = key_base + lax.broadcasted_iota(jnp.int32, (1, n_suffix), 1)
        suffix_ok = (key_slot >= start) & (key_slot <= slot) & live

        def raw(k):
            return lax.dot_general(
                q, k, (((1,), (1,)), ((), ())), preferred_element_type=jnp.float32
            )

        n_chunks = kref.shape[0] // CHUNK

        def max_step(c, m):
            s = raw(kref[pl.ds(pl.multiple_of(c * CHUNK, CHUNK), CHUNK), :])
            return jnp.maximum(m, jnp.max(s, axis=1, keepdims=True))

        m = jnp.full((rows, 1), masked_score, jnp.float32)
        m = lax.fori_loop(0, n_chunks, max_step, m)
        s_suf = raw(s_ref[0]) * scale
        m = jnp.maximum(m * scale, jnp.max(jnp.where(suffix_ok, s_suf, masked_score), axis=1, keepdims=True))

        def sum_step(c, carry):
            l, acc = carry
            at = pl.ds(pl.multiple_of(c * CHUNK, CHUNK), CHUNK)
            p = jnp.exp(raw(kref[at, :]) * scale - m)
            l = l + jnp.sum(p, axis=1, keepdims=True)
            acc = acc + jnp.dot(
                p.astype(jnp.bfloat16), vref[at, :], preferred_element_type=jnp.float32
            )
            return (l, acc)

        l = jnp.zeros((rows, 1), jnp.float32)
        acc = jnp.zeros((rows, HD), jnp.float32)
        l, acc = lax.fori_loop(0, n_chunks, sum_step, (l, acc))
        p = jnp.where(suffix_ok, jnp.exp(s_suf - m), 0.0)
        l = l + jnp.sum(p, axis=1, keepdims=True)
        acc = acc + jnp.dot(p.astype(jnp.bfloat16), s_ref[1], preferred_element_type=jnp.float32)
        out = jnp.where(live, acc / jnp.where(live, l, 1.0), 0.0).astype(o_ref.dtype)
        for j in range(per_kv):
            o_ref[:, j * HD : (j + 1) * HD] = out[j * TILE : (j + 1) * TILE, :]

    @pl.when(h == 0)
    def _():
        body(0, s0_ref, base - half, s0_ref.shape[1])

    @pl.when(h == 1)
    def _():
        body(1, s1_ref, base + half, s1_ref.shape[1])


def per_device(
    queries, suffix_kv, prefix_kv, suffix_length, request_group, request_order, owner_map
):
    tok_rows = queries.shape[0]
    head_cols = suffix_kv.shape[2]
    kv_heads = head_cols // HD
    per_kv = queries.shape[1] // head_cols
    stored_count = owner_map.shape[0]
    per_group = stored_count // GROUPS
    requests = suffix_length.shape[0]
    half = tok_rows // 2
    packed_length = jnp.take(suffix_length, request_order)
    packed_group = jnp.take(request_group, request_order)
    starts = (jnp.arange(requests, dtype=jnp.int32) + 1) * tok_rows - packed_length // 2
    stops = starts + packed_length
    device = lax.axis_index("req")
    base = device * tok_rows
    first = jnp.clip(device - 1, 0, requests - 1)
    second = jnp.clip(device, 0, requests - 1)
    has_first = device >= 1
    has_second = device < requests
    start0 = jnp.where(has_first, starts[first], -1)
    stop0 = jnp.where(has_first, stops[first], -1)
    start1 = jnp.where(has_second, starts[second], -1)
    stop1 = jnp.where(has_second, stops[second], -1)
    groups = jnp.stack([packed_group[first], packed_group[second]])
    rows_of = jnp.take(
        owner_map, groups[:, None] * per_group + jnp.arange(per_group, dtype=jnp.int32)[None, :]
    )
    head = jnp.stack([base, start0, stop0, start1, stop1, base, base, base])

    local = lax.all_to_all(prefix_kv, "tp", split_axis=3, concat_axis=2, tiled=True)
    stored, where_block = ring_gather(local, rows_of.reshape(-1))
    scal = jnp.concatenate([head, where_block]).astype(jnp.int32)
    earlier = from_behind(suffix_kv[:, half:, :], "req", 1)
    s0 = jnp.concatenate([earlier, suffix_kv[:, :half, :]], axis=1)
    pad = (-half) % 128
    s1 = jnp.concatenate(
        [suffix_kv[:, half:, :], jnp.zeros((2, pad, head_cols), suffix_kv.dtype)], axis=1
    )

    tiles_per_half = half // TILE
    grid = (2, tiles_per_half)
    kernel = functools.partial(attend_kernel, per_kv=per_kv, half=half, n_blocks=per_group)
    block_rows = stored.shape[2]
    prefix_rows = per_group * block_rows
    tile_map = lambda h, i, s: (h * tiles_per_half + i, 0)
    return pl.pallas_call(
        kernel,
        out_shape=jax.ShapeDtypeStruct((tok_rows, per_kv * HD), queries.dtype),
        grid_spec=pltpu.PrefetchScalarGridSpec(
            num_scalar_prefetch=1,
            grid=grid,
            in_specs=[
                pl.BlockSpec((TILE, per_kv * HD), tile_map),
                pl.BlockSpec(memory_space=pl.ANY),
                pl.BlockSpec(s0.shape, lambda h, i, s: (0, 0, 0)),
                pl.BlockSpec(s1.shape, lambda h, i, s: (0, 0, 0)),
            ],
            out_specs=pl.BlockSpec((TILE, per_kv * HD), tile_map),
            scratch_shapes=[
                pltpu.VMEM((2, 2, prefix_rows, HD), stored.dtype),
                pltpu.SemaphoreType.DMA((2, per_group)),
            ],
        ),
        compiler_params=pltpu.CompilerParams(dimension_semantics=("arbitrary", "arbitrary")),
    )(scal, queries, stored, s0, s1)


def solution(mesh):
    in_specs = (
        P("req", "tp"),
        P(None, "req", "tp"),
        P(None, "req", "tp", None),
        P(),
        P(),
        P(),
        P(),
    )
    out_specs = P("req", "tp")
    return jax.shard_map(
        per_device, mesh=mesh, in_specs=in_specs, out_specs=out_specs, check_vma=False
    )
```

profile of v0, /device:TPU:98, one launch (start us, length us, event | category | flops | bytes accessed | tf_op | source)
XLA Modules:
  0.0 110.1 jit_solution(11365014557727261142)
XLA Ops:
  0.0 1.2 %copy.15 = bf16[2,1,32,1024]{2,0,1,3:T(2,128)(2,1)S(1)} copy(bf16[2,1,32,1024]{3,2,1,0:T(8,128)(2,1)} %param.11) | data formatting | bytes 262144 | tf_op args[2]
  1.8 13.9 %all_to_all.18 = bf16[8,2,4096]{2,1,0:T(2,128)(2,1)S(1)} all-to-all(bf16[8,2,4096]{2,1,0:T(2,128)(2,1)S(1)} %reshape.109), channel_id=1, replica_groups=mesh['req'=32,'tp'=8] {'tp'}, dimensions={0} | all-to-all | bytes 262144 | tf_op jit(solution)/shard_map/all_to_all | solution.py:181
  16.5 1.3 %collective-permute-done = bf16[2,1,256,128]{3,2,1,0:T(8,128)(2,1)S(1)} collective-permute-done((bf16[2,1,256,128]{3,2,1,0:T(8,128)(2,1)S(1)}, bf16[2,1,256,128]{3,2,1,0:T(8,128)(2,1)S(1)}, u32[]{:S(2)}, u32[]{:S(2)}) %collective-permute-start) | collective-permute-done | bytes 131104 | tf_op jit(solution)/shard_map/ppermute | solution.py:38
  17.8 1.5 %collective-permute-start.1 = (bf16[2,2,256,128]{3,2,1,0:T(8,128)(2,1)S(1)}, bf16[2,2,256,128]{3,2,1,0:T(8,128)(2,1)S(1)}, u32[]{:S(2)}, u32[]{:S(2)}) collective-permute-start(bf16[2,2,256,128]{3,2,1,0:T(8,128)(2,1)S(1)} %maximum_select_fusion.1), channel_id=1, source_target_pairs={{0,16},{8,24},{16,0},{24,8},{32,48},{40,56},{48,32},{56,40},{64,80... | collective-permute-start | bytes 786440 | tf_op jit(solution)/shard_map/ppermute | solution.py:40
  19.3 6.9 %collective-permute-done.1 = bf16[2,2,256,128]{3,2,1,0:T(8,128)(2,1)S(1)} collective-permute-done((bf16[2,2,256,128]{3,2,1,0:T(8,128)(2,1)S(1)}, bf16[2,2,256,128]{3,2,1,0:T(8,128)(2,1)S(1)}, u32[]{:S(2)}, u32[]{:S(2)}) %collective-permute-start.1) | collective-permute-done | bytes 262176 | tf_op jit(solution)/shard_map/ppermute | solution.py:40
  26.3 1.0 constant_dynamic-update-slice_fusion.5
  27.3 3.1 %collective-permute-start.2 = (bf16[2,4,256,128]{3,2,1,0:T(8,128)(2,1)S(1)}, bf16[2,4,256,128]{3,2,1,0:T(8,128)(2,1)S(1)}, u32[]{:S(2)}, u32[]{:S(2)}) collective-permute-start(bf16[2,4,256,128]{3,2,1,0:T(8,128)(2,1)S(1)} %get-tuple-element.7), channel_id=1, source_target_pairs={{0,32},{8,232},{16,48},{24,248},{32,64},{40,8},{48,80},{56,24},{64... | collective-permute-start | bytes 1572872 | tf_op jit(solution)/shard_map/ppermute | solution.py:45
  30.4 6.7 %collective-permute-done.2 = bf16[2,4,256,128]{3,2,1,0:T(8,128)(2,1)S(1)} collective-permute-done((bf16[2,4,256,128]{3,2,1,0:T(8,128)(2,1)S(1)}, bf16[2,4,256,128]{3,2,1,0:T(8,128)(2,1)S(1)}, u32[]{:S(2)}, u32[]{:S(2)}) %collective-permute-start.2) | collective-permute-done | bytes 524320 | tf_op jit(solution)/shard_map/ppermute | solution.py:45
  37.1 3.7 %collective-permute-start.3 = (bf16[2,4,256,128]{3,2,1,0:T(8,128)(2,1)S(1)}, bf16[2,4,256,128]{3,2,1,0:T(8,128)(2,1)S(1)}, u32[]{:S(2)}, u32[]{:S(2)}) collective-permute-start(bf16[2,4,256,128]{3,2,1,0:T(8,128)(2,1)S(1)} %collective-permute-done.2), channel_id=1, source_target_pairs={{0,32},{8,232},{16,48},{24,248},{32,64},{40,8},{48,80},{56,24},{64... | collective-permute-start | bytes 1572872 | tf_op jit(solution)/shard_map/ppermute | solution.py:45
  40.8 6.7 %collective-permute-done.3 = bf16[2,4,256,128]{3,2,1,0:T(8,128)(2,1)S(1)} collective-permute-done((bf16[2,4,256,128]{3,2,1,0:T(8,128)(2,1)S(1)}, bf16[2,4,256,128]{3,2,1,0:T(8,128)(2,1)S(1)}, u32[]{:S(2)}, u32[]{:S(2)}) %collective-permute-start.3) | collective-permute-done | bytes 524320 | tf_op jit(solution)/shard_map/ppermute | solution.py:45
  47.5 3.7 %collective-permute-start.4 = (bf16[2,4,256,128]{3,2,1,0:T(8,128)(2,1)S(1)}, bf16[2,4,256,128]{3,2,1,0:T(8,128)(2,1)S(1)}, u32[]{:S(2)}, u32[]{:S(2)}) collective-permute-start(bf16[2,4,256,128]{3,2,1,0:T(8,128)(2,1)S(1)} %collective-permute-done.3), channel_id=1, source_target_pairs={{0,32},{8,232},{16,48},{24,248},{32,64},{40,8},{48,80},{56,24},{64... | collective-permute-start | bytes 1572872 | tf_op jit(solution)/shard_map/ppermute | solution.py:45
  51.2 1.9 %collective-permute-start.7 = (bf16[2,192,128]{2,1,0:T(8,128)(2,1)S(1)}, bf16[2,192,128]{2,1,0:T(8,128)(2,1)S(1)}, u32[]{:S(2)}, u32[]{:S(2)}) collective-permute-start(bf16[2,192,128]{2,1,0:T(8,128)(2,1)S(1)} %get-tuple-element.12), channel_id=1, source_target_pairs={{0,8},{8,16},{16,24},{24,32},{32,40},{40,48},{48,56},{56,64},{64,7... | collective-permute-start | bytes 294920 | tf_op jit(solution)/shard_map/ppermute | solution.py:24
  53.2 0.7 gather_fusion.2
  53.9 5.1 %collective-permute-done.4 = bf16[2,4,256,128]{3,2,1,0:T(8,128)(2,1)S(1)} collective-permute-done((bf16[2,4,256,128]{3,2,1,0:T(8,128)(2,1)S(1)}, bf16[2,4,256,128]{3,2,1,0:T(8,128)(2,1)S(1)}, u32[]{:S(2)}, u32[]{:S(2)}) %collective-permute-start.4) | collective-permute-done | bytes 524320 | tf_op jit(solution)/shard_map/ppermute | solution.py:45
  58.9 1.4 %pad_maximum_fusion = bf16[2,12,256,128]{3,2,1,0:T(8,128)(2,1)} fusion(bf16[2,4,256,128]{3,2,1,0:T(8,128)(2,1)S(1)} %collective-permute-done.4, bf16[2,4,256,128]{3,2,1,0:T(8,128)(2,1)S(1)} %collective-permute-done.3, bf16[2,4,256,128]{3,2,1,0:T(8,128)(2,1)S(1)} %collective-permute-done.2), kind=kLoop, calls=%fused_computation.3 | loop fusion | flops 1572864 | bytes 3145728 | tf_op jit(solution)/shard_map/concatenate | solution.py:47
  60.3 0.7 gather_fusion.1
  61.7 1.4 %add_multiply_fusion = s32[2]{0:T(128)S(1)} fusion(s32[1]{0:T(128)} %get-tuple-element.15, s32[1]{0:T(128)} %get-tuple-element.14), kind=kLoop, calls=%fused_computation.38 | loop fusion | flops 4 | bytes 16 | tf_op jit(solution)/shard_map/mul | solution.py:177
  64.2 3.8 %collective-permute-start.5 = (bf16[2,4,256,128]{3,2,1,0:T(8,128)(2,1)S(1)}, bf16[2,4,256,128]{3,2,1,0:T(8,128)(2,1)}, u32[]{:S(2)}, u32[]{:S(2)}) collective-permute-start(bf16[2,4,256,128]{3,2,1,0:T(8,128)(2,1)S(1)} %collective-permute-done.4), channel_id=1, source_target_pairs={{0,32},{8,232},{16,48},{24,248},{32,64},{40,8},{48,80},{56,24},{64... | collective-permute-start | bytes 1572872 | tf_op jit(solution)/shard_map/ppermute | solution.py:45
  73.2 0.9 constant_dynamic-update-slice_fusion.4
  74.1 0.9 constant_dynamic-update-slice_fusion.3
  75.0 0.9 constant_dynamic-update-slice_fusion.2
  75.8 1.9 %constant_dynamic-update-slice_fusion.1 = bf16[2,32,256,128]{3,2,1,0:T(8,128)(2,1)} fusion(bf16[2,32,256,128]{3,2,1,0:T(8,128)(2,1)} %constant_dynamic-update-slice_fusion.2, bf16[2,4,256,128]{3,2,1,0:T(8,128)(2,1)} %collective-permute-done.5), kind=kLoop, calls=%fused_computation.8 | loop fusion | bytes 1048576
  77.8 1.4 %constant_dynamic-update-slice_fusion.stored_ref = bf16[2,32,256,128]{3,2,1,0:T(8,128)(2,1)} fusion(bf16[2,32,256,128]{3,2,1,0:T(8,128)(2,1)} %constant_dynamic-update-slice_fusion.1, bf16[2,12,256,128]{3,2,1,0:T(8,128)(2,1)S(1)} %collective-permute-done.6), kind=kLoop, calls=%fused_computation.7 | loop fusion | bytes 3145728 | tf_op jit(solution)/shard_map/concatenate | solution.py:48
  79.2 30.9 %shard_map.73 = bf16[384,1024]{1,0:T(8,128)(2,1)} custom-call(s32[24]{0:T(128)} %concatenate.31.scal_ref, bf16[384,1024]{1,0:T(8,128)(2,1)} %q_ref.1, bf16[2,32,256,128]{3,2,1,0:T(8,128)(2,1)} %constant_dynamic-update-slice_fusion.stored_ref, bf16[2,384,128]{2,1,0:T(8,128)(2,1)} %pad_maximum_fusion.1.s0_ref, bf16[2,256,128]{2,1,0:T(8,128)(2,1)} %concatenate.39.s1_ref), custom_call_target="tpu_custom_call" | custom-call | tf_op jit(solution)/shard_map/pallas_call | solution.py:197
  (38 shorter events, 5.8 us)
Async XLA Ops:
  0.0 53.2 %copy-start = (s32[31]{0:T(128)S(1)}, s32[31]{0:T(128)}, u32[]{:S(2)}) copy-start(s32[31]{0:T(128)} %param.13) | copy-start | bytes 376
  0.0 51.2 %copy-start.3 = (bf16[2,384,128]{2,1,0:T(8,128)(2,1)S(1)}, bf16[2,384,128]{2,1,0:T(8,128)(2,1)}, u32[]{:S(2)}) copy-start(bf16[2,384,128]{2,1,0:T(8,128)(2,1)} %param.10) | copy-start | bytes 589828
  0.0 53.1 %copy-start.4 = (s32[31]{0:T(128)S(1)}, s32[31]{0:T(128)}, u32[]{:S(2)}) copy-start(s32[31]{0:T(128)} %param.14) | copy-start | bytes 376
  1.3 59.1 %copy-start.2 = (s32[31]{0:T(128)S(1)}, s32[31]{0:T(128)}, u32[]{:S(2)}) copy-start(s32[31]{0:T(128)} %param.12) | copy-start | bytes 376
  1.8 61.7 %copy-start.1 = (s32[32]{0:T(128)S(1)}, s32[32]{0:T(128)}, u32[]{:S(2)}) copy-start(s32[32]{0:T(128)} %param.15) | copy-start | bytes 388
  16.4 1.4 %collective-permute-start = (bf16[2,1,256,128]{3,2,1,0:T(8,128)(2,1)S(1)}, bf16[2,1,256,128]{3,2,1,0:T(8,128)(2,1)S(1)}, u32[]{:S(2)}, u32[]{:S(2)}) collective-permute-start(bf16[2,1,256,128]{3,2,1,0:T(8,128)(2,1)S(1)} %bitcast.22), channel_id=1, source_target_pairs={{0,8},{8,0},{16,24},{24,16},{32,40},{40,32},{48,56},{56,48},{64,72... | collective-permute-start | bytes 393224 | tf_op jit(solution)/shard_map/ppermute | solution.py:38
  17.8 8.4 %collective-permute-start.1 = (bf16[2,2,256,128]{3,2,1,0:T(8,128)(2,1)S(1)}, bf16[2,2,256,128]{3,2,1,0:T(8,128)(2,1)S(1)}, u32[]{:S(2)}, u32[]{:S(2)}) collective-permute-start(bf16[2,2,256,128]{3,2,1,0:T(8,128)(2,1)S(1)} %maximum_select_fusion.1), channel_id=1, source_target_pairs={{0,16},{8,24},{16,0},{24,8},{32,48},{40,56},{48,32},{56,40},{64,80... | collective-permute-start | bytes 786440 | tf_op jit(solution)/shard_map/ppermute | solution.py:40
  27.3 9.8 %collective-permute-start.2 = (bf16[2,4,256,128]{3,2,1,0:T(8,128)(2,1)S(1)}, bf16[2,4,256,128]{3,2,1,0:T(8,128)(2,1)S(1)}, u32[]{:S(2)}, u32[]{:S(2)}) collective-permute-start(bf16[2,4,256,128]{3,2,1,0:T(8,128)(2,1)S(1)} %get-tuple-element.7), channel_id=1, source_target_pairs={{0,32},{8,232},{16,48},{24,248},{32,64},{40,8},{48,80},{56,24},{64... | collective-permute-start | bytes 1572872 | tf_op jit(solution)/shard_map/ppermute | solution.py:45
  37.1 10.4 %collective-permute-start.3 = (bf16[2,4,256,128]{3,2,1,0:T(8,128)(2,1)S(1)}, bf16[2,4,256,128]{3,2,1,0:T(8,128)(2,1)S(1)}, u32[]{:S(2)}, u32[]{:S(2)}) collective-permute-start(bf16[2,4,256,128]{3,2,1,0:T(8,128)(2,1)S(1)} %collective-permute-done.2), channel_id=1, source_target_pairs={{0,32},{8,232},{16,48},{24,248},{32,64},{40,8},{48,80},{56,24},{64... | collective-permute-start | bytes 1572872 | tf_op jit(solution)/shard_map/ppermute | solution.py:45
  47.5 11.4 %collective-permute-start.4 = (bf16[2,4,256,128]{3,2,1,0:T(8,128)(2,1)S(1)}, bf16[2,4,256,128]{3,2,1,0:T(8,128)(2,1)S(1)}, u32[]{:S(2)}, u32[]{:S(2)}) collective-permute-start(bf16[2,4,256,128]{3,2,1,0:T(8,128)(2,1)S(1)} %collective-permute-done.3), channel_id=1, source_target_pairs={{0,32},{8,232},{16,48},{24,248},{32,64},{40,8},{48,80},{56,24},{64... | collective-permute-start | bytes 1572872 | tf_op jit(solution)/shard_map/ppermute | solution.py:45
  51.2 21.3 %collective-permute-start.7 = (bf16[2,192,128]{2,1,0:T(8,128)(2,1)S(1)}, bf16[2,192,128]{2,1,0:T(8,128)(2,1)S(1)}, u32[]{:S(2)}, u32[]{:S(2)}) collective-permute-start(bf16[2,192,128]{2,1,0:T(8,128)(2,1)S(1)} %get-tuple-element.12), channel_id=1, source_target_pairs={{0,8},{8,16},{16,24},{24,32},{32,40},{40,48},{48,56},{56,64},{64,7... | collective-permute-start | bytes 294920 | tf_op jit(solution)/shard_map/ppermute | solution.py:24
  60.3 17.5 %collective-permute-start.6 = (bf16[2,12,256,128]{3,2,1,0:T(8,128)(2,1)}, bf16[2,12,256,128]{3,2,1,0:T(8,128)(2,1)S(1)}, u32[]{:S(2)}, u32[]{:S(2)}) collective-permute-start(bf16[2,12,256,128]{3,2,1,0:T(8,128)(2,1)} %pad_maximum_fusion), channel_id=1, source_target_pairs={{0,8},{8,0},{16,24},{24,16},{32,40},{40,32},{48,56},{56,48},{64,72... | collective-permute-start | bytes 4718600 | tf_op jit(solution)/shard_map/ppermute | solution.py:47
  64.2 11.6 %collective-permute-start.5 = (bf16[2,4,256,128]{3,2,1,0:T(8,128)(2,1)S(1)}, bf16[2,4,256,128]{3,2,1,0:T(8,128)(2,1)}, u32[]{:S(2)}, u32[]{:S(2)}) collective-permute-start(bf16[2,4,256,128]{3,2,1,0:T(8,128)(2,1)S(1)} %collective-permute-done.4), channel_id=1, source_target_pairs={{0,32},{8,232},{16,48},{24,248},{32,64},{40,8},{48,80},{56,24},{64... | collective-permute-start | bytes 1572872 | tf_op jit(solution)/shard_map/ppermute | solution.py:45
where the time goes:
time: 110 us
  Pallas kernels  30.9 us (28%)
  waiting for transfers between devices  26.7 us (24%)
  starting transfers between devices  17.8 us (16%)
  blocking collectives  13.9 us (13%)
  local copies, waits for them, and re-layouts  13.4 us (12%)
  other arithmetic  4.63 us (4%)
  between operations  2.67 us (2%)
    pallas_call x1, Pallas kernels, per_device(): pl.pallas_call(kernel, out_shape=jax.ShapeDtypeStruct((tok_rows, per_kv *...  30.9 us
    ppermute x4, waiting for transfers between devices, ring_gather(): lax.ppermute(walked[-1], 'req', route(lambda i: i + 4 if i % 2 == 0 else...  18.5 us
    ppermute x4, starting transfers between devices, ring_gather(): lax.ppermute(walked[-1], 'req', route(lambda i: i + 4 if i % 2 == 0 else...  14.3 us
    all_to_all x1, blocking collectives, per_device(): lax.all_to_all(prefix_kv, 'tp', split_axis=3, concat_axis=2, tiled=True)  13.9 us
    ppermute x1, waiting for transfers between devices, ring_gather(): other = lax.ppermute(two, 'req', route(lambda i: i ^ 2))  6.92 us
    unnamed x17, local copies, waits for them, and re-layouts  6.63 us
  transfers between devices with their start and end apart: 8, of which 5 were waited for; matrix products, arithmetic and copies ran while one was open for 12% of the time, Pallas kernels for 0%

commit v1 on v0

--- a/solution.py
+++ b/solution.py
@@ -35,27 +35,33 @@
     def route(fn):
         return [(i, fn(i) % n) for i in range(n)]
 
+    def both(x, fn):
+        return [lax.ppermute(x[kv], "req", route(fn)) for kv in range(2)]
+
     other = lax.ppermute(block, "req", route(lambda i: i ^ 1))
     two = jnp.where(core == 0, jnp.concatenate([block, other], 1), jnp.concatenate([other, block], 1))
-    other = lax.ppermute(two, "req", route(lambda i: i ^ 2))
-    four = jnp.where(pair == 0, jnp.concatenate([two, other], 1), jnp.concatenate([other, two], 1))
+    two = [two[0], two[1]]
+    other = both(two, lambda i: i ^ 2)
+    four = [
+        jnp.where(pair == 0, jnp.concatenate([t, o], 0), jnp.concatenate([o, t], 0))
+        for t, o in zip(two, other)
+    ]
     walked = [four]
     for _ in range(reach):
-        walked.append(
-            lax.ppermute(walked[-1], "req", route(lambda i: i + 4 if i % 2 == 0 else i - 4))
-        )
-    swapped = lax.ppermute(jnp.concatenate(walked[1:reach], 1), "req", route(lambda i: i ^ 1))
-    stored = jnp.concatenate(walked + [swapped], 1)
+        walked.append(both(walked[-1], lambda i: i + 4 if i % 2 == 0 else i - 4))
+    mine = [jnp.concatenate([w[kv] for w in walked[1:reach]], 0) for kv in range(2)]
+    swapped = both(mine, lambda i: i ^ 1)
+    pieces = [[w[kv] for w in walked] + [swapped[kv]] for kv in range(2)]
     z = r // 4
     o = (wanted // 4 - z) % n_z
     p0 = jnp.where(o == 0, 0, jnp.where(o >= reach, n_z - o, reach + o))
     p1 = jnp.where(o <= reach, o, reach + n_z - o)
-    return stored, jnp.where(core == 0, p0, p1) * 4 + wanted % 4
-
-
-def attend_kernel(
-    scal_ref, q_ref, stored_ref, s0_ref, s1_ref, o_ref, buf, sems, *, per_kv, half, n_blocks
-):
+    return pieces, jnp.where(core == 0, p0, p1) * 4 + wanted % 4
+
+
+def attend_kernel(scal_ref, q_ref, *refs, per_kv, half, n_blocks, n_pieces):
+    piece_refs = (refs[:n_pieces], refs[n_pieces : 2 * n_pieces])
+    s0_ref, s1_ref, o_ref, buf, sems = refs[2 * n_pieces :]
     h = pl.program_id(0)
     i = pl.program_id(1)
     base = scal_ref[0]
@@ -65,18 +71,38 @@
     any_live = (start < slot0 + TILE) & (stop > slot0)
     rows = per_kv * TILE
     scale = 1.0 / math.sqrt(HD)
-    block_rows = stored_ref.shape[2]
-
-    def block_copy(hh, b):
-        src = stored_ref.at[:, scal_ref[8 + hh * n_blocks + b]]
-        dst = buf.at[hh, :, pl.ds(b * block_rows, block_rows), :]
-        return pltpu.make_async_copy(src, dst, sems.at[hh, b])
+    block_rows = piece_refs[0][0].shape[1]
+    group = piece_refs[0][0].shape[0]
+    last = n_pieces - 1
+
+    def dst(hh, kv, b):
+        return buf.at[hh, kv, pl.ds(b * block_rows, block_rows), :]
+
+    def start_copy(hh, b):
+        where = scal_ref[8 + hh * n_blocks + b]
+        place = where // group
+        for p in range(n_pieces):
+            hit = (place == p) if p < last else (place >= last)
+            at = where % group if p < last else where - last * group
+
+            @pl.when(hit)
+            def _():
+                for kv in range(2):
+                    pltpu.make_async_copy(
+                        piece_refs[kv][p].at[at], dst(hh, kv, b), sems.at[hh, kv, b]
+                    ).start()
+
+    def wait_copy(hh, b):
+        for kv in range(2):
+            pltpu.make_async_copy(
+                piece_refs[kv][0].at[0], dst(hh, kv, b), sems.at[hh, kv, b]
+            ).wait()
 
     @pl.when((h == 0) & (i == 0))
     def _():
         for hh in range(2):
             for b in range(n_blocks):
-                block_copy(hh, b).start()
+                start_copy(hh, b)
 
     @pl.when(jnp.logical_not(any_live))
     def _():
@@ -86,7 +112,7 @@
         @pl.when(i == 0)
         def _():
             for b in range(n_blocks):
-                block_copy(hh, b).wait()
+                wait_copy(hh, b)
 
         @pl.when(any_live)
         def _():
@@ -179,7 +205,7 @@
     head = jnp.stack([base, start0, stop0, start1, stop1, base, base, base])
 
     local = lax.all_to_all(prefix_kv, "tp", split_axis=3, concat_axis=2, tiled=True)
-    stored, where_block = ring_gather(local, rows_of.reshape(-1))
+    pieces, where_block = ring_gather(local, rows_of.reshape(-1))
     scal = jnp.concatenate([head, where_block]).astype(jnp.int32)
     earlier = from_behind(suffix_kv[:, half:, :], "req", 1)
     s0 = jnp.concatenate([earlier, suffix_kv[:, :half, :]], axis=1)
@@ -190,8 +216,11 @@
 
     tiles_per_half = half // TILE
     grid = (2, tiles_per_half)
-    kernel = functools.partial(attend_kernel, per_kv=per_kv, half=half, n_blocks=per_group)
-    block_rows = stored.shape[2]
+    n_pieces = len(pieces[0])
+    kernel = functools.partial(
+        attend_kernel, per_kv=per_kv, half=half, n_blocks=per_group, n_pieces=n_pieces
+    )
+    block_rows = pieces[0][0].shape[1]
     prefix_rows = per_group * block_rows
     tile_map = lambda h, i, s: (h * tiles_per_half + i, 0)
     return pl.pallas_call(
@@ -202,18 +231,18 @@
             grid=grid,
             in_specs=[
                 pl.BlockSpec((TILE, per_kv * HD), tile_map),
-                pl.BlockSpec(memory_space=pl.ANY),
+                *[pl.BlockSpec(memory_space=pl.ANY)] * (2 * n_pieces),
                 pl.BlockSpec(s0.shape, lambda h, i, s: (0, 0, 0)),
                 pl.BlockSpec(s1.shape, lambda h, i, s: (0, 0, 0)),
             ],
             out_specs=pl.BlockSpec((TILE, per_kv * HD), tile_map),
             scratch_shapes=[
-                pltpu.VMEM((2, 2, prefix_rows, HD), stored.dtype),
-                pltpu.SemaphoreType.DMA((2, per_group)),
+                pltpu.VMEM((2, 2, prefix_rows, HD), queries.dtype),
+                pltpu.SemaphoreType.DMA((2, 2, per_group)),
             ],
         ),
         compiler_params=pltpu.CompilerParams(dimension_semantics=("arbitrary", "arbitrary")),
-    )(scal, queries, stored, s0, s1)
+    )(scal, queries, *pieces[0], *pieces[1], s0, s1)
 
 
 def solution(mesh):

time: 110 us -> 98.1 us (0.89)
  the two profiles are of different devices: /device:TPU:98 before, /device:TPU:64 now
where the time goes in v1:
time: 98.1 us; the launch traced here: 97.6 us
  Pallas kernels  31.1 us (32%)
  starting transfers between devices  28 us (29%)
  blocking collectives  14.8 us (15%)
  local copies, waits for them, and re-layouts  9.8 us (10%)
  waiting for transfers between devices  7.82 us (8%)
  other arithmetic  3.24 us (3%)
  between operations  2.91 us (3%)
    pallas_call x1, Pallas kernels, per_device(): pl.pallas_call(kernel, out_shape=jax.ShapeDtypeStruct((tok_rows, per_kv *...  31.1 us
    ppermute x12, starting transfers between devices, both(): return [lax.ppermute(x[kv], 'req', route(fn)) for kv in range(2)]  26 us
    all_to_all x1, blocking collectives, per_device(): lax.all_to_all(prefix_kv, 'tp', split_axis=3, concat_axis=2, tiled=True)  14.8 us
    ppermute x12, waiting for transfers between devices, both(): return [lax.ppermute(x[kv], 'req', route(fn)) for kv in range(2)]  6.49 us
    unnamed x35, local copies, waits for them, and re-layouts  4.48 us
  transfers between devices with their start and end apart: 14, of which 5 were waited for; matrix products, arithmetic and copies ran while one was open for 8% of the time, Pallas kernels for 0%

profile of v1, /device:TPU:64, one launch (start us, length us, event | category | flops | bytes accessed | tf_op | source)
XLA Modules:
  0.0 97.6 jit_solution(15309835560860620922)
XLA Ops:
  0.0 1.2 %copy.15 = bf16[2,1,32,1024]{2,0,1,3:T(2,128)(2,1)S(1)} copy(bf16[2,1,32,1024]{3,2,1,0:T(8,128)(2,1)} %param.11) | data formatting | bytes 262144 | tf_op args[2]
  1.7 14.8 %all_to_all.18 = bf16[8,2,4096]{2,1,0:T(2,128)(2,1)S(1)} all-to-all(bf16[8,2,4096]{2,1,0:T(2,128)(2,1)S(1)} %reshape.109), channel_id=1, replica_groups=mesh['req'=32,'tp'=8] {'tp'}, dimensions={0} | all-to-all | bytes 262144 | tf_op jit(solution)/shard_map/all_to_all | solution.py:207
  17.3 1.3 %collective-permute-done = bf16[2,1,256,128]{3,2,1,0:T(8,128)(2,1)S(1)} collective-permute-done((bf16[2,1,256,128]{3,2,1,0:T(8,128)(2,1)S(1)}, bf16[2,1,256,128]{3,2,1,0:T(8,128)(2,1)S(1)}, u32[]{:S(2)}, u32[]{:S(2)}) %collective-permute-start) | collective-permute-done | bytes 131104 | tf_op jit(solution)/shard_map/ppermute | solution.py:41
  18.7 0.7 collective-permute-start.7
  19.4 1.4 %collective-permute-start.1 = (bf16[2,256,128]{2,1,0:T(8,128)(2,1)S(1)}, bf16[2,256,128]{2,1,0:T(8,128)(2,1)S(1)}, u32[]{:S(2)}, u32[]{:S(2)}) collective-permute-start(bf16[2,256,128]{2,1,0:T(8,128)(2,1)S(1)} %get-tuple-element.11), channel_id=1, source_target_pairs={{0,16},{8,24},{16,0},{24,8},{32,48},{40,56},{48,32},{56,40},{64,80... | collective-permute-start | bytes 393224 | tf_op jit(solution)/shard_map/ppermute | solution.py:39
  20.8 4.3 %collective-permute-done.7 = bf16[2,256,128]{2,1,0:T(8,128)(2,1)S(1)} collective-permute-done((bf16[2,256,128]{2,1,0:T(8,128)(2,1)S(1)}, bf16[2,256,128]{2,1,0:T(8,128)(2,1)S(1)}, u32[]{:S(2)}, u32[]{:S(2)}) %collective-permute-start.7) | collective-permute-done | bytes 131104 | tf_op jit(solution)/shard_map/ppermute | solution.py:39
  25.2 2.0 %collective-permute-start.8 = (bf16[4,256,128]{2,1,0:T(8,128)(2,1)S(1)}, bf16[4,256,128]{2,1,0:T(8,128)(2,1)S(1)}, u32[]{:S(2)}, u32[]{:S(2)}) collective-permute-start(bf16[4,256,128]{2,1,0:T(8,128)(2,1)S(1)} %maximum_select_fusion.2.refs_6_), channel_id=1, source_target_pairs={{0,32},{8,232},{16,48},{24,248},{32,64},{40,8},{48,80},{56,24},{64... | collective-permute-start | bytes 786440 | tf_op jit(solution)/shard_map/ppermute | solution.py:39
  27.2 3.2 %collective-permute-start.2 = (bf16[4,256,128]{2,1,0:T(8,128)(2,1)S(1)}, bf16[4,256,128]{2,1,0:T(8,128)(2,1)S(1)}, u32[]{:S(2)}, u32[]{:S(2)}) collective-permute-start(bf16[4,256,128]{2,1,0:T(8,128)(2,1)S(1)} %maximum_select_fusion.1.refs_0_), channel_id=1, source_target_pairs={{0,32},{8,232},{16,48},{24,248},{32,64},{40,8},{48,80},{56,24},{64... | collective-permute-start | bytes 786440 | tf_op jit(solution)/shard_map/ppermute | solution.py:39
  30.5 1.9 %collective-permute-start.13 = (bf16[2,192,128]{2,1,0:T(8,128)(2,1)S(1)}, bf16[2,192,128]{2,1,0:T(8,128)(2,1)S(1)}, u32[]{:S(2)}, u32[]{:S(2)}) collective-permute-start(bf16[2,192,128]{2,1,0:T(8,128)(2,1)S(1)} %get-tuple-element.12), channel_id=1, source_target_pairs={{0,8},{8,16},{16,24},{24,32},{32,40},{40,48},{48,56},{56,64},{64,7... | collective-permute-start | bytes 294920 | tf_op jit(solution)/shard_map/ppermute | solution.py:24
  32.4 1.9 %collective-permute-start.9 = (bf16[4,256,128]{2,1,0:T(8,128)(2,1)S(1)}, bf16[4,256,128]{2,1,0:T(8,128)(2,1)S(1)}, u32[]{:S(2)}, u32[]{:S(2)}) collective-permute-start(bf16[4,256,128]{2,1,0:T(8,128)(2,1)S(1)} %collective-permute-done.8.refs_7_), channel_id=1, source_target_pairs={{0,32},{8,232},{16,48},{24,248},{32,64},{40,8},{48,80},{56,24},{64... | collective-permute-start | bytes 786440 | tf_op jit(solution)/shard_map/ppermute | solution.py:39
  34.5 3.5 %collective-permute-start.3 = (bf16[4,256,128]{2,1,0:T(8,128)(2,1)S(1)}, bf16[4,256,128]{2,1,0:T(8,128)(2,1)S(1)}, u32[]{:S(2)}, u32[]{:S(2)}) collective-permute-start(bf16[4,256,128]{2,1,0:T(8,128)(2,1)S(1)} %collective-permute-done.2.refs_1_), channel_id=1, source_target_pairs={{0,32},{8,232},{16,48},{24,248},{32,64},{40,8},{48,80},{56,24},{64... | collective-permute-start | bytes 786440 | tf_op jit(solution)/shard_map/ppermute | solution.py:39
  37.9 0.7 gather_fusion.2
  38.9 2.9 %collective-permute-start.10 = (bf16[4,256,128]{2,1,0:T(8,128)(2,1)S(1)}, bf16[4,256,128]{2,1,0:T(8,128)(2,1)S(1)}, u32[]{:S(2)}, u32[]{:S(2)}) collective-permute-start(bf16[4,256,128]{2,1,0:T(8,128)(2,1)S(1)} %collective-permute-done.9.refs_8_), channel_id=1, source_target_pairs={{0,32},{8,232},{16,48},{24,248},{32,64},{40,8},{48,80},{56,24},{64... | collective-permute-start | bytes 786440 | tf_op jit(solution)/shard_map/ppermute | solution.py:39
  41.8 3.7 %collective-permute-start.4 = (bf16[4,256,128]{2,1,0:T(8,128)(2,1)S(1)}, bf16[4,256,128]{2,1,0:T(8,128)(2,1)S(1)}, u32[]{:S(2)}, u32[]{:S(2)}) collective-permute-start(bf16[4,256,128]{2,1,0:T(8,128)(2,1)S(1)} %collective-permute-done.3.refs_2_), channel_id=1, source_target_pairs={{0,32},{8,232},{16,48},{24,248},{32,64},{40,8},{48,80},{56,24},{64... | collective-permute-start | bytes 786440 | tf_op jit(solution)/shard_map/ppermute | solution.py:39
  46.1 1.3 %add_multiply_fusion = s32[2]{0:T(128)S(1)} fusion(s32[1]{0:T(128)} %get-tuple-element.15, s32[1]{0:T(128)} %get-tuple-element.14), kind=kLoop, calls=%fused_computation.36 | loop fusion | flops 4 | bytes 16 | tf_op jit(solution)/shard_map/mul | solution.py:203
  47.6 1.8 %collective-permute-done.4.refs_3_ = bf16[4,256,128]{2,1,0:T(8,128)(2,1)S(1)} collective-permute-done((bf16[4,256,128]{2,1,0:T(8,128)(2,1)S(1)}, bf16[4,256,128]{2,1,0:T(8,128)(2,1)S(1)}, u32[]{:S(2)}, u32[]{:S(2)}) %collective-permute-start.4) | collective-permute-done | bytes 262176 | tf_op jit(solution)/shard_map/ppermute | solution.py:39
  49.4 1.0 pad_maximum_fusion
  51.3 0.7 gather_fusion.1
  52.7 2.9 %collective-permute-start.11 = (bf16[4,256,128]{2,1,0:T(8,128)(2,1)S(1)}, bf16[4,256,128]{2,1,0:T(8,128)(2,1)S(1)}, u32[]{:S(2)}, u32[]{:S(2)}) collective-permute-start(bf16[4,256,128]{2,1,0:T(8,128)(2,1)S(1)} %collective-permute-done.10.refs_9_), channel_id=1, source_target_pairs={{0,32},{8,232},{16,48},{24,248},{32,64},{40,8},{48,80},{56,24},{64... | collective-permute-start | bytes 786440 | tf_op jit(solution)/shard_map/ppermute | solution.py:39
  55.6 3.7 %collective-permute-start.5 = (bf16[4,256,128]{2,1,0:T(8,128)(2,1)S(1)}, bf16[4,256,128]{2,1,0:T(8,128)(2,1)}, u32[]{:S(2)}, u32[]{:S(2)}) collective-permute-start(bf16[4,256,128]{2,1,0:T(8,128)(2,1)S(1)} %collective-permute-done.4.refs_3_), channel_id=1, source_target_pairs={{0,32},{8,232},{16,48},{24,248},{32,64},{40,8},{48,80},{56,24},{64... | collective-permute-start | bytes 786440 | tf_op jit(solution)/shard_map/ppermute | solution.py:39
  63.8 0.7 pad_maximum_fusion.2.refs_12_
  64.5 0.7 copy-done.13
  65.5 0.9 copy-done.12
  66.4 31.1 %shard_map.73 = bf16[384,1024]{1,0:T(8,128)(2,1)} custom-call(s32[24]{0:T(128)} %concatenate.37.scal_ref, bf16[384,1024]{1,0:T(8,128)(2,1)} %q_ref.1, bf16[4,256,128]{2,1,0:T(8,128)(2,1)} %copy-done.4, bf16[4,256,128]{2,1,0:T(8,128)(2,1)} %copy-done.6, bf16[4,256,128]{2,1,0:T(8,128)(2,1)} %copy-done.8, bf16[4,256,128]{2,1,0:T(8,128)(2,1)} %copy-done.10, ...), custom_call_target="tpu_custom_call" | custom-call | tf_op jit(solution)/shard_map/pallas_call | solution.py:226
  (70 shorter events, 6.5 us)
Async XLA Ops:
  0.0 37.9 %copy-start = (s32[31]{0:T(128)S(1)}, s32[31]{0:T(128)}, u32[]{:S(2)}) copy-start(s32[31]{0:T(128)} %param.13) | copy-start | bytes 376
  17.2 1.4 %collective-permute-start = (bf16[2,1,256,128]{3,2,1,0:T(8,128)(2,1)S(1)}, bf16[2,1,256,128]{3,2,1,0:T(8,128)(2,1)S(1)}, u32[]{:S(2)}, u32[]{:S(2)}) collective-permute-start(bf16[2,1,256,128]{3,2,1,0:T(8,128)(2,1)S(1)} %bitcast.26), channel_id=1, source_target_pairs={{0,8},{8,0},{16,24},{24,16},{32,40},{40,32},{48,56},{56,48},{64,72... | collective-permute-start | bytes 393224 | tf_op jit(solution)/shard_map/ppermute | solution.py:41
  18.7 6.5 %collective-permute-start.7 = (bf16[2,256,128]{2,1,0:T(8,128)(2,1)S(1)}, bf16[2,256,128]{2,1,0:T(8,128)(2,1)S(1)}, u32[]{:S(2)}, u32[]{:S(2)}) collective-permute-start(bf16[2,256,128]{2,1,0:T(8,128)(2,1)S(1)} %get-tuple-element.10), channel_id=1, source_target_pairs={{0,16},{8,24},{16,0},{24,8},{32,48},{40,56},{48,32},{56,40},{64,80... | collective-permute-start | bytes 393224 | tf_op jit(solution)/shard_map/ppermute | solution.py:39
  19.4 7.8 %collective-permute-start.1 = (bf16[2,256,128]{2,1,0:T(8,128)(2,1)S(1)}, bf16[2,256,128]{2,1,0:T(8,128)(2,1)S(1)}, u32[]{:S(2)}, u32[]{:S(2)}) collective-permute-start(bf16[2,256,128]{2,1,0:T(8,128)(2,1)S(1)} %get-tuple-element.11), channel_id=1, source_target_pairs={{0,16},{8,24},{16,0},{24,8},{32,48},{40,56},{48,32},{56,40},{64,80... | collective-permute-start | bytes 393224 | tf_op jit(solution)/shard_map/ppermute | solution.py:39
  25.2 5.3 %copy-start.14 = (bf16[2,384,128]{2,1,0:T(8,128)(2,1)S(1)}, bf16[2,384,128]{2,1,0:T(8,128)(2,1)}, u32[]{:S(2)}) copy-start(bf16[2,384,128]{2,1,0:T(8,128)(2,1)} %param.10) | copy-start | bytes 589828
  25.2 7.2 %collective-permute-start.8 = (bf16[4,256,128]{2,1,0:T(8,128)(2,1)S(1)}, bf16[4,256,128]{2,1,0:T(8,128)(2,1)S(1)}, u32[]{:S(2)}, u32[]{:S(2)}) collective-permute-start(bf16[4,256,128]{2,1,0:T(8,128)(2,1)S(1)} %maximum_select_fusion.2.refs_6_), channel_id=1, source_target_pairs={{0,32},{8,232},{16,48},{24,248},{32,64},{40,8},{48,80},{56,24},{64... | collective-permute-start | bytes 786440 | tf_op jit(solution)/shard_map/ppermute | solution.py:39
  27.2 11.4 %copy-start.4 = (bf16[4,256,128]{2,1,0:T(8,128)(2,1)}, bf16[4,256,128]{2,1,0:T(8,128)(2,1)S(1)}, u32[]{:S(2)}) copy-start(bf16[4,256,128]{2,1,0:T(8,128)(2,1)S(1)} %maximum_select_fusion.1.refs_0_) | copy-start | bytes 786436
  27.2 7.2 %collective-permute-start.2 = (bf16[4,256,128]{2,1,0:T(8,128)(2,1)S(1)}, bf16[4,256,128]{2,1,0:T(8,128)(2,1)S(1)}, u32[]{:S(2)}, u32[]{:S(2)}) collective-permute-start(bf16[4,256,128]{2,1,0:T(8,128)(2,1)S(1)} %maximum_select_fusion.1.refs_0_), channel_id=1, source_target_pairs={{0,32},{8,232},{16,48},{24,248},{32,64},{40,8},{48,80},{56,24},{64... | collective-permute-start | bytes 786440 | tf_op jit(solution)/shard_map/ppermute | solution.py:39
  30.5 7.4 %copy-start.15 = (s32[31]{0:T(128)S(1)}, s32[31]{0:T(128)}, u32[]{:S(2)}) copy-start(s32[31]{0:T(128)} %param.14) | copy-start | bytes 376
  30.5 33.3 %collective-permute-start.13 = (bf16[2,192,128]{2,1,0:T(8,128)(2,1)S(1)}, bf16[2,192,128]{2,1,0:T(8,128)(2,1)S(1)}, u32[]{:S(2)}, u32[]{:S(2)}) collective-permute-start(bf16[2,192,128]{2,1,0:T(8,128)(2,1)S(1)} %get-tuple-element.12), channel_id=1, source_target_pairs={{0,8},{8,16},{16,24},{24,32},{32,40},{40,48},{48,56},{56,64},{64,7... | collective-permute-start | bytes 294920 | tf_op jit(solution)/shard_map/ppermute | solution.py:24
  32.4 15.0 %copy-start.5 = (bf16[4,256,128]{2,1,0:T(8,128)(2,1)}, bf16[4,256,128]{2,1,0:T(8,128)(2,1)S(1)}, u32[]{:S(2)}) copy-start(bf16[4,256,128]{2,1,0:T(8,128)(2,1)S(1)} %collective-permute-done.8.refs_7_) | copy-start | bytes 786436
  32.4 6.4 %collective-permute-start.9 = (bf16[4,256,128]{2,1,0:T(8,128)(2,1)S(1)}, bf16[4,256,128]{2,1,0:T(8,128)(2,1)S(1)}, u32[]{:S(2)}, u32[]{:S(2)}) collective-permute-start(bf16[4,256,128]{2,1,0:T(8,128)(2,1)S(1)} %collective-permute-done.8.refs_7_), channel_id=1, source_target_pairs={{0,32},{8,232},{16,48},{24,248},{32,64},{40,8},{48,80},{56,24},{64... | collective-permute-start | bytes 786440 | tf_op jit(solution)/shard_map/ppermute | solution.py:39
  34.5 14.9 %copy-start.6 = (bf16[4,256,128]{2,1,0:T(8,128)(2,1)}, bf16[4,256,128]{2,1,0:T(8,128)(2,1)S(1)}, u32[]{:S(2)}) copy-start(bf16[4,256,128]{2,1,0:T(8,128)(2,1)S(1)} %collective-permute-done.2.refs_1_) | copy-start | bytes 786436
  34.5 7.3 %collective-permute-start.3 = (bf16[4,256,128]{2,1,0:T(8,128)(2,1)S(1)}, bf16[4,256,128]{2,1,0:T(8,128)(2,1)S(1)}, u32[]{:S(2)}, u32[]{:S(2)}) collective-permute-start(bf16[4,256,128]{2,1,0:T(8,128)(2,1)S(1)} %collective-permute-done.2.refs_1_), channel_id=1, source_target_pairs={{0,32},{8,232},{16,48},{24,248},{32,64},{40,8},{48,80},{56,24},{64... | collective-permute-start | bytes 786440 | tf_op jit(solution)/shard_map/ppermute | solution.py:39
  38.9 8.6 %copy-start.7 = (bf16[4,256,128]{2,1,0:T(8,128)(2,1)}, bf16[4,256,128]{2,1,0:T(8,128)(2,1)S(1)}, u32[]{:S(2)}) copy-start(bf16[4,256,128]{2,1,0:T(8,128)(2,1)S(1)} %collective-permute-done.9.refs_8_) | copy-start | bytes 786436
  38.9 8.5 %collective-permute-start.10 = (bf16[4,256,128]{2,1,0:T(8,128)(2,1)S(1)}, bf16[4,256,128]{2,1,0:T(8,128)(2,1)S(1)}, u32[]{:S(2)}, u32[]{:S(2)}) collective-permute-start(bf16[4,256,128]{2,1,0:T(8,128)(2,1)S(1)} %collective-permute-done.9.refs_8_), channel_id=1, source_target_pairs={{0,32},{8,232},{16,48},{24,248},{32,64},{40,8},{48,80},{56,24},{64... | collective-permute-start | bytes 786440 | tf_op jit(solution)/shard_map/ppermute | solution.py:39
  41.8 7.6 %copy-start.8 = (bf16[4,256,128]{2,1,0:T(8,128)(2,1)}, bf16[4,256,128]{2,1,0:T(8,128)(2,1)S(1)}, u32[]{:S(2)}) copy-start(bf16[4,256,128]{2,1,0:T(8,128)(2,1)S(1)} %collective-permute-done.3.refs_2_) | copy-start | bytes 786436
  41.8 7.6 %collective-permute-start.4 = (bf16[4,256,128]{2,1,0:T(8,128)(2,1)S(1)}, bf16[4,256,128]{2,1,0:T(8,128)(2,1)S(1)}, u32[]{:S(2)}, u32[]{:S(2)}) collective-permute-start(bf16[4,256,128]{2,1,0:T(8,128)(2,1)S(1)} %collective-permute-done.3.refs_2_), channel_id=1, source_target_pairs={{0,32},{8,232},{16,48},{24,248},{32,64},{40,8},{48,80},{56,24},{64... | collective-permute-start | bytes 786440 | tf_op jit(solution)/shard_map/ppermute | solution.py:39
  47.4 5.4 %copy-start.9 = (bf16[4,256,128]{2,1,0:T(8,128)(2,1)}, bf16[4,256,128]{2,1,0:T(8,128)(2,1)S(1)}, u32[]{:S(2)}) copy-start(bf16[4,256,128]{2,1,0:T(8,128)(2,1)S(1)} %collective-permute-done.10.refs_9_) | copy-start | bytes 786436
  47.5 17.0 %collective-permute-start.12 = (bf16[12,256,128]{2,1,0:T(8,128)(2,1)S(1)}, bf16[12,256,128]{2,1,0:T(8,128)(2,1)S(1)}, u32[]{:S(2)}, u32[]{:S(2)}) collective-permute-start(bf16[12,256,128]{2,1,0:T(8,128)(2,1)S(1)} %pad_maximum_fusion.1), channel_id=1, source_target_pairs={{0,8},{8,0},{16,24},{24,16},{32,40},{40,32},{48,56},{56,48},{64,72... | collective-permute-start | bytes 2359304 | tf_op jit(solution)/shard_map/ppermute | solution.py:39
  49.4 6.2 %copy-start.10 = (bf16[4,256,128]{2,1,0:T(8,128)(2,1)}, bf16[4,256,128]{2,1,0:T(8,128)(2,1)S(1)}, u32[]{:S(2)}) copy-start(bf16[4,256,128]{2,1,0:T(8,128)(2,1)S(1)} %collective-permute-done.4.refs_3_) | copy-start | bytes 786436
  50.4 14.2 %collective-permute-start.6 = (bf16[12,256,128]{2,1,0:T(8,128)(2,1)}, bf16[12,256,128]{2,1,0:T(8,128)(2,1)S(1)}, u32[]{:S(2)}, u32[]{:S(2)}) collective-permute-start(bf16[12,256,128]{2,1,0:T(8,128)(2,1)} %pad_maximum_fusion), channel_id=1, source_target_pairs={{0,8},{8,0},{16,24},{24,16},{32,40},{40,32},{48,56},{56,48},{64,72... | collective-permute-start | bytes 2359304 | tf_op jit(solution)/shard_map/ppermute | solution.py:39
  52.7 11.7 %collective-permute-start.11 = (bf16[4,256,128]{2,1,0:T(8,128)(2,1)S(1)}, bf16[4,256,128]{2,1,0:T(8,128)(2,1)S(1)}, u32[]{:S(2)}, u32[]{:S(2)}) collective-permute-start(bf16[4,256,128]{2,1,0:T(8,128)(2,1)S(1)} %collective-permute-done.10.refs_9_), channel_id=1, source_target_pairs={{0,32},{8,232},{16,48},{24,248},{32,64},{40,8},{48,80},{56,24},{64... | collective-permute-start | bytes 786440 | tf_op jit(solution)/shard_map/ppermute | solution.py:39
  55.6 8.9 %collective-permute-start.5 = (bf16[4,256,128]{2,1,0:T(8,128)(2,1)S(1)}, bf16[4,256,128]{2,1,0:T(8,128)(2,1)}, u32[]{:S(2)}, u32[]{:S(2)}) collective-permute-start(bf16[4,256,128]{2,1,0:T(8,128)(2,1)S(1)} %collective-permute-done.4.refs_3_), channel_id=1, source_target_pairs={{0,32},{8,232},{16,48},{24,248},{32,64},{40,8},{48,80},{56,24},{64... | collective-permute-start | bytes 786440 | tf_op jit(solution)/shard_map/ppermute | solution.py:39
  (6 other events, 6.0 us)

commit v2 on v1

--- a/solution.py
+++ b/solution.py
@@ -15,7 +15,7 @@
 
 masked_score = -1e30
 TILE = 64
-CHUNK = 512
+CHUNK = 2048
 
 
 def from_behind(block, axis, distance):

time: 98.1 us -> 92.7 us (0.945)
  the two profiles are of different devices: /device:TPU:64 before, /device:TPU:2 now
where the time goes in v2:
time: 92.7 us; the launch traced here: 93.4 us
  waiting for transfers between devices  27.2 us (29%)
  Pallas kernels  24.9 us (27%)
  blocking collectives  13.9 us (15%)
  starting transfers between devices  11.4 us (12%)
  local copies, waits for them, and re-layouts  9.73 us (10%)
  other arithmetic  3.24 us (3%)
  between operations  2.92 us (3%)
    ppermute x12, waiting for transfers between devices, both(): return [lax.ppermute(x[kv], 'req', route(fn)) for kv in range(2)]  25.9 us
    pallas_call x1, Pallas kernels, per_device(): pl.pallas_call(kernel, out_shape=jax.ShapeDtypeStruct((tok_rows, per_kv *...  24.9 us
    all_to_all x1, blocking collectives, per_device(): lax.all_to_all(prefix_kv, 'tp', split_axis=3, concat_axis=2, tiled=True)  13.9 us
    ppermute x12, starting transfers between devices, both(): return [lax.ppermute(x[kv], 'req', route(fn)) for kv in range(2)]  6.56 us
    ppermute x1, starting transfers between devices, from_behind(): return lax.ppermute(block, axis, route)  4.8 us
    unnamed x35, local copies, waits for them, and re-layouts  4.39 us
  transfers between devices with their start and end apart: 14, of which 10 were waited for; matrix products, arithmetic and copies ran while one was open for 9% of the time, Pallas kernels for 0%

profile of v2, /device:TPU:2, one launch (start us, length us, event | category | flops | bytes accessed | tf_op | source)
XLA Modules:
  0.0 93.4 jit_solution(5165057629884497788)
XLA Ops:
  0.0 1.2 %copy.15 = bf16[2,1,32,1024]{2,0,1,3:T(2,128)(2,1)S(1)} copy(bf16[2,1,32,1024]{3,2,1,0:T(8,128)(2,1)} %param.11) | data formatting | bytes 262144 | tf_op args[2]
  1.7 13.9 %all_to_all.18 = bf16[8,2,4096]{2,1,0:T(2,128)(2,1)S(1)} all-to-all(bf16[8,2,4096]{2,1,0:T(2,128)(2,1)S(1)} %reshape.109), channel_id=1, replica_groups=mesh['req'=32,'tp'=8] {'tp'}, dimensions={0} | all-to-all | bytes 262144 | tf_op jit(solution)/shard_map/all_to_all | solution.py:207
  16.4 1.3 %collective-permute-done = bf16[2,1,256,128]{3,2,1,0:T(8,128)(2,1)S(1)} collective-permute-done((bf16[2,1,256,128]{3,2,1,0:T(8,128)(2,1)S(1)}, bf16[2,1,256,128]{3,2,1,0:T(8,128)(2,1)S(1)}, u32[]{:S(2)}, u32[]{:S(2)}) %collective-permute-start) | collective-permute-done | bytes 131104 | tf_op jit(solution)/shard_map/ppermute | solution.py:41
  17.8 1.5 %collective-permute-start.7 = (bf16[2,256,128]{2,1,0:T(8,128)(2,1)S(1)}, bf16[2,256,128]{2,1,0:T(8,128)(2,1)S(1)}, u32[]{:S(2)}, u32[]{:S(2)}) collective-permute-start(bf16[2,256,128]{2,1,0:T(8,128)(2,1)S(1)} %get-tuple-element.10), channel_id=1, source_target_pairs={{0,16},{8,24},{16,0},{24,8},{32,48},{40,56},{48,32},{56,40},{64,80... | collective-permute-start | bytes 393224 | tf_op jit(solution)/shard_map/ppermute | solution.py:39
  19.9 4.3 %collective-permute-done.7 = bf16[2,256,128]{2,1,0:T(8,128)(2,1)S(1)} collective-permute-done((bf16[2,256,128]{2,1,0:T(8,128)(2,1)S(1)}, bf16[2,256,128]{2,1,0:T(8,128)(2,1)S(1)}, u32[]{:S(2)}, u32[]{:S(2)}) %collective-permute-start.7) | collective-permute-done | bytes 131104 | tf_op jit(solution)/shard_map/ppermute | solution.py:39
  24.3 2.0 %collective-permute-start.8 = (bf16[4,256,128]{2,1,0:T(8,128)(2,1)S(1)}, bf16[4,256,128]{2,1,0:T(8,128)(2,1)S(1)}, u32[]{:S(2)}, u32[]{:S(2)}) collective-permute-start(bf16[4,256,128]{2,1,0:T(8,128)(2,1)S(1)} %maximum_select_fusion.2.refs_6_), channel_id=1, source_target_pairs={{0,32},{8,232},{16,48},{24,248},{32,64},{40,8},{48,80},{56,24},{64... | collective-permute-start | bytes 786440 | tf_op jit(solution)/shard_map/ppermute | solution.py:39
  26.3 2.0 %collective-permute-start.2 = (bf16[4,256,128]{2,1,0:T(8,128)(2,1)S(1)}, bf16[4,256,128]{2,1,0:T(8,128)(2,1)S(1)}, u32[]{:S(2)}, u32[]{:S(2)}) collective-permute-start(bf16[4,256,128]{2,1,0:T(8,128)(2,1)S(1)} %maximum_select_fusion.1.refs_0_), channel_id=1, source_target_pairs={{0,32},{8,232},{16,48},{24,248},{32,64},{40,8},{48,80},{56,24},{64... | collective-permute-start | bytes 786440 | tf_op jit(solution)/shard_map/ppermute | solution.py:39
  28.4 4.8 %collective-permute-start.13 = (bf16[2,192,128]{2,1,0:T(8,128)(2,1)S(1)}, bf16[2,192,128]{2,1,0:T(8,128)(2,1)S(1)}, u32[]{:S(2)}, u32[]{:S(2)}) collective-permute-start(bf16[2,192,128]{2,1,0:T(8,128)(2,1)S(1)} %get-tuple-element.12), channel_id=1, source_target_pairs={{0,8},{8,16},{16,24},{24,32},{32,40},{40,48},{48,56},{56,64},{64,7... | collective-permute-start | bytes 294920 | tf_op jit(solution)/shard_map/ppermute | solution.py:24
  33.2 1.4 %collective-permute-done.8.refs_7_ = bf16[4,256,128]{2,1,0:T(8,128)(2,1)S(1)} collective-permute-done((bf16[4,256,128]{2,1,0:T(8,128)(2,1)S(1)}, bf16[4,256,128]{2,1,0:T(8,128)(2,1)S(1)}, u32[]{:S(2)}, u32[]{:S(2)}) %collective-permute-start.8) | collective-permute-done | bytes 262176 | tf_op jit(solution)/shard_map/ppermute | solution.py:39
  34.6 2.8 %collective-permute-done.2.refs_1_ = bf16[4,256,128]{2,1,0:T(8,128)(2,1)S(1)} collective-permute-done((bf16[4,256,128]{2,1,0:T(8,128)(2,1)S(1)}, bf16[4,256,128]{2,1,0:T(8,128)(2,1)S(1)}, u32[]{:S(2)}, u32[]{:S(2)}) %collective-permute-start.2) | collective-permute-done | bytes 262176 | tf_op jit(solution)/shard_map/ppermute | solution.py:39
  37.4 0.7 gather_fusion.2
  38.1 4.0 %collective-permute-done.9.refs_8_ = bf16[4,256,128]{2,1,0:T(8,128)(2,1)S(1)} collective-permute-done((bf16[4,256,128]{2,1,0:T(8,128)(2,1)S(1)}, bf16[4,256,128]{2,1,0:T(8,128)(2,1)S(1)}, u32[]{:S(2)}, u32[]{:S(2)}) %collective-permute-start.9) | collective-permute-done | bytes 262176 | tf_op jit(solution)/shard_map/ppermute | solution.py:39
  42.2 2.8 %collective-permute-done.3.refs_2_ = bf16[4,256,128]{2,1,0:T(8,128)(2,1)S(1)} collective-permute-done((bf16[4,256,128]{2,1,0:T(8,128)(2,1)S(1)}, bf16[4,256,128]{2,1,0:T(8,128)(2,1)S(1)}, u32[]{:S(2)}, u32[]{:S(2)}) %collective-permute-start.3) | collective-permute-done | bytes 262176 | tf_op jit(solution)/shard_map/ppermute | solution.py:39
  45.6 1.3 %add_multiply_fusion = s32[2]{0:T(128)S(1)} fusion(s32[1]{0:T(128)} %get-tuple-element.15, s32[1]{0:T(128)} %get-tuple-element.14), kind=kLoop, calls=%fused_computation.36 | loop fusion | flops 4 | bytes 16 | tf_op jit(solution)/shard_map/mul | solution.py:203
  46.9 2.9 %collective-permute-done.10.refs_9_ = bf16[4,256,128]{2,1,0:T(8,128)(2,1)S(1)} collective-permute-done((bf16[4,256,128]{2,1,0:T(8,128)(2,1)S(1)}, bf16[4,256,128]{2,1,0:T(8,128)(2,1)S(1)}, u32[]{:S(2)}, u32[]{:S(2)}) %collective-permute-start.10) | collective-permute-done | bytes 262176 | tf_op jit(solution)/shard_map/ppermute | solution.py:39
  50.0 2.6 %collective-permute-done.4.refs_3_ = bf16[4,256,128]{2,1,0:T(8,128)(2,1)S(1)} collective-permute-done((bf16[4,256,128]{2,1,0:T(8,128)(2,1)S(1)}, bf16[4,256,128]{2,1,0:T(8,128)(2,1)S(1)}, u32[]{:S(2)}, u32[]{:S(2)}) %collective-permute-start.4) | collective-permute-done | bytes 262176 | tf_op jit(solution)/shard_map/ppermute | solution.py:39
  52.6 1.0 %pad_maximum_fusion = bf16[12,256,128]{2,1,0:T(8,128)(2,1)} fusion(bf16[4,256,128]{2,1,0:T(8,128)(2,1)S(1)} %collective-permute-done.4.refs_3_, bf16[4,256,128]{2,1,0:T(8,128)(2,1)S(1)} %collective-permute-done.3.refs_2_, bf16[4,256,128]{2,1,0:T(8,128)(2,1)S(1)} %collective-permute-done.2.refs_1_), kind=kLoop, calls=%fused_computation.3 | loop fusion | flops 786432 | bytes 1572864 | tf_op jit(solution)/shard_map/concatenate | solution.py:52
  54.5 0.7 gather_fusion.1
  60.8 0.7 pad_maximum_fusion.2.refs_12_
  61.5 2.1 %collective-permute-done.11.refs_10_ = bf16[4,256,128]{2,1,0:T(8,128)(2,1)S(1)} collective-permute-done((bf16[4,256,128]{2,1,0:T(8,128)(2,1)S(1)}, bf16[4,256,128]{2,1,0:T(8,128)(2,1)S(1)}, u32[]{:S(2)}, u32[]{:S(2)}) %collective-permute-start.11) | collective-permute-done | bytes 262176 | tf_op jit(solution)/shard_map/ppermute | solution.py:39
  63.6 2.9 %collective-permute-done.5.refs_4_ = bf16[4,256,128]{2,1,0:T(8,128)(2,1)} collective-permute-done((bf16[4,256,128]{2,1,0:T(8,128)(2,1)S(1)}, bf16[4,256,128]{2,1,0:T(8,128)(2,1)}, u32[]{:S(2)}, u32[]{:S(2)}) %collective-permute-start.5) | collective-permute-done | bytes 262176 | tf_op jit(solution)/shard_map/ppermute | solution.py:39
  66.5 0.9 copy-done.11
  67.4 0.9 copy-done.12
  68.3 24.9 %shard_map.73 = bf16[384,1024]{1,0:T(8,128)(2,1)} custom-call(s32[24]{0:T(128)} %concatenate.37.scal_ref, bf16[384,1024]{1,0:T(8,128)(2,1)} %q_ref.1, bf16[4,256,128]{2,1,0:T(8,128)(2,1)} %copy-done.4, bf16[4,256,128]{2,1,0:T(8,128)(2,1)} %copy-done.6, bf16[4,256,128]{2,1,0:T(8,128)(2,1)} %copy-done.8, bf16[4,256,128]{2,1,0:T(8,128)(2,1)} %copy-done.10, ...), custom_call_target="tpu_custom_call" | custom-call | tf_op jit(solution)/shard_map/pallas_call | solution.py:226
  (70 shorter events, 6.8 us)
Async XLA Ops:
  0.0 37.4 %copy-start = (s32[31]{0:T(128)S(1)}, s32[31]{0:T(128)}, u32[]{:S(2)}) copy-start(s32[31]{0:T(128)} %param.13) | copy-start | bytes 376
  16.3 1.4 %collective-permute-start = (bf16[2,1,256,128]{3,2,1,0:T(8,128)(2,1)S(1)}, bf16[2,1,256,128]{3,2,1,0:T(8,128)(2,1)S(1)}, u32[]{:S(2)}, u32[]{:S(2)}) collective-permute-start(bf16[2,1,256,128]{3,2,1,0:T(8,128)(2,1)S(1)} %bitcast.26), channel_id=1, source_target_pairs={{0,8},{8,0},{16,24},{24,16},{32,40},{40,32},{48,56},{56,48},{64,72... | collective-permute-start | bytes 393224 | tf_op jit(solution)/shard_map/ppermute | solution.py:41
  17.8 6.5 %collective-permute-start.7 = (bf16[2,256,128]{2,1,0:T(8,128)(2,1)S(1)}, bf16[2,256,128]{2,1,0:T(8,128)(2,1)S(1)}, u32[]{:S(2)}, u32[]{:S(2)}) collective-permute-start(bf16[2,256,128]{2,1,0:T(8,128)(2,1)S(1)} %get-tuple-element.10), channel_id=1, source_target_pairs={{0,16},{8,24},{16,0},{24,8},{32,48},{40,56},{48,32},{56,40},{64,80... | collective-permute-start | bytes 393224 | tf_op jit(solution)/shard_map/ppermute | solution.py:39
  19.3 7.0 %collective-permute-start.1 = (bf16[2,256,128]{2,1,0:T(8,128)(2,1)S(1)}, bf16[2,256,128]{2,1,0:T(8,128)(2,1)S(1)}, u32[]{:S(2)}, u32[]{:S(2)}) collective-permute-start(bf16[2,256,128]{2,1,0:T(8,128)(2,1)S(1)} %get-tuple-element.11), channel_id=1, source_target_pairs={{0,16},{8,24},{16,0},{24,8},{32,48},{40,56},{48,32},{56,40},{64,80... | collective-permute-start | bytes 393224 | tf_op jit(solution)/shard_map/ppermute | solution.py:39
  24.3 4.1 %copy-start.14 = (bf16[2,384,128]{2,1,0:T(8,128)(2,1)S(1)}, bf16[2,384,128]{2,1,0:T(8,128)(2,1)}, u32[]{:S(2)}) copy-start(bf16[2,384,128]{2,1,0:T(8,128)(2,1)} %param.10) | copy-start | bytes 589828
  24.3 10.3 %collective-permute-start.8 = (bf16[4,256,128]{2,1,0:T(8,128)(2,1)S(1)}, bf16[4,256,128]{2,1,0:T(8,128)(2,1)S(1)}, u32[]{:S(2)}, u32[]{:S(2)}) collective-permute-start(bf16[4,256,128]{2,1,0:T(8,128)(2,1)S(1)} %maximum_select_fusion.2.refs_6_), channel_id=1, source_target_pairs={{0,32},{8,232},{16,48},{24,248},{32,64},{40,8},{48,80},{56,24},{64... | collective-permute-start | bytes 786440 | tf_op jit(solution)/shard_map/ppermute | solution.py:39
  26.3 11.8 %copy-start.4 = (bf16[4,256,128]{2,1,0:T(8,128)(2,1)}, bf16[4,256,128]{2,1,0:T(8,128)(2,1)S(1)}, u32[]{:S(2)}) copy-start(bf16[4,256,128]{2,1,0:T(8,128)(2,1)S(1)} %maximum_select_fusion.1.refs_0_) | copy-start | bytes 786436
  26.3 11.0 %collective-permute-start.2 = (bf16[4,256,128]{2,1,0:T(8,128)(2,1)S(1)}, bf16[4,256,128]{2,1,0:T(8,128)(2,1)S(1)}, u32[]{:S(2)}, u32[]{:S(2)}) collective-permute-start(bf16[4,256,128]{2,1,0:T(8,128)(2,1)S(1)} %maximum_select_fusion.1.refs_0_), channel_id=1, source_target_pairs={{0,32},{8,232},{16,48},{24,248},{32,64},{40,8},{48,80},{56,24},{64... | collective-permute-start | bytes 786440 | tf_op jit(solution)/shard_map/ppermute | solution.py:39
  28.4 9.0 %copy-start.15 = (s32[31]{0:T(128)S(1)}, s32[31]{0:T(128)}, u32[]{:S(2)}) copy-start(s32[31]{0:T(128)} %param.14) | copy-start | bytes 376
  28.4 32.4 %collective-permute-start.13 = (bf16[2,192,128]{2,1,0:T(8,128)(2,1)S(1)}, bf16[2,192,128]{2,1,0:T(8,128)(2,1)S(1)}, u32[]{:S(2)}, u32[]{:S(2)}) collective-permute-start(bf16[2,192,128]{2,1,0:T(8,128)(2,1)S(1)} %get-tuple-element.12), channel_id=1, source_target_pairs={{0,8},{8,16},{16,24},{24,32},{32,40},{40,48},{48,56},{56,64},{64,7... | collective-permute-start | bytes 294920 | tf_op jit(solution)/shard_map/ppermute | solution.py:24
  34.6 15.2 %copy-start.5 = (bf16[4,256,128]{2,1,0:T(8,128)(2,1)}, bf16[4,256,128]{2,1,0:T(8,128)(2,1)S(1)}, u32[]{:S(2)}) copy-start(bf16[4,256,128]{2,1,0:T(8,128)(2,1)S(1)} %collective-permute-done.8.refs_7_) | copy-start | bytes 786436
  34.6 7.6 %collective-permute-start.9 = (bf16[4,256,128]{2,1,0:T(8,128)(2,1)S(1)}, bf16[4,256,128]{2,1,0:T(8,128)(2,1)S(1)}, u32[]{:S(2)}, u32[]{:S(2)}) collective-permute-start(bf16[4,256,128]{2,1,0:T(8,128)(2,1)S(1)} %collective-permute-done.8.refs_7_), channel_id=1, source_target_pairs={{0,32},{8,232},{16,48},{24,248},{32,64},{40,8},{48,80},{56,24},{64... | collective-permute-start | bytes 786440 | tf_op jit(solution)/shard_map/ppermute | solution.py:39
  37.4 15.2 %copy-start.6 = (bf16[4,256,128]{2,1,0:T(8,128)(2,1)}, bf16[4,256,128]{2,1,0:T(8,128)(2,1)S(1)}, u32[]{:S(2)}) copy-start(bf16[4,256,128]{2,1,0:T(8,128)(2,1)S(1)} %collective-permute-done.2.refs_1_) | copy-start | bytes 786436
  37.4 7.6 %collective-permute-start.3 = (bf16[4,256,128]{2,1,0:T(8,128)(2,1)S(1)}, bf16[4,256,128]{2,1,0:T(8,128)(2,1)S(1)}, u32[]{:S(2)}, u32[]{:S(2)}) collective-permute-start(bf16[4,256,128]{2,1,0:T(8,128)(2,1)S(1)} %collective-permute-done.2.refs_1_), channel_id=1, source_target_pairs={{0,32},{8,232},{16,48},{24,248},{32,64},{40,8},{48,80},{56,24},{64... | collective-permute-start | bytes 786440 | tf_op jit(solution)/shard_map/ppermute | solution.py:39
  42.2 7.7 %copy-start.7 = (bf16[4,256,128]{2,1,0:T(8,128)(2,1)}, bf16[4,256,128]{2,1,0:T(8,128)(2,1)S(1)}, u32[]{:S(2)}) copy-start(bf16[4,256,128]{2,1,0:T(8,128)(2,1)S(1)} %collective-permute-done.9.refs_8_) | copy-start | bytes 786436
  42.2 7.6 %collective-permute-start.10 = (bf16[4,256,128]{2,1,0:T(8,128)(2,1)S(1)}, bf16[4,256,128]{2,1,0:T(8,128)(2,1)S(1)}, u32[]{:S(2)}, u32[]{:S(2)}) collective-permute-start(bf16[4,256,128]{2,1,0:T(8,128)(2,1)S(1)} %collective-permute-done.9.refs_8_), channel_id=1, source_target_pairs={{0,32},{8,232},{16,48},{24,248},{32,64},{40,8},{48,80},{56,24},{64... | collective-permute-start | bytes 786440 | tf_op jit(solution)/shard_map/ppermute | solution.py:39
  45.0 7.6 %copy-start.8 = (bf16[4,256,128]{2,1,0:T(8,128)(2,1)}, bf16[4,256,128]{2,1,0:T(8,128)(2,1)S(1)}, u32[]{:S(2)}) copy-start(bf16[4,256,128]{2,1,0:T(8,128)(2,1)S(1)} %collective-permute-done.3.refs_2_) | copy-start | bytes 786436
  45.0 7.6 %collective-permute-start.4 = (bf16[4,256,128]{2,1,0:T(8,128)(2,1)S(1)}, bf16[4,256,128]{2,1,0:T(8,128)(2,1)S(1)}, u32[]{:S(2)}, u32[]{:S(2)}) collective-permute-start(bf16[4,256,128]{2,1,0:T(8,128)(2,1)S(1)} %collective-permute-done.3.refs_2_), channel_id=1, source_target_pairs={{0,32},{8,232},{16,48},{24,248},{32,64},{40,8},{48,80},{56,24},{64... | collective-permute-start | bytes 786440 | tf_op jit(solution)/shard_map/ppermute | solution.py:39
  49.8 6.2 %copy-start.9 = (bf16[4,256,128]{2,1,0:T(8,128)(2,1)}, bf16[4,256,128]{2,1,0:T(8,128)(2,1)S(1)}, u32[]{:S(2)}) copy-start(bf16[4,256,128]{2,1,0:T(8,128)(2,1)S(1)} %collective-permute-done.10.refs_9_) | copy-start | bytes 786436
  49.9 16.6 %collective-permute-start.12 = (bf16[12,256,128]{2,1,0:T(8,128)(2,1)S(1)}, bf16[12,256,128]{2,1,0:T(8,128)(2,1)S(1)}, u32[]{:S(2)}, u32[]{:S(2)}) collective-permute-start(bf16[12,256,128]{2,1,0:T(8,128)(2,1)S(1)} %pad_maximum_fusion.1), channel_id=1, source_target_pairs={{0,8},{8,0},{16,24},{24,16},{32,40},{40,32},{48,56},{56,48},{64,72... | collective-permute-start | bytes 2359304 | tf_op jit(solution)/shard_map/ppermute | solution.py:39
  52.6 3.5 %copy-start.10 = (bf16[4,256,128]{2,1,0:T(8,128)(2,1)}, bf16[4,256,128]{2,1,0:T(8,128)(2,1)S(1)}, u32[]{:S(2)}) copy-start(bf16[4,256,128]{2,1,0:T(8,128)(2,1)S(1)} %collective-permute-done.4.refs_3_) | copy-start | bytes 786436
  53.5 13.0 %collective-permute-start.6 = (bf16[12,256,128]{2,1,0:T(8,128)(2,1)}, bf16[12,256,128]{2,1,0:T(8,128)(2,1)S(1)}, u32[]{:S(2)}, u32[]{:S(2)}) collective-permute-start(bf16[12,256,128]{2,1,0:T(8,128)(2,1)} %pad_maximum_fusion), channel_id=1, source_target_pairs={{0,8},{8,0},{16,24},{24,16},{32,40},{40,32},{48,56},{56,48},{64,72... | collective-permute-start | bytes 2359304 | tf_op jit(solution)/shard_map/ppermute | solution.py:39
  55.9 7.7 %collective-permute-start.11 = (bf16[4,256,128]{2,1,0:T(8,128)(2,1)S(1)}, bf16[4,256,128]{2,1,0:T(8,128)(2,1)S(1)}, u32[]{:S(2)}, u32[]{:S(2)}) collective-permute-start(bf16[4,256,128]{2,1,0:T(8,128)(2,1)S(1)} %collective-permute-done.10.refs_9_), channel_id=1, source_target_pairs={{0,32},{8,232},{16,48},{24,248},{32,64},{40,8},{48,80},{56,24},{64... | collective-permute-start | bytes 786440 | tf_op jit(solution)/shard_map/ppermute | solution.py:39
  56.0 10.5 %collective-permute-start.5 = (bf16[4,256,128]{2,1,0:T(8,128)(2,1)S(1)}, bf16[4,256,128]{2,1,0:T(8,128)(2,1)}, u32[]{:S(2)}, u32[]{:S(2)}) collective-permute-start(bf16[4,256,128]{2,1,0:T(8,128)(2,1)S(1)} %collective-permute-done.4.refs_3_), channel_id=1, source_target_pairs={{0,32},{8,232},{16,48},{24,248},{32,64},{40,8},{48,80},{56,24},{64... | collective-permute-start | bytes 786440 | tf_op jit(solution)/shard_map/ppermute | solution.py:39
  (6 other events, 8.2 us)

commit v3 on v2

v3 whole, which is shorter than its diff:
```python
import functools
import math

import jax
import jax.numpy as jnp
from jax import lax
from jax.experimental import pallas as pl
from jax.experimental.pallas import tpu as pltpu
from jax.sharding import PartitionSpec as P

QH = 64
KVH = 8
HD = 128
GROUPS = 4

masked_score = -1e30
TILE = 64
WINDOW = 256


def from_behind(block, axis, distance):
    devices = range(lax.axis_size(axis))
    route = [(i - distance, i) for i in devices if i - distance in devices]
    return lax.ppermute(block, axis, route)


def ring_gather(block):
    n = lax.axis_size("req")
    r = lax.axis_index("req")
    core = r % 2
    pair = (r // 2) % 2
    reach = n // 8

    def route(fn):
        return [(i, fn(i) % n) for i in range(n)]

    def both(x, fn):
        return [lax.ppermute(x[kv], "req", route(fn)) for kv in range(2)]

    other = lax.ppermute(block, "req", route(lambda i: i ^ 1))
    two = jnp.where(core == 0, jnp.concatenate([block, other], 1), jnp.concatenate([other, block], 1))
    two = [two[0], two[1]]
    other = both(two, lambda i: i ^ 2)
    four = [
        jnp.where(pair == 0, jnp.concatenate([t, o], 0), jnp.concatenate([o, t], 0))
        for t, o in zip(two, other)
    ]
    walked = [four]
    for _ in range(reach):
        walked.append(both(walked[-1], lambda i: i + 4 if i % 2 == 0 else i - 4))
    mine = [jnp.concatenate([w[kv] for w in walked[1:reach]], 0) for kv in range(2)]
    swapped = both(mine, lambda i: i ^ 1)
    return [[w[kv] for w in walked] + [swapped[kv]] for kv in range(2)]


def attend_kernel(
    len_ref, group_ref, order_ref, owner_ref, q_ref, *refs,
    per_kv, half, n_blocks, n_pieces, n_dev, requests, tok_rows
):
    piece_refs = (refs[:n_pieces], refs[n_pieces : 2 * n_pieces])
    prev_ref, own_ref, o_ref, buf, sems = refs[2 * n_pieces :]
    h = pl.program_id(0)
    i = pl.program_id(1)
    r = lax.axis_index("req")
    base = r * tok_rows

    def span(k):
        length = len_ref[order_ref[k]]
        first = (k + 1) * tok_rows - length // 2
        return first, first + length

    k0 = jnp.maximum(r - 1, 0)
    k1 = jnp.minimum(r, requests - 1)
    start0, stop0 = span(k0)
    start1, stop1 = span(k1)
    start0 = jnp.where(r >= 1, start0, -1)
    stop0 = jnp.where(r >= 1, stop0, -1)
    start1 = jnp.where(r < requests, start1, -1)
    stop1 = jnp.where(r < requests, stop1, -1)
    start = jnp.where(h == 0, start0, start1)
    stop = jnp.where(h == 0, stop0, stop1)
    slot0 = base + h * half + i * TILE
    any_live = (start < slot0 + TILE) & (stop > slot0)
    rows = per_kv * TILE
    scale = 1.0 / math.sqrt(HD)
    block_rows = piece_refs[0][0].shape[1]
    group = piece_refs[0][0].shape[0]
    last = n_pieces - 1
    n_z = n_dev // 4
    reach = n_z // 2
    core = r % 2
    z = r // 4

    def position(hh, b):
        g = group_ref[order_ref[k0 if hh == 0 else k1]]
        d = owner_ref[g * n_blocks + b]
        o = (d // 4 - z + n_z) % n_z
        p0 = jnp.where(o == 0, 0, jnp.where(o >= reach, n_z - o, reach + o))
        p1 = jnp.where(o <= reach, o, reach + n_z - o)
        return jnp.where(core == 0, p0, p1) * 4 + d % 4

    def dst(hh, kv, b):
        return buf.at[hh, kv, pl.ds(b * block_rows, block_rows), :]

    def start_copy(hh, b):
        where = position(hh, b)
        place = where // group
        for p in range(n_pieces):
            hit = (place == p) if p < last else (place >= last)
            at = where % group if p < last else where - last * group

            @pl.when(hit)
            def _():
                for kv in range(2):
                    pltpu.make_async_copy(
                        piece_refs[kv][p].at[at], dst(hh, kv, b), sems.at[hh, kv, b]
                    ).start()

    def wait_copy(hh, b):
        for kv in range(2):
            pltpu.make_async_copy(
                piece_refs[kv][0].at[0], dst(hh, kv, b), sems.at[hh, kv, b]
            ).wait()

    @pl.when((h == 0) & (i == 0))
    def _():
        for hh in range(2):
            for b in range(n_blocks):
                start_copy(hh, b)

    @pl.when(jnp.logical_not(any_live))
    def _():
        o_ref[...] = jnp.zeros_like(o_ref)

    def body(hh, chunks):
        @pl.when(i == 0)
        def _():
            for b in range(n_blocks):
                wait_copy(hh, b)

        @pl.when(any_live)
        def _():
            compute(hh, chunks)

    def compute(hh, chunks):
        kref = buf.at[hh, 0]
        vref = buf.at[hh, 1]
        q = jnp.concatenate([q_ref[:, j * HD : (j + 1) * HD] for j in range(per_kv)], axis=0)
        row = lax.broadcasted_iota(jnp.int32, (rows, 1), 0)
        slot = slot0 + jnp.bitwise_and(row, TILE - 1)
        live = (slot >= start) & (slot < stop)

        def raw(k):
            return lax.dot_general(
                q, k, (((1,), (1,)), ((), ())), preferred_element_type=jnp.float32
            )

        s_pre = raw(kref[...])
        m = jnp.max(s_pre, axis=1, keepdims=True) * scale
        suffix = []
        for kc, vc, key_base in chunks:
            key_slot = key_base + lax.broadcasted_iota(jnp.int32, (1, kc.shape[0]), 1)
            ok = (key_slot >= start) & (key_slot <= slot) & live
            s = raw(kc) * scale
            m = jnp.maximum(m, jnp.max(jnp.where(ok, s, masked_score), axis=1, keepdims=True))
            suffix.append((s, ok, vc))
        p = jnp.exp(s_pre * scale - m)
        l = jnp.sum(p, axis=1, keepdims=True)
        acc = jnp.dot(p.astype(jnp.bfloat16), vref[...], preferred_element_type=jnp.float32)
        for s, ok, vc in suffix:
            p = jnp.where(ok, jnp.exp(s - m), 0.0)
            l = l + jnp.sum(p, axis=1, keepdims=True)
            acc = acc + jnp.dot(p.astype(jnp.bfloat16), vc, preferred_element_type=jnp.float32)
        out = jnp.where(live, acc / jnp.where(live, l, 1.0), 0.0).astype(o_ref.dtype)
        for j in range(per_kv):
            o_ref[:, j * HD : (j + 1) * HD] = out[j * TILE : (j + 1) * TILE, :]

    skip = tok_rows - WINDOW

    @pl.when(h == 0)
    def _():
        body(
            0,
            [
                (prev_ref[0], prev_ref[1], base - WINDOW),
                (own_ref[0, :WINDOW], own_ref[1, :WINDOW], base),
            ],
        )

    @pl.when(h == 1)
    def _():
        body(1, [(own_ref[0, skip:], own_ref[1, skip:], base + skip)])


def per_device(
    queries, suffix_kv, prefix_kv, suffix_length, request_group, request_order, owner_map
):
    tok_rows = queries.shape[0]
    head_cols = suffix_kv.shape[2]
    per_kv = queries.shape[1] // head_cols
    stored_count = owner_map.shape[0]
    per_group = stored_count // GROUPS
    requests = suffix_length.shape[0]
    half = tok_rows // 2

    local = lax.all_to_all(prefix_kv, "tp", split_axis=3, concat_axis=2, tiled=True)
    pieces = ring_gather(local)
    earlier = from_behind(suffix_kv[:, tok_rows - WINDOW :, :], "req", 1)

    tiles_per_half = half // TILE
    grid = (2, tiles_per_half)
    n_pieces = len(pieces[0])
    kernel = functools.partial(
        attend_kernel,
        per_kv=per_kv,
        half=half,
        n_blocks=per_group,
        n_pieces=n_pieces,
        n_dev=lax.axis_size("req"),
        requests=requests,
        tok_rows=tok_rows,
    )
    block_rows = pieces[0][0].shape[1]
    prefix_rows = per_group * block_rows
    tile_map = lambda h, i, *s: (h * tiles_per_half + i, 0)
    whole = lambda h, i, *s: (0, 0, 0)
    return pl.pallas_call(
        kernel,
        out_shape=jax.ShapeDtypeStruct((tok_rows, per_kv * HD), queries.dtype),
        grid_spec=pltpu.PrefetchScalarGridSpec(
            num_scalar_prefetch=4,
            grid=grid,
            in_specs=[
                pl.BlockSpec((TILE, per_kv * HD), tile_map),
                *[pl.BlockSpec(memory_space=pl.ANY)] * (2 * n_pieces),
                pl.BlockSpec(earlier.shape, whole),
                pl.BlockSpec(suffix_kv.shape, whole),
            ],
            out_specs=pl.BlockSpec((TILE, per_kv * HD), tile_map),
            scratch_shapes=[
                pltpu.VMEM((2, 2, prefix_rows, HD), queries.dtype),
                pltpu.SemaphoreType.DMA((2, 2, per_group)),
            ],
        ),
        compiler_params=pltpu.CompilerParams(dimension_semantics=("arbitrary", "arbitrary")),
    )(
        suffix_length,
        request_group,
        request_order,
        owner_map,
        queries,
        *pieces[0],
        *pieces[1],
        earlier,
        suffix_kv,
    )


def solution(mesh):
    in_specs = (
        P("req", "tp"),
        P(None, "req", "tp"),
        P(None, "req", "tp", None),
        P(),
        P(),
        P(),
        P(),
    )
    out_specs = P("req", "tp")
    return jax.shard_map(
        per_device, mesh=mesh, in_specs=in_specs, out_specs=out_specs, check_vma=False
    )
```

time: 92.7 us -> 91.9 us (level)
  the two profiles are of different devices: /device:TPU:2 before, /device:TPU:1 now
where the time goes in v3:
time: 91.9 us; the launch traced here: 91.5 us
  starting transfers between devices  35.2 us (38%)
  Pallas kernels  26 us (28%)
  blocking collectives  14.2 us (15%)
  waiting for transfers between devices  11.2 us (12%)
  local copies, waits for them, and re-layouts  4.28 us (5%)
    ppermute x12, starting transfers between devices, both(): return [lax.ppermute(x[kv], 'req', route(fn)) for kv in range(2)]  30.3 us
    pallas_call x1, Pallas kernels, per_device(): pl.pallas_call(kernel, out_shape=jax.ShapeDtypeStruct((tok_rows, per_kv *...  26 us
    all_to_all x1, blocking collectives, per_device(): lax.all_to_all(prefix_kv, 'tp', split_axis=3, concat_axis=2, tiled=True)  14.2 us
    ppermute x12, waiting for transfers between devices, both(): return [lax.ppermute(x[kv], 'req', route(fn)) for kv in range(2)]  8.47 us
    unnamed x31, local copies, waits for them, and re-layouts  3.87 us
    ppermute x1, starting transfers between devices, from_behind(): return lax.ppermute(block, axis, route)  2.7 us
    ppermute x1, starting transfers between devices, ring_gather(): other = lax.ppermute(block, 'req', route(lambda i: i ^ 1))  2.19 us
  transfers between devices with their start and end apart: 14, of which 8 were waited for; matrix products, arithmetic and copies ran while one was open for 0% of the time, Pallas kernels for 0%

profile of v3, /device:TPU:1, one launch (start us, length us, event | category | flops | bytes accessed | tf_op | source)
XLA Modules:
  0.0 91.5 jit_solution(5384614407292228147)
XLA Ops:
  0.0 1.2 %copy.14 = bf16[2,1,32,1024]{2,0,1,3:T(2,128)(2,1)S(1)} copy(bf16[2,1,32,1024]{3,2,1,0:T(8,128)(2,1)} %param.9) | data formatting | bytes 262144 | tf_op args[2]
  1.2 0.5 reshape
  1.7 14.2 %all_to_all.18 = bf16[8,2,4096]{2,1,0:T(2,128)(2,1)S(1)} all-to-all(bf16[8,2,4096]{2,1,0:T(2,128)(2,1)S(1)} %reshape), channel_id=1, replica_groups=mesh['req'=32,'tp'=8] {'tp'}, dimensions={0} | all-to-all | bytes 262144 | tf_op jit(solution)/shard_map/all_to_all | solution.py:206
  16.6 2.2 %collective-permute-start = (bf16[2,1,256,128]{3,2,1,0:T(8,128)(2,1)S(1)}, bf16[2,1,256,128]{3,2,1,0:T(8,128)(2,1)S(1)}, u32[]{:S(2)}, u32[]{:S(2)}) collective-permute-start(bf16[2,1,256,128]{3,2,1,0:T(8,128)(2,1)S(1)} %bitcast.13), channel_id=1, source_target_pairs={{0,8},{8,0},{16,24},{24,16},{32,40},{40,32},{48,56},{56,48},{64,72... | collective-permute-start | bytes 393224 | tf_op jit(solution)/shard_map/ppermute | solution.py:40
  18.7 1.0 %collective-permute-done = bf16[2,1,256,128]{3,2,1,0:T(8,128)(2,1)S(1)} collective-permute-done((bf16[2,1,256,128]{3,2,1,0:T(8,128)(2,1)S(1)}, bf16[2,1,256,128]{3,2,1,0:T(8,128)(2,1)S(1)}, u32[]{:S(2)}, u32[]{:S(2)}) %collective-permute-start) | collective-permute-done | bytes 131104 | tf_op jit(solution)/shard_map/ppermute | solution.py:40
  20.2 1.2 %collective-permute-start.1 = (bf16[2,256,128]{2,1,0:T(8,128)(2,1)S(1)}, bf16[2,256,128]{2,1,0:T(8,128)(2,1)S(1)}, u32[]{:S(2)}, u32[]{:S(2)}) collective-permute-start(bf16[2,256,128]{2,1,0:T(8,128)(2,1)S(1)} %get-tuple-element.6), channel_id=1, source_target_pairs={{0,16},{8,24},{16,0},{24,8},{32,48},{40,56},{48,32},{56,40},{64,80... | collective-permute-start | bytes 393224 | tf_op jit(solution)/shard_map/ppermute | solution.py:38
  21.3 3.2 %collective-permute-done.7 = bf16[2,256,128]{2,1,0:T(8,128)(2,1)S(1)} collective-permute-done((bf16[2,256,128]{2,1,0:T(8,128)(2,1)S(1)}, bf16[2,256,128]{2,1,0:T(8,128)(2,1)S(1)}, u32[]{:S(2)}, u32[]{:S(2)}) %collective-permute-start.7) | collective-permute-done | bytes 131104 | tf_op jit(solution)/shard_map/ppermute | solution.py:38
  24.6 5.7 %collective-permute-start.8 = (bf16[4,256,128]{2,1,0:T(8,128)(2,1)S(1)}, bf16[4,256,128]{2,1,0:T(8,128)(2,1)S(1)}, u32[]{:S(2)}, u32[]{:S(2)}) collective-permute-start(bf16[4,256,128]{2,1,0:T(8,128)(2,1)S(1)} %maximum_select_fusion.2.refs_6_), channel_id=1, source_target_pairs={{0,32},{8,232},{16,48},{24,248},{32,64},{40,8},{48,80},{56,24},{64... | collective-permute-start | bytes 786440 | tf_op jit(solution)/shard_map/ppermute | solution.py:38
  30.3 2.8 %collective-permute-start.2 = (bf16[4,256,128]{2,1,0:T(8,128)(2,1)S(1)}, bf16[4,256,128]{2,1,0:T(8,128)(2,1)S(1)}, u32[]{:S(2)}, u32[]{:S(2)}) collective-permute-start(bf16[4,256,128]{2,1,0:T(8,128)(2,1)S(1)} %maximum_select_fusion.1.refs_0_), channel_id=1, source_target_pairs={{0,32},{8,232},{16,48},{24,248},{32,64},{40,8},{48,80},{56,24},{64... | collective-permute-start | bytes 786440 | tf_op jit(solution)/shard_map/ppermute | solution.py:38
  33.1 0.5 collective-permute-done.8.refs_7_
  33.6 3.1 %collective-permute-start.9 = (bf16[4,256,128]{2,1,0:T(8,128)(2,1)S(1)}, bf16[4,256,128]{2,1,0:T(8,128)(2,1)S(1)}, u32[]{:S(2)}, u32[]{:S(2)}) collective-permute-start(bf16[4,256,128]{2,1,0:T(8,128)(2,1)S(1)} %collective-permute-done.8.refs_7_), channel_id=1, source_target_pairs={{0,32},{8,232},{16,48},{24,248},{32,64},{40,8},{48,80},{56,24},{64... | collective-permute-start | bytes 786440 | tf_op jit(solution)/shard_map/ppermute | solution.py:38
  36.7 2.8 %collective-permute-start.3 = (bf16[4,256,128]{2,1,0:T(8,128)(2,1)S(1)}, bf16[4,256,128]{2,1,0:T(8,128)(2,1)S(1)}, u32[]{:S(2)}, u32[]{:S(2)}) collective-permute-start(bf16[4,256,128]{2,1,0:T(8,128)(2,1)S(1)} %collective-permute-done.2.refs_1_), channel_id=1, source_target_pairs={{0,32},{8,232},{16,48},{24,248},{32,64},{40,8},{48,80},{56,24},{64... | collective-permute-start | bytes 786440 | tf_op jit(solution)/shard_map/ppermute | solution.py:38
  40.0 3.1 %collective-permute-start.10 = (bf16[4,256,128]{2,1,0:T(8,128)(2,1)S(1)}, bf16[4,256,128]{2,1,0:T(8,128)(2,1)S(1)}, u32[]{:S(2)}, u32[]{:S(2)}) collective-permute-start(bf16[4,256,128]{2,1,0:T(8,128)(2,1)S(1)} %collective-permute-done.9.refs_8_), channel_id=1, source_target_pairs={{0,32},{8,232},{16,48},{24,248},{32,64},{40,8},{48,80},{56,24},{64... | collective-permute-start | bytes 786440 | tf_op jit(solution)/shard_map/ppermute | solution.py:38
  43.1 2.8 %collective-permute-start.4 = (bf16[4,256,128]{2,1,0:T(8,128)(2,1)S(1)}, bf16[4,256,128]{2,1,0:T(8,128)(2,1)S(1)}, u32[]{:S(2)}, u32[]{:S(2)}) collective-permute-start(bf16[4,256,128]{2,1,0:T(8,128)(2,1)S(1)} %collective-permute-done.3.refs_2_), channel_id=1, source_target_pairs={{0,32},{8,232},{16,48},{24,248},{32,64},{40,8},{48,80},{56,24},{64... | collective-permute-start | bytes 786440 | tf_op jit(solution)/shard_map/ppermute | solution.py:38
  46.0 0.5 collective-permute-done.10.refs_9_
  46.6 5.7 %collective-permute-start.12 = (bf16[12,256,128]{2,1,0:T(8,128)(2,1)S(1)}, bf16[12,256,128]{2,1,0:T(8,128)(2,1)S(1)}, u32[]{:S(2)}, u32[]{:S(2)}) collective-permute-start(bf16[12,256,128]{2,1,0:T(8,128)(2,1)S(1)} %pad_maximum_fusion.1), channel_id=1, source_target_pairs={{0,8},{8,0},{16,24},{24,16},{32,40},{40,32},{48,56},{56,48},{64,72... | collective-permute-start | bytes 2359304 | tf_op jit(solution)/shard_map/ppermute | solution.py:38
  52.4 2.7 %collective-permute-start.6 = (bf16[12,256,128]{2,1,0:T(8,128)(2,1)S(1)}, bf16[12,256,128]{2,1,0:T(8,128)(2,1)S(1)}, u32[]{:S(2)}, u32[]{:S(2)}) collective-permute-start(bf16[12,256,128]{2,1,0:T(8,128)(2,1)S(1)} %pad_maximum_fusion), channel_id=1, source_target_pairs={{0,8},{8,0},{16,24},{24,16},{32,40},{40,32},{48,56},{56,48},{64,72... | collective-permute-start | bytes 2359304 | tf_op jit(solution)/shard_map/ppermute | solution.py:38
  55.2 2.7 %collective-permute-start.13 = (bf16[2,256,128]{2,1,0:T(8,128)(2,1)S(1)}, bf16[2,256,128]{2,1,0:T(8,128)(2,1)S(1)}, u32[]{:S(2)}, u32[]{:S(2)}) collective-permute-start(bf16[2,256,128]{2,1,0:T(8,128)(2,1)S(1)} %slice.11), channel_id=1, source_target_pairs={{0,8},{8,16},{16,24},{24,32},{32,40},{40,48},{48,56},{56,64},{64,7... | collective-permute-start | bytes 393224 | tf_op jit(solution)/shard_map/ppermute | solution.py:24
  57.9 1.7 %collective-permute-done.13.refs_12_ = bf16[2,256,128]{2,1,0:T(8,128)(2,1)S(1)} collective-permute-done((bf16[2,256,128]{2,1,0:T(8,128)(2,1)S(1)}, bf16[2,256,128]{2,1,0:T(8,128)(2,1)S(1)}, u32[]{:S(2)}, u32[]{:S(2)}) %collective-permute-start.13) | collective-permute-done | bytes 131104 | tf_op jit(solution)/shard_map/ppermute | solution.py:24
  59.7 0.9 %collective-permute-done.11.refs_10_ = bf16[4,256,128]{2,1,0:T(8,128)(2,1)S(1)} collective-permute-done((bf16[4,256,128]{2,1,0:T(8,128)(2,1)S(1)}, bf16[4,256,128]{2,1,0:T(8,128)(2,1)S(1)}, u32[]{:S(2)}, u32[]{:S(2)}) %collective-permute-start.11) | collective-permute-done | bytes 262176 | tf_op jit(solution)/shard_map/ppermute | solution.py:38
  60.6 2.8 %collective-permute-done.5.refs_4_ = bf16[4,256,128]{2,1,0:T(8,128)(2,1)S(1)} collective-permute-done((bf16[4,256,128]{2,1,0:T(8,128)(2,1)S(1)}, bf16[4,256,128]{2,1,0:T(8,128)(2,1)S(1)}, u32[]{:S(2)}, u32[]{:S(2)}) %collective-permute-start.5) | collective-permute-done | bytes 262176 | tf_op jit(solution)/shard_map/ppermute | solution.py:38
  63.5 0.7 copy-done.12
  64.4 0.9 copy-done.9
  65.3 26.0 %shard_map.73 = bf16[384,1024]{1,0:T(8,128)(2,1)} custom-call(s32[31]{0:T(128)} %len_ref.1, s32[31]{0:T(128)} %group_ref.1, s32[31]{0:T(128)} %order_ref.1, s32[32]{0:T(128)} %owner_ref.1, bf16[384,1024]{1,0:T(8,128)(2,1)} %q_ref.1, bf16[4,256,128]{2,1,0:T(8,128)(2,1)} %copy-done.1, bf16[4,256,128]{2,1,0:T(8,128)(2,1)} %copy-done.3, ...), custom_call_target="tpu_custom_call" | custom-call | tf_op jit(solution)/shard_map/pallas_call | solution.py:227
  (45 shorter events, 2.2 us)
Async XLA Ops:
  16.6 3.2 %collective-permute-start = (bf16[2,1,256,128]{3,2,1,0:T(8,128)(2,1)S(1)}, bf16[2,1,256,128]{3,2,1,0:T(8,128)(2,1)S(1)}, u32[]{:S(2)}, u32[]{:S(2)}) collective-permute-start(bf16[2,1,256,128]{3,2,1,0:T(8,128)(2,1)S(1)} %bitcast.13), channel_id=1, source_target_pairs={{0,8},{8,0},{16,24},{24,16},{32,40},{40,32},{48,56},{56,48},{64,72... | collective-permute-start | bytes 393224 | tf_op jit(solution)/shard_map/ppermute | solution.py:40
  19.8 4.8 %collective-permute-start.7 = (bf16[2,256,128]{2,1,0:T(8,128)(2,1)S(1)}, bf16[2,256,128]{2,1,0:T(8,128)(2,1)S(1)}, u32[]{:S(2)}, u32[]{:S(2)}) collective-permute-start(bf16[2,256,128]{2,1,0:T(8,128)(2,1)S(1)} %get-tuple-element.5), channel_id=1, source_target_pairs={{0,16},{8,24},{16,0},{24,8},{32,48},{40,56},{48,32},{56,40},{64,80... | collective-permute-start | bytes 393224 | tf_op jit(solution)/shard_map/ppermute | solution.py:38
  20.2 10.1 %collective-permute-start.1 = (bf16[2,256,128]{2,1,0:T(8,128)(2,1)S(1)}, bf16[2,256,128]{2,1,0:T(8,128)(2,1)S(1)}, u32[]{:S(2)}, u32[]{:S(2)}) collective-permute-start(bf16[2,256,128]{2,1,0:T(8,128)(2,1)S(1)} %get-tuple-element.6), channel_id=1, source_target_pairs={{0,16},{8,24},{16,0},{24,8},{32,48},{40,56},{48,32},{56,40},{64,80... | collective-permute-start | bytes 393224 | tf_op jit(solution)/shard_map/ppermute | solution.py:38
  24.6 5.7 %copy-start = (bf16[4,256,128]{2,1,0:T(8,128)(2,1)}, bf16[4,256,128]{2,1,0:T(8,128)(2,1)S(1)}, u32[]{:S(2)}) copy-start(bf16[4,256,128]{2,1,0:T(8,128)(2,1)S(1)} %maximum_select_fusion.2.refs_6_) | copy-start | bytes 786436
  24.6 9.0 %collective-permute-start.8 = (bf16[4,256,128]{2,1,0:T(8,128)(2,1)S(1)}, bf16[4,256,128]{2,1,0:T(8,128)(2,1)S(1)}, u32[]{:S(2)}, u32[]{:S(2)}) collective-permute-start(bf16[4,256,128]{2,1,0:T(8,128)(2,1)S(1)} %maximum_select_fusion.2.refs_6_), channel_id=1, source_target_pairs={{0,32},{8,232},{16,48},{24,248},{32,64},{40,8},{48,80},{56,24},{64... | collective-permute-start | bytes 786440 | tf_op jit(solution)/shard_map/ppermute | solution.py:38
  30.3 16.2 %copy-start.1 = (bf16[4,256,128]{2,1,0:T(8,128)(2,1)}, bf16[4,256,128]{2,1,0:T(8,128)(2,1)S(1)}, u32[]{:S(2)}) copy-start(bf16[4,256,128]{2,1,0:T(8,128)(2,1)S(1)} %maximum_select_fusion.1.refs_0_) | copy-start | bytes 786436
  30.3 6.4 %collective-permute-start.2 = (bf16[4,256,128]{2,1,0:T(8,128)(2,1)S(1)}, bf16[4,256,128]{2,1,0:T(8,128)(2,1)S(1)}, u32[]{:S(2)}, u32[]{:S(2)}) collective-permute-start(bf16[4,256,128]{2,1,0:T(8,128)(2,1)S(1)} %maximum_select_fusion.1.refs_0_), channel_id=1, source_target_pairs={{0,32},{8,232},{16,48},{24,248},{32,64},{40,8},{48,80},{56,24},{64... | collective-permute-start | bytes 786440 | tf_op jit(solution)/shard_map/ppermute | solution.py:38
  33.6 13.0 %copy-start.2 = (bf16[4,256,128]{2,1,0:T(8,128)(2,1)}, bf16[4,256,128]{2,1,0:T(8,128)(2,1)S(1)}, u32[]{:S(2)}) copy-start(bf16[4,256,128]{2,1,0:T(8,128)(2,1)S(1)} %collective-permute-done.8.refs_7_) | copy-start | bytes 786436
  33.6 6.4 %collective-permute-start.9 = (bf16[4,256,128]{2,1,0:T(8,128)(2,1)S(1)}, bf16[4,256,128]{2,1,0:T(8,128)(2,1)S(1)}, u32[]{:S(2)}, u32[]{:S(2)}) collective-permute-start(bf16[4,256,128]{2,1,0:T(8,128)(2,1)S(1)} %collective-permute-done.8.refs_7_), channel_id=1, source_target_pairs={{0,32},{8,232},{16,48},{24,248},{32,64},{40,8},{48,80},{56,24},{64... | collective-permute-start | bytes 786440 | tf_op jit(solution)/shard_map/ppermute | solution.py:38
  36.7 15.6 %copy-start.3 = (bf16[4,256,128]{2,1,0:T(8,128)(2,1)}, bf16[4,256,128]{2,1,0:T(8,128)(2,1)S(1)}, u32[]{:S(2)}) copy-start(bf16[4,256,128]{2,1,0:T(8,128)(2,1)S(1)} %collective-permute-done.2.refs_1_) | copy-start | bytes 786436
  36.7 6.4 %collective-permute-start.3 = (bf16[4,256,128]{2,1,0:T(8,128)(2,1)S(1)}, bf16[4,256,128]{2,1,0:T(8,128)(2,1)S(1)}, u32[]{:S(2)}, u32[]{:S(2)}) collective-permute-start(bf16[4,256,128]{2,1,0:T(8,128)(2,1)S(1)} %collective-permute-done.2.refs_1_), channel_id=1, source_target_pairs={{0,32},{8,232},{16,48},{24,248},{32,64},{40,8},{48,80},{56,24},{64... | collective-permute-start | bytes 786440 | tf_op jit(solution)/shard_map/ppermute | solution.py:38
  40.0 6.6 %copy-start.4 = (bf16[4,256,128]{2,1,0:T(8,128)(2,1)}, bf16[4,256,128]{2,1,0:T(8,128)(2,1)S(1)}, u32[]{:S(2)}) copy-start(bf16[4,256,128]{2,1,0:T(8,128)(2,1)S(1)} %collective-permute-done.9.refs_8_) | copy-start | bytes 786436
  40.0 6.4 %collective-permute-start.10 = (bf16[4,256,128]{2,1,0:T(8,128)(2,1)S(1)}, bf16[4,256,128]{2,1,0:T(8,128)(2,1)S(1)}, u32[]{:S(2)}, u32[]{:S(2)}) collective-permute-start(bf16[4,256,128]{2,1,0:T(8,128)(2,1)S(1)} %collective-permute-done.9.refs_8_), channel_id=1, source_target_pairs={{0,32},{8,232},{16,48},{24,248},{32,64},{40,8},{48,80},{56,24},{64... | collective-permute-start | bytes 786440 | tf_op jit(solution)/shard_map/ppermute | solution.py:38
  43.1 9.2 %copy-start.5 = (bf16[4,256,128]{2,1,0:T(8,128)(2,1)}, bf16[4,256,128]{2,1,0:T(8,128)(2,1)S(1)}, u32[]{:S(2)}) copy-start(bf16[4,256,128]{2,1,0:T(8,128)(2,1)S(1)} %collective-permute-done.3.refs_2_) | copy-start | bytes 786436
  43.1 9.2 %collective-permute-start.4 = (bf16[4,256,128]{2,1,0:T(8,128)(2,1)S(1)}, bf16[4,256,128]{2,1,0:T(8,128)(2,1)S(1)}, u32[]{:S(2)}, u32[]{:S(2)}) collective-permute-start(bf16[4,256,128]{2,1,0:T(8,128)(2,1)S(1)} %collective-permute-done.3.refs_2_), channel_id=1, source_target_pairs={{0,32},{8,232},{16,48},{24,248},{32,64},{40,8},{48,80},{56,24},{64... | collective-permute-start | bytes 786440 | tf_op jit(solution)/shard_map/ppermute | solution.py:38
  46.5 8.6 %copy-start.6 = (bf16[4,256,128]{2,1,0:T(8,128)(2,1)}, bf16[4,256,128]{2,1,0:T(8,128)(2,1)S(1)}, u32[]{:S(2)}) copy-start(bf16[4,256,128]{2,1,0:T(8,128)(2,1)S(1)} %collective-permute-done.10.refs_9_) | copy-start | bytes 786436
  46.6 8.6 %copy-start.10 = (bf16[2,384,128]{2,1,0:T(8,128)(2,1)S(1)}, bf16[2,384,128]{2,1,0:T(8,128)(2,1)}, u32[]{:S(2)}) copy-start(bf16[2,384,128]{2,1,0:T(8,128)(2,1)} %refs_13_.1) | copy-start | bytes 589828
  46.6 16.8 %collective-permute-start.12 = (bf16[12,256,128]{2,1,0:T(8,128)(2,1)S(1)}, bf16[12,256,128]{2,1,0:T(8,128)(2,1)S(1)}, u32[]{:S(2)}, u32[]{:S(2)}) collective-permute-start(bf16[12,256,128]{2,1,0:T(8,128)(2,1)S(1)} %pad_maximum_fusion.1), channel_id=1, source_target_pairs={{0,8},{8,0},{16,24},{24,16},{32,40},{40,32},{48,56},{56,48},{64,72... | collective-permute-start | bytes 2359304 | tf_op jit(solution)/shard_map/ppermute | solution.py:38
  52.4 11.0 %collective-permute-start.6 = (bf16[12,256,128]{2,1,0:T(8,128)(2,1)S(1)}, bf16[12,256,128]{2,1,0:T(8,128)(2,1)S(1)}, u32[]{:S(2)}, u32[]{:S(2)}) collective-permute-start(bf16[12,256,128]{2,1,0:T(8,128)(2,1)S(1)} %pad_maximum_fusion), channel_id=1, source_target_pairs={{0,8},{8,0},{16,24},{24,16},{32,40},{40,32},{48,56},{56,48},{64,72... | collective-permute-start | bytes 2359304 | tf_op jit(solution)/shard_map/ppermute | solution.py:38
  55.1 5.5 %collective-permute-start.11 = (bf16[4,256,128]{2,1,0:T(8,128)(2,1)S(1)}, bf16[4,256,128]{2,1,0:T(8,128)(2,1)S(1)}, u32[]{:S(2)}, u32[]{:S(2)}) collective-permute-start(bf16[4,256,128]{2,1,0:T(8,128)(2,1)S(1)} %collective-permute-done.10.refs_9_), channel_id=1, source_target_pairs={{0,32},{8,232},{16,48},{24,248},{32,64},{40,8},{48,80},{56,24},{64... | collective-permute-start | bytes 786440 | tf_op jit(solution)/shard_map/ppermute | solution.py:38
  55.1 8.3 %collective-permute-start.5 = (bf16[4,256,128]{2,1,0:T(8,128)(2,1)S(1)}, bf16[4,256,128]{2,1,0:T(8,128)(2,1)S(1)}, u32[]{:S(2)}, u32[]{:S(2)}) collective-permute-start(bf16[4,256,128]{2,1,0:T(8,128)(2,1)S(1)} %collective-permute-done.4.refs_3_), channel_id=1, source_target_pairs={{0,32},{8,232},{16,48},{24,248},{32,64},{40,8},{48,80},{56,24},{64... | collective-permute-start | bytes 786440 | tf_op jit(solution)/shard_map/ppermute | solution.py:38
  55.2 4.5 %collective-permute-start.13 = (bf16[2,256,128]{2,1,0:T(8,128)(2,1)S(1)}, bf16[2,256,128]{2,1,0:T(8,128)(2,1)S(1)}, u32[]{:S(2)}, u32[]{:S(2)}) collective-permute-start(bf16[2,256,128]{2,1,0:T(8,128)(2,1)S(1)} %slice.11), channel_id=1, source_target_pairs={{0,8},{8,16},{16,24},{24,32},{32,40},{40,48},{48,56},{56,64},{64,7... | collective-permute-start | bytes 393224 | tf_op jit(solution)/shard_map/ppermute | solution.py:24
  59.7 3.8 %copy-start.13 = (bf16[2,256,128]{2,1,0:T(8,128)(2,1)}, bf16[2,256,128]{2,1,0:T(8,128)(2,1)S(1)}, u32[]{:S(2)}) copy-start(bf16[2,256,128]{2,1,0:T(8,128)(2,1)S(1)} %collective-permute-done.13.refs_12_) | copy-start | bytes 393220
  60.6 2.8 %copy-start.11 = (bf16[4,256,128]{2,1,0:T(8,128)(2,1)}, bf16[4,256,128]{2,1,0:T(8,128)(2,1)S(1)}, u32[]{:S(2)}) copy-start(bf16[4,256,128]{2,1,0:T(8,128)(2,1)S(1)} %collective-permute-done.11.refs_10_) | copy-start | bytes 786436
  (4 other events, 5.4 us)

commit v4 on v3

--- a/solution.py
+++ b/solution.py
@@ -203,9 +203,10 @@
     requests = suffix_length.shape[0]
     half = tok_rows // 2
 
+    earlier = from_behind(suffix_kv[:, tok_rows - WINDOW :, :], "req", 1)
     local = lax.all_to_all(prefix_kv, "tp", split_axis=3, concat_axis=2, tiled=True)
+    local, earlier = lax.optimization_barrier((local, earlier))
     pieces = ring_gather(local)
-    earlier = from_behind(suffix_kv[:, tok_rows - WINDOW :, :], "req", 1)
 
     tiles_per_half = half // TILE
     grid = (2, tiles_per_half)

time: 91.9 us -> 92 us (level)
  Pallas kernels: 26 us -> 23 us
  waiting for transfers between devices: 11.2 us -> 13.9 us
    ppermute x12, waiting for transfers between devices: 8.47 us -> 12.9 us  [both(): return [lax.ppermute(x[kv], 'req', route(fn)) for kv in range(2)]]
    pallas_call x1, Pallas kernels: 26 us -> 23 us  [per_device(): pl.pallas_call(kernel, out_shape=jax.ShapeDtypeStruct((tok_rows, per_kv *...]
    ppermute x1, starting transfers between devices: 2.19 us -> 0.36 us  [ring_gather(): other = lax.ppermute(block, 'req', route(lambda i: i ^ 1))]
    ppermute x1, starting transfers between devices: 2.7 us -> 4.5 us  [from_behind(): return lax.ppermute(block, axis, route)]
    ppermute x1, waiting for transfers between devices: 1.75 us -> 0.01 us  [from_behind(): return lax.ppermute(block, axis, route)]
    slice x1, local copies, waits for them, and re-layouts: 0.01 us -> 0.95 us  [per_device(): earlier = from_behind(suffix_kv[:, tok_rows - WINDOW:, :], 'req', 1)]
  transfers between devices with their start and end apart: 14 -> 14, of which waited for: 8 -> 7; matrix products, arithmetic and copies ran while one was open for 0% -> 2% of each run, Pallas kernels for 0% -> 0%
where the time goes in v4:
time: 92 us; the launch traced here: 91.2 us
  starting transfers between devices  35.8 us (39%)
  Pallas kernels  23 us (25%)
  waiting for transfers between devices  13.9 us (15%)
  blocking collectives  13.4 us (15%)
  local copies, waits for them, and re-layouts  4.42 us (5%)
    ppermute x12, starting transfers between devices, both(): return [lax.ppermute(x[kv], 'req', route(fn)) for kv in range(2)]  30.9 us
    pallas_call x1, Pallas kernels, per_device(): pl.pallas_call(kernel, out_shape=jax.ShapeDtypeStruct((tok_rows, per_kv *...  23 us
    all_to_all x1, blocking collectives, per_device(): lax.all_to_all(prefix_kv, 'tp', split_axis=3, concat_axis=2, tiled=True)  13.4 us
    ppermute x12, waiting for transfers between devices, both(): return [lax.ppermute(x[kv], 'req', route(fn)) for kv in range(2)]  12.9 us
    ppermute x1, starting transfers between devices, from_behind(): return lax.ppermute(block, axis, route)  4.5 us
    unnamed x31, local copies, waits for them, and re-layouts  3.08 us
  transfers between devices with their start and end apart: 14, of which 7 were waited for; matrix products, arithmetic and copies ran while one was open for 2% of the time, Pallas kernels for 0%

profile of v4, /device:TPU:1, one launch (start us, length us, event | category | flops | bytes accessed | tf_op | source)
XLA Modules:
  0.0 91.2 jit_solution(4832943755836520671)
XLA Ops:
  0.0 0.9 %slice.9 = bf16[2,256,128]{2,1,0:T(8,128)(2,1)S(1)} slice(bf16[2,384,128]{2,1,0:T(8,128)(2,1)} %refs_13_.1), slice={[0:2], [128:384], [0:128]} | slice | bytes 262144 | tf_op jit(solution)/shard_map/slice | solution.py:206
  1.0 4.5 %collective-permute-start = (bf16[2,256,128]{2,1,0:T(8,128)(2,1)S(1)}, bf16[2,256,128]{2,1,0:T(8,128)(2,1)S(1)}, u32[]{:S(2)}, u32[]{:S(2)}) collective-permute-start(bf16[2,256,128]{2,1,0:T(8,128)(2,1)S(1)} %slice.9), channel_id=1, source_target_pairs={{0,8},{8,16},{16,24},{24,32},{32,40},{40,48},{48,56},{56,64},{64,7... | collective-permute-start | bytes 393224 | tf_op jit(solution)/shard_map/ppermute | solution.py:24
  5.9 0.5 reshape
  6.4 13.4 %all_to_all.18 = bf16[8,2,4096]{2,1,0:T(2,128)(2,1)S(1)} all-to-all(bf16[8,2,4096]{2,1,0:T(2,128)(2,1)S(1)} %reshape), channel_id=1, replica_groups=mesh['req'=32,'tp'=8] {'tp'}, dimensions={0} | all-to-all | bytes 262144 | tf_op jit(solution)/shard_map/all_to_all | solution.py:207
  20.8 1.1 %collective-permute-done.1 = bf16[2,1,256,128]{3,2,1,0:T(8,128)(2,1)S(1)} collective-permute-done((bf16[2,1,256,128]{3,2,1,0:T(8,128)(2,1)S(1)}, bf16[2,1,256,128]{3,2,1,0:T(8,128)(2,1)S(1)}, u32[]{:S(2)}, u32[]{:S(2)}) %collective-permute-start.1) | collective-permute-done | bytes 131104 | tf_op jit(solution)/shard_map/ppermute | solution.py:40
  22.0 1.1 %collective-permute-start.8 = (bf16[2,256,128]{2,1,0:T(8,128)(2,1)S(1)}, bf16[2,256,128]{2,1,0:T(8,128)(2,1)S(1)}, u32[]{:S(2)}, u32[]{:S(2)}) collective-permute-start(bf16[2,256,128]{2,1,0:T(8,128)(2,1)S(1)} %get-tuple-element.9), channel_id=1, source_target_pairs={{0,16},{8,24},{16,0},{24,8},{32,48},{40,56},{48,32},{56,40},{64,80... | collective-permute-start | bytes 393224 | tf_op jit(solution)/shard_map/ppermute | solution.py:38
  23.0 0.5 collective-permute-start.2
  23.5 3.3 %collective-permute-done.8 = bf16[2,256,128]{2,1,0:T(8,128)(2,1)S(1)} collective-permute-done((bf16[2,256,128]{2,1,0:T(8,128)(2,1)S(1)}, bf16[2,256,128]{2,1,0:T(8,128)(2,1)S(1)}, u32[]{:S(2)}, u32[]{:S(2)}) %collective-permute-start.8) | collective-permute-done | bytes 131104 | tf_op jit(solution)/shard_map/ppermute | solution.py:38
  26.9 6.1 %collective-permute-start.9 = (bf16[4,256,128]{2,1,0:T(8,128)(2,1)S(1)}, bf16[4,256,128]{2,1,0:T(8,128)(2,1)S(1)}, u32[]{:S(2)}, u32[]{:S(2)}) collective-permute-start(bf16[4,256,128]{2,1,0:T(8,128)(2,1)S(1)} %maximum_select_fusion.2.refs_6_), channel_id=1, source_target_pairs={{0,32},{8,232},{16,48},{24,248},{32,64},{40,8},{48,80},{56,24},{64... | collective-permute-start | bytes 786440 | tf_op jit(solution)/shard_map/ppermute | solution.py:38
  33.0 2.8 %collective-permute-start.3 = (bf16[4,256,128]{2,1,0:T(8,128)(2,1)S(1)}, bf16[4,256,128]{2,1,0:T(8,128)(2,1)S(1)}, u32[]{:S(2)}, u32[]{:S(2)}) collective-permute-start(bf16[4,256,128]{2,1,0:T(8,128)(2,1)S(1)} %maximum_select_fusion.1.refs_0_), channel_id=1, source_target_pairs={{0,32},{8,232},{16,48},{24,248},{32,64},{40,8},{48,80},{56,24},{64... | collective-permute-start | bytes 786440 | tf_op jit(solution)/shard_map/ppermute | solution.py:38
  35.7 0.5 collective-permute-done.9.refs_7_
  36.2 3.1 %collective-permute-start.10 = (bf16[4,256,128]{2,1,0:T(8,128)(2,1)S(1)}, bf16[4,256,128]{2,1,0:T(8,128)(2,1)S(1)}, u32[]{:S(2)}, u32[]{:S(2)}) collective-permute-start(bf16[4,256,128]{2,1,0:T(8,128)(2,1)S(1)} %collective-permute-done.9.refs_7_), channel_id=1, source_target_pairs={{0,32},{8,232},{16,48},{24,248},{32,64},{40,8},{48,80},{56,24},{64... | collective-permute-start | bytes 786440 | tf_op jit(solution)/shard_map/ppermute | solution.py:38
  39.4 2.8 %collective-permute-start.4 = (bf16[4,256,128]{2,1,0:T(8,128)(2,1)S(1)}, bf16[4,256,128]{2,1,0:T(8,128)(2,1)S(1)}, u32[]{:S(2)}, u32[]{:S(2)}) collective-permute-start(bf16[4,256,128]{2,1,0:T(8,128)(2,1)S(1)} %collective-permute-done.3.refs_1_), channel_id=1, source_target_pairs={{0,32},{8,232},{16,48},{24,248},{32,64},{40,8},{48,80},{56,24},{64... | collective-permute-start | bytes 786440 | tf_op jit(solution)/shard_map/ppermute | solution.py:38
  42.2 0.5 collective-permute-done.10.refs_8_
  42.7 3.1 %collective-permute-start.11 = (bf16[4,256,128]{2,1,0:T(8,128)(2,1)S(1)}, bf16[4,256,128]{2,1,0:T(8,128)(2,1)S(1)}, u32[]{:S(2)}, u32[]{:S(2)}) collective-permute-start(bf16[4,256,128]{2,1,0:T(8,128)(2,1)S(1)} %collective-permute-done.10.refs_8_), channel_id=1, source_target_pairs={{0,32},{8,232},{16,48},{24,248},{32,64},{40,8},{48,80},{56,24},{64... | collective-permute-start | bytes 786440 | tf_op jit(solution)/shard_map/ppermute | solution.py:38
  45.8 2.8 %collective-permute-start.5 = (bf16[4,256,128]{2,1,0:T(8,128)(2,1)S(1)}, bf16[4,256,128]{2,1,0:T(8,128)(2,1)S(1)}, u32[]{:S(2)}, u32[]{:S(2)}) collective-permute-start(bf16[4,256,128]{2,1,0:T(8,128)(2,1)S(1)} %collective-permute-done.4.refs_2_), channel_id=1, source_target_pairs={{0,32},{8,232},{16,48},{24,248},{32,64},{40,8},{48,80},{56,24},{64... | collective-permute-start | bytes 786440 | tf_op jit(solution)/shard_map/ppermute | solution.py:38
  48.6 0.5 collective-permute-done.11.refs_9_
  49.2 5.7 %collective-permute-start.13 = (bf16[12,256,128]{2,1,0:T(8,128)(2,1)S(1)}, bf16[12,256,128]{2,1,0:T(8,128)(2,1)S(1)}, u32[]{:S(2)}, u32[]{:S(2)}) collective-permute-start(bf16[12,256,128]{2,1,0:T(8,128)(2,1)S(1)} %pad_maximum_fusion.1), channel_id=1, source_target_pairs={{0,8},{8,0},{16,24},{24,16},{32,40},{40,32},{48,56},{56,48},{64,72... | collective-permute-start | bytes 2359304 | tf_op jit(solution)/shard_map/ppermute | solution.py:38
  55.1 2.7 %collective-permute-start.7 = (bf16[12,256,128]{2,1,0:T(8,128)(2,1)S(1)}, bf16[12,256,128]{2,1,0:T(8,128)(2,1)S(1)}, u32[]{:S(2)}, u32[]{:S(2)}) collective-permute-start(bf16[12,256,128]{2,1,0:T(8,128)(2,1)S(1)} %pad_maximum_fusion), channel_id=1, source_target_pairs={{0,8},{8,0},{16,24},{24,16},{32,40},{40,32},{48,56},{56,48},{64,72... | collective-permute-start | bytes 2359304 | tf_op jit(solution)/shard_map/ppermute | solution.py:38
  58.0 5.2 %collective-permute-done.12.refs_10_ = bf16[4,256,128]{2,1,0:T(8,128)(2,1)S(1)} collective-permute-done((bf16[4,256,128]{2,1,0:T(8,128)(2,1)S(1)}, bf16[4,256,128]{2,1,0:T(8,128)(2,1)S(1)}, u32[]{:S(2)}, u32[]{:S(2)}) %collective-permute-start.12) | collective-permute-done | bytes 262176 | tf_op jit(solution)/shard_map/ppermute | solution.py:38
  63.3 2.8 %collective-permute-done.6.refs_4_ = bf16[4,256,128]{2,1,0:T(8,128)(2,1)S(1)} collective-permute-done((bf16[4,256,128]{2,1,0:T(8,128)(2,1)S(1)}, bf16[4,256,128]{2,1,0:T(8,128)(2,1)S(1)}, u32[]{:S(2)}, u32[]{:S(2)}) %collective-permute-start.6) | collective-permute-done | bytes 262176 | tf_op jit(solution)/shard_map/ppermute | solution.py:38
  66.1 0.7 copy-done.11
  67.1 0.9 copy-done.9
  68.0 23.0 %shard_map.73 = bf16[384,1024]{1,0:T(8,128)(2,1)} custom-call(s32[31]{0:T(128)} %len_ref.1, s32[31]{0:T(128)} %group_ref.1, s32[31]{0:T(128)} %order_ref.1, s32[32]{0:T(128)} %owner_ref.1, bf16[384,1024]{1,0:T(8,128)(2,1)} %q_ref.1, bf16[4,256,128]{2,1,0:T(8,128)(2,1)} %copy-done.1, bf16[4,256,128]{2,1,0:T(8,128)(2,1)} %copy-done.3, ...), custom_call_target="tpu_custom_call" | custom-call | tf_op jit(solution)/shard_map/pallas_call | solution.py:228
  (45 shorter events, 2.3 us)
Async XLA Ops:
  0.0 5.5 %copy-start.12 = (bf16[2,1,32,1024]{3,2,1,0:T(8,128)(2,1)S(1)}, bf16[2,1,32,1024]{3,2,1,0:T(8,128)(2,1)}, u32[]{:S(2)}) copy-start(bf16[2,1,32,1024]{3,2,1,0:T(8,128)(2,1)} %param.9) | copy-start | bytes 393220
  1.0 19.5 %collective-permute-start = (bf16[2,256,128]{2,1,0:T(8,128)(2,1)S(1)}, bf16[2,256,128]{2,1,0:T(8,128)(2,1)S(1)}, u32[]{:S(2)}, u32[]{:S(2)}) collective-permute-start(bf16[2,256,128]{2,1,0:T(8,128)(2,1)S(1)} %slice.9), channel_id=1, source_target_pairs={{0,8},{8,16},{16,24},{24,32},{32,40},{40,48},{48,56},{56,64},{64,7... | collective-permute-start | bytes 393224 | tf_op jit(solution)/shard_map/ppermute | solution.py:24
  20.5 1.4 %collective-permute-start.1 = (bf16[2,1,256,128]{3,2,1,0:T(8,128)(2,1)S(1)}, bf16[2,1,256,128]{3,2,1,0:T(8,128)(2,1)S(1)}, u32[]{:S(2)}, u32[]{:S(2)}) collective-permute-start(bf16[2,1,256,128]{3,2,1,0:T(8,128)(2,1)S(1)} %bitcast.13), channel_id=1, source_target_pairs={{0,8},{8,0},{16,24},{24,16},{32,40},{40,32},{48,56},{56,48},{64,72... | collective-permute-start | bytes 393224 | tf_op jit(solution)/shard_map/ppermute | solution.py:40
  22.0 4.9 %collective-permute-start.8 = (bf16[2,256,128]{2,1,0:T(8,128)(2,1)S(1)}, bf16[2,256,128]{2,1,0:T(8,128)(2,1)S(1)}, u32[]{:S(2)}, u32[]{:S(2)}) collective-permute-start(bf16[2,256,128]{2,1,0:T(8,128)(2,1)S(1)} %get-tuple-element.9), channel_id=1, source_target_pairs={{0,16},{8,24},{16,0},{24,8},{32,48},{40,56},{48,32},{56,40},{64,80... | collective-permute-start | bytes 393224 | tf_op jit(solution)/shard_map/ppermute | solution.py:38
  23.0 9.9 %collective-permute-start.2 = (bf16[2,256,128]{2,1,0:T(8,128)(2,1)S(1)}, bf16[2,256,128]{2,1,0:T(8,128)(2,1)S(1)}, u32[]{:S(2)}, u32[]{:S(2)}) collective-permute-start(bf16[2,256,128]{2,1,0:T(8,128)(2,1)S(1)} %get-tuple-element.10), channel_id=1, source_target_pairs={{0,16},{8,24},{16,0},{24,8},{32,48},{40,56},{48,32},{56,40},{64,80... | collective-permute-start | bytes 393224 | tf_op jit(solution)/shard_map/ppermute | solution.py:38
  26.9 6.1 %copy-start = (bf16[4,256,128]{2,1,0:T(8,128)(2,1)}, bf16[4,256,128]{2,1,0:T(8,128)(2,1)S(1)}, u32[]{:S(2)}) copy-start(bf16[4,256,128]{2,1,0:T(8,128)(2,1)S(1)} %maximum_select_fusion.2.refs_6_) | copy-start | bytes 786436
  26.9 9.4 %collective-permute-start.9 = (bf16[4,256,128]{2,1,0:T(8,128)(2,1)S(1)}, bf16[4,256,128]{2,1,0:T(8,128)(2,1)S(1)}, u32[]{:S(2)}, u32[]{:S(2)}) collective-permute-start(bf16[4,256,128]{2,1,0:T(8,128)(2,1)S(1)} %maximum_select_fusion.2.refs_6_), channel_id=1, source_target_pairs={{0,32},{8,232},{16,48},{24,248},{32,64},{40,8},{48,80},{56,24},{64... | collective-permute-start | bytes 786440 | tf_op jit(solution)/shard_map/ppermute | solution.py:38
  33.0 16.2 %copy-start.1 = (bf16[4,256,128]{2,1,0:T(8,128)(2,1)}, bf16[4,256,128]{2,1,0:T(8,128)(2,1)S(1)}, u32[]{:S(2)}) copy-start(bf16[4,256,128]{2,1,0:T(8,128)(2,1)S(1)} %maximum_select_fusion.1.refs_0_) | copy-start | bytes 786436
  33.0 6.4 %collective-permute-start.3 = (bf16[4,256,128]{2,1,0:T(8,128)(2,1)S(1)}, bf16[4,256,128]{2,1,0:T(8,128)(2,1)S(1)}, u32[]{:S(2)}, u32[]{:S(2)}) collective-permute-start(bf16[4,256,128]{2,1,0:T(8,128)(2,1)S(1)} %maximum_select_fusion.1.refs_0_), channel_id=1, source_target_pairs={{0,32},{8,232},{16,48},{24,248},{32,64},{40,8},{48,80},{56,24},{64... | collective-permute-start | bytes 786440 | tf_op jit(solution)/shard_map/ppermute | solution.py:38
  36.2 13.0 %copy-start.2 = (bf16[4,256,128]{2,1,0:T(8,128)(2,1)}, bf16[4,256,128]{2,1,0:T(8,128)(2,1)S(1)}, u32[]{:S(2)}) copy-start(bf16[4,256,128]{2,1,0:T(8,128)(2,1)S(1)} %collective-permute-done.9.refs_7_) | copy-start | bytes 786436
  36.2 6.4 %collective-permute-start.10 = (bf16[4,256,128]{2,1,0:T(8,128)(2,1)S(1)}, bf16[4,256,128]{2,1,0:T(8,128)(2,1)S(1)}, u32[]{:S(2)}, u32[]{:S(2)}) collective-permute-start(bf16[4,256,128]{2,1,0:T(8,128)(2,1)S(1)} %collective-permute-done.9.refs_7_), channel_id=1, source_target_pairs={{0,32},{8,232},{16,48},{24,248},{32,64},{40,8},{48,80},{56,24},{64... | collective-permute-start | bytes 786440 | tf_op jit(solution)/shard_map/ppermute | solution.py:38
  39.4 15.6 %copy-start.3 = (bf16[4,256,128]{2,1,0:T(8,128)(2,1)}, bf16[4,256,128]{2,1,0:T(8,128)(2,1)S(1)}, u32[]{:S(2)}) copy-start(bf16[4,256,128]{2,1,0:T(8,128)(2,1)S(1)} %collective-permute-done.3.refs_1_) | copy-start | bytes 786436
  39.4 6.4 %collective-permute-start.4 = (bf16[4,256,128]{2,1,0:T(8,128)(2,1)S(1)}, bf16[4,256,128]{2,1,0:T(8,128)(2,1)S(1)}, u32[]{:S(2)}, u32[]{:S(2)}) collective-permute-start(bf16[4,256,128]{2,1,0:T(8,128)(2,1)S(1)} %collective-permute-done.3.refs_1_), channel_id=1, source_target_pairs={{0,32},{8,232},{16,48},{24,248},{32,64},{40,8},{48,80},{56,24},{64... | collective-permute-start | bytes 786440 | tf_op jit(solution)/shard_map/ppermute | solution.py:38
  42.7 6.6 %copy-start.4 = (bf16[4,256,128]{2,1,0:T(8,128)(2,1)}, bf16[4,256,128]{2,1,0:T(8,128)(2,1)S(1)}, u32[]{:S(2)}) copy-start(bf16[4,256,128]{2,1,0:T(8,128)(2,1)S(1)} %collective-permute-done.10.refs_8_) | copy-start | bytes 786436
  42.7 6.4 %collective-permute-start.11 = (bf16[4,256,128]{2,1,0:T(8,128)(2,1)S(1)}, bf16[4,256,128]{2,1,0:T(8,128)(2,1)S(1)}, u32[]{:S(2)}, u32[]{:S(2)}) collective-permute-start(bf16[4,256,128]{2,1,0:T(8,128)(2,1)S(1)} %collective-permute-done.10.refs_8_), channel_id=1, source_target_pairs={{0,32},{8,232},{16,48},{24,248},{32,64},{40,8},{48,80},{56,24},{64... | collective-permute-start | bytes 786440 | tf_op jit(solution)/shard_map/ppermute | solution.py:38
  45.8 9.2 %copy-start.5 = (bf16[4,256,128]{2,1,0:T(8,128)(2,1)}, bf16[4,256,128]{2,1,0:T(8,128)(2,1)S(1)}, u32[]{:S(2)}) copy-start(bf16[4,256,128]{2,1,0:T(8,128)(2,1)S(1)} %collective-permute-done.4.refs_2_) | copy-start | bytes 786436
  45.8 9.2 %collective-permute-start.5 = (bf16[4,256,128]{2,1,0:T(8,128)(2,1)S(1)}, bf16[4,256,128]{2,1,0:T(8,128)(2,1)S(1)}, u32[]{:S(2)}, u32[]{:S(2)}) collective-permute-start(bf16[4,256,128]{2,1,0:T(8,128)(2,1)S(1)} %collective-permute-done.4.refs_2_), channel_id=1, source_target_pairs={{0,32},{8,232},{16,48},{24,248},{32,64},{40,8},{48,80},{56,24},{64... | collective-permute-start | bytes 786440 | tf_op jit(solution)/shard_map/ppermute | solution.py:38
  49.1 8.6 %copy-start.6 = (bf16[4,256,128]{2,1,0:T(8,128)(2,1)}, bf16[4,256,128]{2,1,0:T(8,128)(2,1)S(1)}, u32[]{:S(2)}) copy-start(bf16[4,256,128]{2,1,0:T(8,128)(2,1)S(1)} %collective-permute-done.11.refs_9_) | copy-start | bytes 786436
  49.2 16.9 %collective-permute-start.13 = (bf16[12,256,128]{2,1,0:T(8,128)(2,1)S(1)}, bf16[12,256,128]{2,1,0:T(8,128)(2,1)S(1)}, u32[]{:S(2)}, u32[]{:S(2)}) collective-permute-start(bf16[12,256,128]{2,1,0:T(8,128)(2,1)S(1)} %pad_maximum_fusion.1), channel_id=1, source_target_pairs={{0,8},{8,0},{16,24},{24,16},{32,40},{40,32},{48,56},{56,48},{64,72... | collective-permute-start | bytes 2359304 | tf_op jit(solution)/shard_map/ppermute | solution.py:38
  55.0 2.8 %copy-start.7 = (bf16[4,256,128]{2,1,0:T(8,128)(2,1)}, bf16[4,256,128]{2,1,0:T(8,128)(2,1)S(1)}, u32[]{:S(2)}) copy-start(bf16[4,256,128]{2,1,0:T(8,128)(2,1)S(1)} %collective-permute-done.5.refs_3_) | copy-start | bytes 786436
  55.1 11.0 %collective-permute-start.7 = (bf16[12,256,128]{2,1,0:T(8,128)(2,1)S(1)}, bf16[12,256,128]{2,1,0:T(8,128)(2,1)S(1)}, u32[]{:S(2)}, u32[]{:S(2)}) collective-permute-start(bf16[12,256,128]{2,1,0:T(8,128)(2,1)S(1)} %pad_maximum_fusion), channel_id=1, source_target_pairs={{0,8},{8,0},{16,24},{24,16},{32,40},{40,32},{48,56},{56,48},{64,72... | collective-permute-start | bytes 2359304 | tf_op jit(solution)/shard_map/ppermute | solution.py:38
  57.8 5.5 %collective-permute-start.12 = (bf16[4,256,128]{2,1,0:T(8,128)(2,1)S(1)}, bf16[4,256,128]{2,1,0:T(8,128)(2,1)S(1)}, u32[]{:S(2)}, u32[]{:S(2)}) collective-permute-start(bf16[4,256,128]{2,1,0:T(8,128)(2,1)S(1)} %collective-permute-done.11.refs_9_), channel_id=1, source_target_pairs={{0,32},{8,232},{16,48},{24,248},{32,64},{40,8},{48,80},{56,24},{64... | collective-permute-start | bytes 786440 | tf_op jit(solution)/shard_map/ppermute | solution.py:38
  57.8 8.3 %collective-permute-start.6 = (bf16[4,256,128]{2,1,0:T(8,128)(2,1)S(1)}, bf16[4,256,128]{2,1,0:T(8,128)(2,1)S(1)}, u32[]{:S(2)}, u32[]{:S(2)}) collective-permute-start(bf16[4,256,128]{2,1,0:T(8,128)(2,1)S(1)} %collective-permute-done.5.refs_3_), channel_id=1, source_target_pairs={{0,32},{8,232},{16,48},{24,248},{32,64},{40,8},{48,80},{56,24},{64... | collective-permute-start | bytes 786440 | tf_op jit(solution)/shard_map/ppermute | solution.py:38
  63.3 2.8 %copy-start.10 = (bf16[4,256,128]{2,1,0:T(8,128)(2,1)}, bf16[4,256,128]{2,1,0:T(8,128)(2,1)S(1)}, u32[]{:S(2)}) copy-start(bf16[4,256,128]{2,1,0:T(8,128)(2,1)S(1)} %collective-permute-done.12.refs_10_) | copy-start | bytes 786436
  (4 other events, 4.1 us)

commit v5 on v4

--- a/solution.py
+++ b/solution.py
@@ -46,9 +46,15 @@
         for t, o in zip(two, other)
     ]
     walked = [four]
-    for _ in range(reach):
+    for _ in range(reach - 1):
         walked.append(both(walked[-1], lambda i: i + 4 if i % 2 == 0 else i - 4))
-    mine = [jnp.concatenate([w[kv] for w in walked[1:reach]], 0) for kv in range(2)]
+    walked.append(
+        [
+            lax.ppermute(walked[-1][0], "req", [(i, (i + 4) % n) for i in range(0, n, 2)]),
+            lax.ppermute(walked[-1][1], "req", [(i, (i - 4) % n) for i in range(1, n, 2)]),
+        ]
+    )
+    mine = [jnp.concatenate([w[kv] for w in walked[1:]], 0) for kv in range(2)]
     swapped = both(mine, lambda i: i ^ 1)
     return [[w[kv] for w in walked] + [swapped[kv]] for kv in range(2)]
 
@@ -102,19 +108,38 @@
     def dst(hh, kv, b):
         return buf.at[hh, kv, pl.ds(b * block_rows, block_rows), :]
 
+    def copy(kv, p, at, hh, b):
+        pltpu.make_async_copy(
+            piece_refs[kv][p].at[at], dst(hh, kv, b), sems.at[hh, kv, b]
+        ).start()
+
     def start_copy(hh, b):
         where = position(hh, b)
         place = where // group
-        for p in range(n_pieces):
-            hit = (place == p) if p < last else (place >= last)
-            at = where % group if p < last else where - last * group
-
-            @pl.when(hit)
+        j = where % group
+        for p in range(reach):
+
+            @pl.when(place == p)
             def _():
                 for kv in range(2):
-                    pltpu.make_async_copy(
-                        piece_refs[kv][p].at[at], dst(hh, kv, b), sems.at[hh, kv, b]
-                    ).start()
+                    copy(kv, p, j, hh, b)
+
+        tail = (reach - 1) * group + j
+
+        @pl.when((place == reach) & (core == 0))
+        def _():
+            copy(0, reach, j, hh, b)
+            copy(1, last, tail, hh, b)
+
+        @pl.when((place == reach) & (core == 1))
+        def _():
+            copy(0, last, tail, hh, b)
+            copy(1, reach, j, hh, b)
+
+        @pl.when(place > reach)
+        def _():
+            for kv in range(2):
+                copy(kv, last, where - (reach + 1) * group, hh, b)
 
     def wait_copy(hh, b):
         for kv in range(2):

time: 92 us -> 93.2 us (1.013); the launches traced: 91.2 us -> 93.5 us
  starting transfers between devices: 35.8 us -> 40.4 us
  waiting for transfers between devices: 13.9 us -> 10.7 us
    ppermute x0 -> x2, starting transfers between devices: none -> 5.68 us  [the longest x1 5.01 us: ring_gather(): lax.ppermute(walked[-1][1], 'req', [(i, (i - 4) % n) for i in range(1, n,...]
    ppermute x12 -> x10, waiting for transfers between devices: 12.9 us -> 9.59 us  [both(): return [lax.ppermute(x[kv], 'req', route(fn)) for kv in range(2)]]
    ppermute x12 -> x10, starting transfers between devices: 30.9 us -> 29.9 us  [both(): return [lax.ppermute(x[kv], 'req', route(fn)) for kv in range(2)]]
  transfers between devices with their start and end apart: 14 -> 14, of which waited for: 7 -> 8; matrix products, arithmetic and copies ran while one was open for 2% -> 2% of each run, Pallas kernels for 0% -> 0%
where the time goes in v5:
time: 93.2 us; the launch traced here: 93.5 us
  starting transfers between devices  40.4 us (43%)
  Pallas kernels  23.4 us (25%)
  blocking collectives  13.4 us (14%)
  waiting for transfers between devices  10.7 us (11%)
  local copies, waits for them, and re-layouts  4.91 us (5%)
    ppermute x10, starting transfers between devices, both(): return [lax.ppermute(x[kv], 'req', route(fn)) for kv in range(2)]  29.9 us
    pallas_call x1, Pallas kernels, per_device(): pl.pallas_call(kernel, out_shape=jax.ShapeDtypeStruct((tok_rows, per_kv *...  23.4 us
    all_to_all x1, blocking collectives, per_device(): lax.all_to_all(prefix_kv, 'tp', split_axis=3, concat_axis=2, tiled=True)  13.4 us
    ppermute x10, waiting for transfers between devices, both(): return [lax.ppermute(x[kv], 'req', route(fn)) for kv in range(2)]  9.59 us
    ppermute x1, starting transfers between devices, ring_gather(): lax.ppermute(walked[-1][1], 'req', [(i, (i - 4) % n) for i in range(1, n,...  5.01 us
    ppermute x1, starting transfers between devices, from_behind(): return lax.ppermute(block, axis, route)  4.5 us
    unnamed x31, local copies, waits for them, and re-layouts  3.57 us
  transfers between devices with their start and end apart: 14, of which 8 were waited for; matrix products, arithmetic and copies ran while one was open for 2% of the time, Pallas kernels for 0%

profile of v5, /device:TPU:1, one launch (start us, length us, event | category | flops | bytes accessed | tf_op | source)
XLA Modules:
  0.0 93.5 jit_solution(5925406644127801049)
XLA Ops:
  0.0 0.9 %slice.9 = bf16[2,256,128]{2,1,0:T(8,128)(2,1)S(1)} slice(bf16[2,384,128]{2,1,0:T(8,128)(2,1)} %refs_13_.1), slice={[0:2], [128:384], [0:128]} | slice | bytes 262144 | tf_op jit(solution)/shard_map/slice | solution.py:231
  1.0 4.5 %collective-permute-start = (bf16[2,256,128]{2,1,0:T(8,128)(2,1)S(1)}, bf16[2,256,128]{2,1,0:T(8,128)(2,1)S(1)}, u32[]{:S(2)}, u32[]{:S(2)}) collective-permute-start(bf16[2,256,128]{2,1,0:T(8,128)(2,1)S(1)} %slice.9), channel_id=1, source_target_pairs={{0,8},{8,16},{16,24},{24,32},{32,40},{40,48},{48,56},{56,64},{64,7... | collective-permute-start | bytes 393224 | tf_op jit(solution)/shard_map/ppermute | solution.py:24
  5.9 0.5 reshape
  6.4 13.4 %all_to_all.18 = bf16[8,2,4096]{2,1,0:T(2,128)(2,1)S(1)} all-to-all(bf16[8,2,4096]{2,1,0:T(2,128)(2,1)S(1)} %reshape), channel_id=1, replica_groups=mesh['req'=32,'tp'=8] {'tp'}, dimensions={0} | all-to-all | bytes 262144 | tf_op jit(solution)/shard_map/all_to_all | solution.py:232
  20.8 1.1 %collective-permute-done.1 = bf16[2,1,256,128]{3,2,1,0:T(8,128)(2,1)S(1)} collective-permute-done((bf16[2,1,256,128]{3,2,1,0:T(8,128)(2,1)S(1)}, bf16[2,1,256,128]{3,2,1,0:T(8,128)(2,1)S(1)}, u32[]{:S(2)}, u32[]{:S(2)}) %collective-permute-start.1) | collective-permute-done | bytes 131104 | tf_op jit(solution)/shard_map/ppermute | solution.py:40
  22.0 1.1 %collective-permute-start.2 = (bf16[2,256,128]{2,1,0:T(8,128)(2,1)S(1)}, bf16[2,256,128]{2,1,0:T(8,128)(2,1)S(1)}, u32[]{:S(2)}, u32[]{:S(2)}) collective-permute-start(bf16[2,256,128]{2,1,0:T(8,128)(2,1)S(1)} %get-tuple-element.10), channel_id=1, source_target_pairs={{0,16},{8,24},{16,0},{24,8},{32,48},{40,56},{48,32},{56,40},{64,80... | collective-permute-start | bytes 393224 | tf_op jit(solution)/shard_map/ppermute | solution.py:38
  23.5 3.3 %collective-permute-done.2 = bf16[2,256,128]{2,1,0:T(8,128)(2,1)S(1)} collective-permute-done((bf16[2,256,128]{2,1,0:T(8,128)(2,1)S(1)}, bf16[2,256,128]{2,1,0:T(8,128)(2,1)S(1)}, u32[]{:S(2)}, u32[]{:S(2)}) %collective-permute-start.2) | collective-permute-done | bytes 131104 | tf_op jit(solution)/shard_map/ppermute | solution.py:38
  26.9 6.1 %collective-permute-start.3 = (bf16[4,256,128]{2,1,0:T(8,128)(2,1)S(1)}, bf16[4,256,128]{2,1,0:T(8,128)(2,1)S(1)}, u32[]{:S(2)}, u32[]{:S(2)}) collective-permute-start(bf16[4,256,128]{2,1,0:T(8,128)(2,1)S(1)} %maximum_select_fusion.1.refs_0_), channel_id=1, source_target_pairs={{0,32},{8,232},{16,48},{24,248},{32,64},{40,8},{48,80},{56,24},{64... | collective-permute-start | bytes 786440 | tf_op jit(solution)/shard_map/ppermute | solution.py:38
  33.0 2.8 %collective-permute-start.9 = (bf16[4,256,128]{2,1,0:T(8,128)(2,1)S(1)}, bf16[4,256,128]{2,1,0:T(8,128)(2,1)S(1)}, u32[]{:S(2)}, u32[]{:S(2)}) collective-permute-start(bf16[4,256,128]{2,1,0:T(8,128)(2,1)S(1)} %maximum_select_fusion.2.refs_6_), channel_id=1, source_target_pairs={{0,32},{8,232},{16,48},{24,248},{32,64},{40,8},{48,80},{56,24},{64... | collective-permute-start | bytes 786440 | tf_op jit(solution)/shard_map/ppermute | solution.py:38
  36.2 3.1 %collective-permute-start.4 = (bf16[4,256,128]{2,1,0:T(8,128)(2,1)S(1)}, bf16[4,256,128]{2,1,0:T(8,128)(2,1)S(1)}, u32[]{:S(2)}, u32[]{:S(2)}) collective-permute-start(bf16[4,256,128]{2,1,0:T(8,128)(2,1)S(1)} %collective-permute-done.3.refs_1_), channel_id=1, source_target_pairs={{0,32},{8,232},{16,48},{24,248},{32,64},{40,8},{48,80},{56,24},{64... | collective-permute-start | bytes 786440 | tf_op jit(solution)/shard_map/ppermute | solution.py:38
  39.4 2.8 %collective-permute-start.10 = (bf16[4,256,128]{2,1,0:T(8,128)(2,1)S(1)}, bf16[4,256,128]{2,1,0:T(8,128)(2,1)S(1)}, u32[]{:S(2)}, u32[]{:S(2)}) collective-permute-start(bf16[4,256,128]{2,1,0:T(8,128)(2,1)S(1)} %collective-permute-done.9.refs_7_), channel_id=1, source_target_pairs={{0,32},{8,232},{16,48},{24,248},{32,64},{40,8},{48,80},{56,24},{64... | collective-permute-start | bytes 786440 | tf_op jit(solution)/shard_map/ppermute | solution.py:38
  42.2 0.5 collective-permute-done.4.refs_2_
  42.7 3.1 %collective-permute-start.5 = (bf16[4,256,128]{2,1,0:T(8,128)(2,1)S(1)}, bf16[4,256,128]{2,1,0:T(8,128)(2,1)S(1)}, u32[]{:S(2)}, u32[]{:S(2)}) collective-permute-start(bf16[4,256,128]{2,1,0:T(8,128)(2,1)S(1)} %collective-permute-done.4.refs_2_), channel_id=1, source_target_pairs={{0,32},{8,232},{16,48},{24,248},{32,64},{40,8},{48,80},{56,24},{64... | collective-permute-start | bytes 786440 | tf_op jit(solution)/shard_map/ppermute | solution.py:38
  45.8 2.8 %collective-permute-start.11 = (bf16[4,256,128]{2,1,0:T(8,128)(2,1)S(1)}, bf16[4,256,128]{2,1,0:T(8,128)(2,1)S(1)}, u32[]{:S(2)}, u32[]{:S(2)}) collective-permute-start(bf16[4,256,128]{2,1,0:T(8,128)(2,1)S(1)} %collective-permute-done.10.refs_8_), channel_id=1, source_target_pairs={{0,32},{8,232},{16,48},{24,248},{32,64},{40,8},{48,80},{56,24},{64... | collective-permute-start | bytes 786440 | tf_op jit(solution)/shard_map/ppermute | solution.py:38
  49.1 0.7 collective-permute-start.6
  49.8 2.1 %collective-permute-done.11.refs_9_ = bf16[4,256,128]{2,1,0:T(8,128)(2,1)S(1)} collective-permute-done((bf16[4,256,128]{2,1,0:T(8,128)(2,1)S(1)}, bf16[4,256,128]{2,1,0:T(8,128)(2,1)S(1)}, u32[]{:S(2)}, u32[]{:S(2)}) %collective-permute-start.11) | collective-permute-done | bytes 262176 | tf_op jit(solution)/shard_map/ppermute | solution.py:38
  51.9 5.0 %collective-permute-start.12 = (bf16[4,256,128]{2,1,0:T(8,128)(2,1)S(1)}, bf16[4,256,128]{2,1,0:T(8,128)(2,1)S(1)}, u32[]{:S(2)}, u32[]{:S(2)}) collective-permute-start(bf16[4,256,128]{2,1,0:T(8,128)(2,1)S(1)} %collective-permute-done.11.refs_9_), channel_id=1, source_target_pairs={{8,232},{24,248},{40,8},{56,24},{72,40},{88,56},{104,72},{120,88},... | collective-permute-start | bytes 786440 | tf_op jit(solution)/shard_map/ppermute | solution.py:54
  57.0 0.7 copy-done.10
  57.9 7.3 %collective-permute-start.7 = (bf16[16,256,128]{2,1,0:T(8,128)(2,1)S(1)}, bf16[16,256,128]{2,1,0:T(8,128)(2,1)S(1)}, u32[]{:S(2)}, u32[]{:S(2)}) collective-permute-start(bf16[16,256,128]{2,1,0:T(8,128)(2,1)S(1)} %pad_maximum_fusion), channel_id=1, source_target_pairs={{0,8},{8,0},{16,24},{24,16},{32,40},{40,32},{48,56},{56,48},{64,72... | collective-permute-start | bytes 3145736 | tf_op jit(solution)/shard_map/ppermute | solution.py:38
  65.2 0.7 copy-done.11
  66.4 1.1 %collective-permute-done.7.refs_5_ = bf16[16,256,128]{2,1,0:T(8,128)(2,1)S(1)} collective-permute-done((bf16[16,256,128]{2,1,0:T(8,128)(2,1)S(1)}, bf16[16,256,128]{2,1,0:T(8,128)(2,1)S(1)}, u32[]{:S(2)}, u32[]{:S(2)}) %collective-permute-start.7) | collective-permute-done | bytes 1048608 | tf_op jit(solution)/shard_map/ppermute | solution.py:38
  67.5 1.5 %collective-permute-done.13.refs_11_ = bf16[16,256,128]{2,1,0:T(8,128)(2,1)S(1)} collective-permute-done((bf16[16,256,128]{2,1,0:T(8,128)(2,1)S(1)}, bf16[16,256,128]{2,1,0:T(8,128)(2,1)S(1)}, u32[]{:S(2)}, u32[]{:S(2)}) %collective-permute-start.13) | collective-permute-done | bytes 1048608 | tf_op jit(solution)/shard_map/ppermute | solution.py:38
  69.0 1.0 %copy-done.3 = bf16[16,256,128]{2,1,0:T(8,128)(2,1)} copy-done((bf16[16,256,128]{2,1,0:T(8,128)(2,1)}, bf16[16,256,128]{2,1,0:T(8,128)(2,1)S(1)}, u32[]{:S(2)}) %copy-start.3) | copy-done | bytes 1048600
  70.0 23.4 %shard_map.73 = bf16[384,1024]{1,0:T(8,128)(2,1)} custom-call(s32[31]{0:T(128)} %len_ref.1, s32[31]{0:T(128)} %group_ref.1, s32[31]{0:T(128)} %order_ref.1, s32[32]{0:T(128)} %owner_ref.1, bf16[384,1024]{1,0:T(8,128)(2,1)} %q_ref.1, bf16[4,256,128]{2,1,0:T(8,128)(2,1)} %copy-done, bf16[4,256,128]{2,1,0:T(8,128)(2,1)} %copy-done.4, ...), custom_call_target="tpu_custom_call" | custom-call | tf_op jit(solution)/shard_map/pallas_call | solution.py:253
  (45 shorter events, 3.6 us)
Async XLA Ops:
  0.0 5.5 %copy-start.12 = (bf16[2,1,32,1024]{3,2,1,0:T(8,128)(2,1)S(1)}, bf16[2,1,32,1024]{3,2,1,0:T(8,128)(2,1)}, u32[]{:S(2)}) copy-start(bf16[2,1,32,1024]{3,2,1,0:T(8,128)(2,1)} %param.9) | copy-start | bytes 393220
  1.0 19.5 %collective-permute-start = (bf16[2,256,128]{2,1,0:T(8,128)(2,1)S(1)}, bf16[2,256,128]{2,1,0:T(8,128)(2,1)S(1)}, u32[]{:S(2)}, u32[]{:S(2)}) collective-permute-start(bf16[2,256,128]{2,1,0:T(8,128)(2,1)S(1)} %slice.9), channel_id=1, source_target_pairs={{0,8},{8,16},{16,24},{24,32},{32,40},{40,48},{48,56},{56,64},{64,7... | collective-permute-start | bytes 393224 | tf_op jit(solution)/shard_map/ppermute | solution.py:24
  20.5 1.4 %collective-permute-start.1 = (bf16[2,1,256,128]{3,2,1,0:T(8,128)(2,1)S(1)}, bf16[2,1,256,128]{3,2,1,0:T(8,128)(2,1)S(1)}, u32[]{:S(2)}, u32[]{:S(2)}) collective-permute-start(bf16[2,1,256,128]{3,2,1,0:T(8,128)(2,1)S(1)} %bitcast.13), channel_id=1, source_target_pairs={{0,8},{8,0},{16,24},{24,16},{32,40},{40,32},{48,56},{56,48},{64,72... | collective-permute-start | bytes 393224 | tf_op jit(solution)/shard_map/ppermute | solution.py:40
  22.0 4.9 %collective-permute-start.2 = (bf16[2,256,128]{2,1,0:T(8,128)(2,1)S(1)}, bf16[2,256,128]{2,1,0:T(8,128)(2,1)S(1)}, u32[]{:S(2)}, u32[]{:S(2)}) collective-permute-start(bf16[2,256,128]{2,1,0:T(8,128)(2,1)S(1)} %get-tuple-element.10), channel_id=1, source_target_pairs={{0,16},{8,24},{16,0},{24,8},{32,48},{40,56},{48,32},{56,40},{64,80... | collective-permute-start | bytes 393224 | tf_op jit(solution)/shard_map/ppermute | solution.py:38
  23.0 9.9 %collective-permute-start.8 = (bf16[2,256,128]{2,1,0:T(8,128)(2,1)S(1)}, bf16[2,256,128]{2,1,0:T(8,128)(2,1)S(1)}, u32[]{:S(2)}, u32[]{:S(2)}) collective-permute-start(bf16[2,256,128]{2,1,0:T(8,128)(2,1)S(1)} %get-tuple-element.9), channel_id=1, source_target_pairs={{0,16},{8,24},{16,0},{24,8},{32,48},{40,56},{48,32},{56,40},{64,80... | collective-permute-start | bytes 393224 | tf_op jit(solution)/shard_map/ppermute | solution.py:38
  26.9 6.1 %copy-start = (bf16[4,256,128]{2,1,0:T(8,128)(2,1)}, bf16[4,256,128]{2,1,0:T(8,128)(2,1)S(1)}, u32[]{:S(2)}) copy-start(bf16[4,256,128]{2,1,0:T(8,128)(2,1)S(1)} %maximum_select_fusion.1.refs_0_) | copy-start | bytes 786436
  26.9 9.4 %collective-permute-start.3 = (bf16[4,256,128]{2,1,0:T(8,128)(2,1)S(1)}, bf16[4,256,128]{2,1,0:T(8,128)(2,1)S(1)}, u32[]{:S(2)}, u32[]{:S(2)}) collective-permute-start(bf16[4,256,128]{2,1,0:T(8,128)(2,1)S(1)} %maximum_select_fusion.1.refs_0_), channel_id=1, source_target_pairs={{0,32},{8,232},{16,48},{24,248},{32,64},{40,8},{48,80},{56,24},{64... | collective-permute-start | bytes 786440 | tf_op jit(solution)/shard_map/ppermute | solution.py:38
  33.0 24.9 %copy-start.1 = (bf16[4,256,128]{2,1,0:T(8,128)(2,1)}, bf16[4,256,128]{2,1,0:T(8,128)(2,1)S(1)}, u32[]{:S(2)}) copy-start(bf16[4,256,128]{2,1,0:T(8,128)(2,1)S(1)} %maximum_select_fusion.2.refs_6_) | copy-start | bytes 786436
  33.0 6.4 %collective-permute-start.9 = (bf16[4,256,128]{2,1,0:T(8,128)(2,1)S(1)}, bf16[4,256,128]{2,1,0:T(8,128)(2,1)S(1)}, u32[]{:S(2)}, u32[]{:S(2)}) collective-permute-start(bf16[4,256,128]{2,1,0:T(8,128)(2,1)S(1)} %maximum_select_fusion.2.refs_6_), channel_id=1, source_target_pairs={{0,32},{8,232},{16,48},{24,248},{32,64},{40,8},{48,80},{56,24},{64... | collective-permute-start | bytes 786440 | tf_op jit(solution)/shard_map/ppermute | solution.py:38
  36.2 21.6 %copy-start.4 = (bf16[4,256,128]{2,1,0:T(8,128)(2,1)}, bf16[4,256,128]{2,1,0:T(8,128)(2,1)S(1)}, u32[]{:S(2)}) copy-start(bf16[4,256,128]{2,1,0:T(8,128)(2,1)S(1)} %collective-permute-done.3.refs_1_) | copy-start | bytes 786436
  36.2 6.4 %collective-permute-start.4 = (bf16[4,256,128]{2,1,0:T(8,128)(2,1)S(1)}, bf16[4,256,128]{2,1,0:T(8,128)(2,1)S(1)}, u32[]{:S(2)}, u32[]{:S(2)}) collective-permute-start(bf16[4,256,128]{2,1,0:T(8,128)(2,1)S(1)} %collective-permute-done.3.refs_1_), channel_id=1, source_target_pairs={{0,32},{8,232},{16,48},{24,248},{32,64},{40,8},{48,80},{56,24},{64... | collective-permute-start | bytes 786440 | tf_op jit(solution)/shard_map/ppermute | solution.py:38
  39.4 25.8 %copy-start.5 = (bf16[4,256,128]{2,1,0:T(8,128)(2,1)}, bf16[4,256,128]{2,1,0:T(8,128)(2,1)S(1)}, u32[]{:S(2)}) copy-start(bf16[4,256,128]{2,1,0:T(8,128)(2,1)S(1)} %collective-permute-done.9.refs_7_) | copy-start | bytes 786436
  39.4 6.4 %collective-permute-start.10 = (bf16[4,256,128]{2,1,0:T(8,128)(2,1)S(1)}, bf16[4,256,128]{2,1,0:T(8,128)(2,1)S(1)}, u32[]{:S(2)}, u32[]{:S(2)}) collective-permute-start(bf16[4,256,128]{2,1,0:T(8,128)(2,1)S(1)} %collective-permute-done.9.refs_7_), channel_id=1, source_target_pairs={{0,32},{8,232},{16,48},{24,248},{32,64},{40,8},{48,80},{56,24},{64... | collective-permute-start | bytes 786440 | tf_op jit(solution)/shard_map/ppermute | solution.py:38
  42.7 15.2 %copy-start.6 = (bf16[4,256,128]{2,1,0:T(8,128)(2,1)}, bf16[4,256,128]{2,1,0:T(8,128)(2,1)S(1)}, u32[]{:S(2)}) copy-start(bf16[4,256,128]{2,1,0:T(8,128)(2,1)S(1)} %collective-permute-done.4.refs_2_) | copy-start | bytes 786436
  42.7 6.4 %collective-permute-start.5 = (bf16[4,256,128]{2,1,0:T(8,128)(2,1)S(1)}, bf16[4,256,128]{2,1,0:T(8,128)(2,1)S(1)}, u32[]{:S(2)}, u32[]{:S(2)}) collective-permute-start(bf16[4,256,128]{2,1,0:T(8,128)(2,1)S(1)} %collective-permute-done.4.refs_2_), channel_id=1, source_target_pairs={{0,32},{8,232},{16,48},{24,248},{32,64},{40,8},{48,80},{56,24},{64... | collective-permute-start | bytes 786440 | tf_op jit(solution)/shard_map/ppermute | solution.py:38
  45.8 19.4 %copy-start.7 = (bf16[4,256,128]{2,1,0:T(8,128)(2,1)}, bf16[4,256,128]{2,1,0:T(8,128)(2,1)S(1)}, u32[]{:S(2)}) copy-start(bf16[4,256,128]{2,1,0:T(8,128)(2,1)S(1)} %collective-permute-done.10.refs_8_) | copy-start | bytes 786436
  45.8 6.1 %collective-permute-start.11 = (bf16[4,256,128]{2,1,0:T(8,128)(2,1)S(1)}, bf16[4,256,128]{2,1,0:T(8,128)(2,1)S(1)}, u32[]{:S(2)}, u32[]{:S(2)}) collective-permute-start(bf16[4,256,128]{2,1,0:T(8,128)(2,1)S(1)} %collective-permute-done.10.refs_8_), channel_id=1, source_target_pairs={{0,32},{8,232},{16,48},{24,248},{32,64},{40,8},{48,80},{56,24},{64... | collective-permute-start | bytes 786440 | tf_op jit(solution)/shard_map/ppermute | solution.py:38
  49.1 7.9 %copy-start.8 = (bf16[4,256,128]{2,1,0:T(8,128)(2,1)}, bf16[4,256,128]{2,1,0:T(8,128)(2,1)S(1)}, u32[]{:S(2)}) copy-start(bf16[4,256,128]{2,1,0:T(8,128)(2,1)S(1)} %collective-permute-done.5.refs_3_) | copy-start | bytes 786436
  49.1 7.8 %collective-permute-start.6 = (bf16[4,256,128]{2,1,0:T(8,128)(2,1)S(1)}, bf16[4,256,128]{2,1,0:T(8,128)(2,1)S(1)}, u32[]{:S(2)}, u32[]{:S(2)}) collective-permute-start(bf16[4,256,128]{2,1,0:T(8,128)(2,1)S(1)} %collective-permute-done.5.refs_3_), channel_id=1, source_target_pairs={{0,32},{16,48},{32,64},{48,80},{64,96},{80,112},{96,128},{112,144}... | collective-permute-start | bytes 786440 | tf_op jit(solution)/shard_map/ppermute | solution.py:53
  51.9 13.3 %copy-start.9 = (bf16[4,256,128]{2,1,0:T(8,128)(2,1)}, bf16[4,256,128]{2,1,0:T(8,128)(2,1)S(1)}, u32[]{:S(2)}) copy-start(bf16[4,256,128]{2,1,0:T(8,128)(2,1)S(1)} %collective-permute-done.11.refs_9_) | copy-start | bytes 786436
  51.9 13.3 %collective-permute-start.12 = (bf16[4,256,128]{2,1,0:T(8,128)(2,1)S(1)}, bf16[4,256,128]{2,1,0:T(8,128)(2,1)S(1)}, u32[]{:S(2)}, u32[]{:S(2)}) collective-permute-start(bf16[4,256,128]{2,1,0:T(8,128)(2,1)S(1)} %collective-permute-done.11.refs_9_), channel_id=1, source_target_pairs={{8,232},{24,248},{40,8},{56,24},{72,40},{88,56},{104,72},{120,88},... | collective-permute-start | bytes 786440 | tf_op jit(solution)/shard_map/ppermute | solution.py:54
  57.9 9.6 %collective-permute-start.7 = (bf16[16,256,128]{2,1,0:T(8,128)(2,1)S(1)}, bf16[16,256,128]{2,1,0:T(8,128)(2,1)S(1)}, u32[]{:S(2)}, u32[]{:S(2)}) collective-permute-start(bf16[16,256,128]{2,1,0:T(8,128)(2,1)S(1)} %pad_maximum_fusion), channel_id=1, source_target_pairs={{0,8},{8,0},{16,24},{24,16},{32,40},{40,32},{48,56},{56,48},{64,72... | collective-permute-start | bytes 3145736 | tf_op jit(solution)/shard_map/ppermute | solution.py:38
  66.1 2.9 %collective-permute-start.13 = (bf16[16,256,128]{2,1,0:T(8,128)(2,1)S(1)}, bf16[16,256,128]{2,1,0:T(8,128)(2,1)S(1)}, u32[]{:S(2)}, u32[]{:S(2)}) collective-permute-start(bf16[16,256,128]{2,1,0:T(8,128)(2,1)S(1)} %pad_maximum_fusion.1), channel_id=1, source_target_pairs={{0,8},{8,0},{16,24},{24,16},{32,40},{40,32},{48,56},{56,48},{64,72... | collective-permute-start | bytes 3145736 | tf_op jit(solution)/shard_map/ppermute | solution.py:38
  67.5 1.5 %copy-start.2 = (bf16[16,256,128]{2,1,0:T(8,128)(2,1)}, bf16[16,256,128]{2,1,0:T(8,128)(2,1)S(1)}, u32[]{:S(2)}) copy-start(bf16[16,256,128]{2,1,0:T(8,128)(2,1)S(1)} %collective-permute-done.7.refs_5_) | copy-start | bytes 3145732
  (4 other events, 3.9 us)

commit v6 on v5

--- a/solution.py
+++ b/solution.py
@@ -54,9 +54,13 @@
             lax.ppermute(walked[-1][1], "req", [(i, (i - 4) % n) for i in range(1, n, 2)]),
         ]
     )
-    mine = [jnp.concatenate([w[kv] for w in walked[1:]], 0) for kv in range(2)]
+    mine = [jnp.concatenate([w[kv] for w in walked[1:reach]], 0) for kv in range(2)]
     swapped = both(mine, lambda i: i ^ 1)
-    return [[w[kv] for w in walked] + [swapped[kv]] for kv in range(2)]
+    extra = [
+        lax.ppermute(walked[reach][0], "req", [(i, i + 1) for i in range(0, n, 2)]),
+        lax.ppermute(walked[reach][1], "req", [(i, i - 1) for i in range(1, n, 2)]),
+    ]
+    return [[w[kv] for w in walked] + [swapped[kv], extra[kv]] for kv in range(2)]
 
 
 def attend_kernel(
@@ -124,22 +128,20 @@
                 for kv in range(2):
                     copy(kv, p, j, hh, b)
 
-        tail = (reach - 1) * group + j
-
         @pl.when((place == reach) & (core == 0))
         def _():
             copy(0, reach, j, hh, b)
-            copy(1, last, tail, hh, b)
+            copy(1, reach + 2, j, hh, b)
 
         @pl.when((place == reach) & (core == 1))
         def _():
-            copy(0, last, tail, hh, b)
+            copy(0, reach + 2, j, hh, b)
             copy(1, reach, j, hh, b)
 
         @pl.when(place > reach)
         def _():
             for kv in range(2):
-                copy(kv, last, where - (reach + 1) * group, hh, b)
+                copy(kv, reach + 1, where - (reach + 1) * group, hh, b)
 
     def wait_copy(hh, b):
         for kv in range(2):

time: 93.2 us -> 96.3 us (1.033); the launches traced: 93.5 us -> 95.3 us
  waiting for transfers between devices: 10.7 us -> 13 us
    ppermute x1, waiting for transfers between devices: 0.01 us -> 4.79 us  [ring_gather(): lax.ppermute(walked[-1][1], 'req', [(i, (i - 4) % n) for i in range(1, n,...]
    ppermute x10, waiting for transfers between devices: 9.59 us -> 4.82 us  [both(): return [lax.ppermute(x[kv], 'req', route(fn)) for kv in range(2)]]
    ppermute x1, starting transfers between devices: 5.01 us -> 1.91 us  [ring_gather(): lax.ppermute(walked[-1][1], 'req', [(i, (i - 4) % n) for i in range(1, n,...]
    ppermute x0 -> x2, starting transfers between devices: none -> 2.77 us  [the longest x1 1.47 us: ring_gather(): lax.ppermute(walked[reach][0], 'req', [(i, i + 1) for i in range(0, n, 2)])]
    ppermute x0 -> x2, waiting for transfers between devices: none -> 2.27 us  [the longest x1 2.26 us: ring_gather(): lax.ppermute(walked[reach][0], 'req', [(i, i + 1) for i in range(0, n, 2)])]
    unnamed x31 -> x35, local copies, waits for them, and re-layouts: 3.57 us -> 3.08 us
  transfers between devices with their start and end apart: 14 -> 16, of which waited for: 8 -> 7; matrix products, arithmetic and copies ran while one was open for 2% -> 2% of each run, Pallas kernels for 0% -> 0%
where the time goes in v6:
time: 96.3 us; the launch traced here: 95.3 us
  starting transfers between devices  40.8 us (42%)
  Pallas kernels  23 us (24%)
  blocking collectives  13.4 us (14%)
  waiting for transfers between devices  13 us (13%)
  local copies, waits for them, and re-layouts  4.42 us (5%)
    ppermute x10, starting transfers between devices, both(): return [lax.ppermute(x[kv], 'req', route(fn)) for kv in range(2)]  30.6 us
    pallas_call x1, Pallas kernels, per_device(): pl.pallas_call(kernel, out_shape=jax.ShapeDtypeStruct((tok_rows, per_kv *...  23 us
    all_to_all x1, blocking collectives, per_device(): lax.all_to_all(prefix_kv, 'tp', split_axis=3, concat_axis=2, tiled=True)  13.4 us
    ppermute x10, waiting for transfers between devices, both(): return [lax.ppermute(x[kv], 'req', route(fn)) for kv in range(2)]  4.82 us
    ppermute x1, waiting for transfers between devices, ring_gather(): lax.ppermute(walked[-1][1], 'req', [(i, (i - 4) % n) for i in range(1, n,...  4.79 us
    ppermute x1, starting transfers between devices, from_behind(): return lax.ppermute(block, axis, route)  4.5 us
    unnamed x35, local copies, waits for them, and re-layouts  3.08 us
    ppermute x1, waiting for transfers between devices, ring_gather(): lax.ppermute(walked[reach][0], 'req', [(i, i + 1) for i in range(0, n, 2)])  2.26 us
  transfers between devices with their start and end apart: 16, of which 7 were waited for; matrix products, arithmetic and copies ran while one was open for 2% of the time, Pallas kernels for 0%

profile of v6, /device:TPU:1, one launch (start us, length us, event | category | flops | bytes accessed | tf_op | source)
XLA Modules:
  0.0 95.3 jit_solution(6614250729367680381)
XLA Ops:
  0.0 0.9 slice.9
  1.0 4.5 %collective-permute-start = (bf16[2,256,128]{2,1,0:T(8,128)(2,1)S(1)}, bf16[2,256,128]{2,1,0:T(8,128)(2,1)S(1)}, u32[]{:S(2)}, u32[]{:S(2)}) collective-permute-start(bf16[2,256,128]{2,1,0:T(8,128)(2,1)S(1)} %slice.9), channel_id=1, source_target_pairs={{0,8},{8,16},{16,24},{24,32},{32,40},{40,48},{48,56},{56,64},{64,7... | collective-permute-start | bytes 393224 | tf_op jit(solution)/shard_map/ppermute | solution.py:24
  5.9 0.5 reshape
  6.4 13.4 %all_to_all.18 = bf16[8,2,4096]{2,1,0:T(2,128)(2,1)S(1)} all-to-all(bf16[8,2,4096]{2,1,0:T(2,128)(2,1)S(1)} %reshape), channel_id=1, replica_groups=mesh['req'=32,'tp'=8] {'tp'}, dimensions={0} | all-to-all | bytes 262144 | tf_op jit(solution)/shard_map/all_to_all | solution.py:234
  20.8 1.1 %collective-permute-done.1 = bf16[2,1,256,128]{3,2,1,0:T(8,128)(2,1)S(1)} collective-permute-done((bf16[2,1,256,128]{3,2,1,0:T(8,128)(2,1)S(1)}, bf16[2,1,256,128]{3,2,1,0:T(8,128)(2,1)S(1)}, u32[]{:S(2)}, u32[]{:S(2)}) %collective-permute-start.1) | collective-permute-done | bytes 131104 | tf_op jit(solution)/shard_map/ppermute | solution.py:40
  22.0 1.1 %collective-permute-start.9 = (bf16[2,256,128]{2,1,0:T(8,128)(2,1)S(1)}, bf16[2,256,128]{2,1,0:T(8,128)(2,1)S(1)}, u32[]{:S(2)}, u32[]{:S(2)}) collective-permute-start(bf16[2,256,128]{2,1,0:T(8,128)(2,1)S(1)} %get-tuple-element.9), channel_id=1, source_target_pairs={{0,16},{8,24},{16,0},{24,8},{32,48},{40,56},{48,32},{56,40},{64,80... | collective-permute-start | bytes 393224 | tf_op jit(solution)/shard_map/ppermute | solution.py:38
  23.5 3.3 %collective-permute-done.9 = bf16[2,256,128]{2,1,0:T(8,128)(2,1)S(1)} collective-permute-done((bf16[2,256,128]{2,1,0:T(8,128)(2,1)S(1)}, bf16[2,256,128]{2,1,0:T(8,128)(2,1)S(1)}, u32[]{:S(2)}, u32[]{:S(2)}) %collective-permute-start.9) | collective-permute-done | bytes 131104 | tf_op jit(solution)/shard_map/ppermute | solution.py:38
  26.9 6.1 %collective-permute-start.10 = (bf16[4,256,128]{2,1,0:T(8,128)(2,1)S(1)}, bf16[4,256,128]{2,1,0:T(8,128)(2,1)S(1)}, u32[]{:S(2)}, u32[]{:S(2)}) collective-permute-start(bf16[4,256,128]{2,1,0:T(8,128)(2,1)S(1)} %maximum_select_fusion.2.refs_7_), channel_id=1, source_target_pairs={{0,32},{8,232},{16,48},{24,248},{32,64},{40,8},{48,80},{56,24},{64... | collective-permute-start | bytes 786440 | tf_op jit(solution)/shard_map/ppermute | solution.py:38
  33.0 2.8 %collective-permute-start.3 = (bf16[4,256,128]{2,1,0:T(8,128)(2,1)S(1)}, bf16[4,256,128]{2,1,0:T(8,128)(2,1)S(1)}, u32[]{:S(2)}, u32[]{:S(2)}) collective-permute-start(bf16[4,256,128]{2,1,0:T(8,128)(2,1)S(1)} %maximum_select_fusion.1.refs_0_), channel_id=1, source_target_pairs={{0,32},{8,232},{16,48},{24,248},{32,64},{40,8},{48,80},{56,24},{64... | collective-permute-start | bytes 786440 | tf_op jit(solution)/shard_map/ppermute | solution.py:38
  36.2 3.1 %collective-permute-start.11 = (bf16[4,256,128]{2,1,0:T(8,128)(2,1)S(1)}, bf16[4,256,128]{2,1,0:T(8,128)(2,1)S(1)}, u32[]{:S(2)}, u32[]{:S(2)}) collective-permute-start(bf16[4,256,128]{2,1,0:T(8,128)(2,1)S(1)} %collective-permute-done.10.refs_8_), channel_id=1, source_target_pairs={{0,32},{8,232},{16,48},{24,248},{32,64},{40,8},{48,80},{56,24},{64... | collective-permute-start | bytes 786440 | tf_op jit(solution)/shard_map/ppermute | solution.py:38
  39.4 2.8 %collective-permute-start.4 = (bf16[4,256,128]{2,1,0:T(8,128)(2,1)S(1)}, bf16[4,256,128]{2,1,0:T(8,128)(2,1)S(1)}, u32[]{:S(2)}, u32[]{:S(2)}) collective-permute-start(bf16[4,256,128]{2,1,0:T(8,128)(2,1)S(1)} %collective-permute-done.3.refs_1_), channel_id=1, source_target_pairs={{0,32},{8,232},{16,48},{24,248},{32,64},{40,8},{48,80},{56,24},{64... | collective-permute-start | bytes 786440 | tf_op jit(solution)/shard_map/ppermute | solution.py:38
  42.7 3.1 %collective-permute-start.12 = (bf16[4,256,128]{2,1,0:T(8,128)(2,1)S(1)}, bf16[4,256,128]{2,1,0:T(8,128)(2,1)S(1)}, u32[]{:S(2)}, u32[]{:S(2)}) collective-permute-start(bf16[4,256,128]{2,1,0:T(8,128)(2,1)S(1)} %collective-permute-done.11.refs_9_), channel_id=1, source_target_pairs={{0,32},{8,232},{16,48},{24,248},{32,64},{40,8},{48,80},{56,24},{64... | collective-permute-start | bytes 786440 | tf_op jit(solution)/shard_map/ppermute | solution.py:38
  45.8 2.8 %collective-permute-start.5 = (bf16[4,256,128]{2,1,0:T(8,128)(2,1)S(1)}, bf16[4,256,128]{2,1,0:T(8,128)(2,1)S(1)}, u32[]{:S(2)}, u32[]{:S(2)}) collective-permute-start(bf16[4,256,128]{2,1,0:T(8,128)(2,1)S(1)} %collective-permute-done.4.refs_2_), channel_id=1, source_target_pairs={{0,32},{8,232},{16,48},{24,248},{32,64},{40,8},{48,80},{56,24},{64... | collective-permute-start | bytes 786440 | tf_op jit(solution)/shard_map/ppermute | solution.py:38
  49.2 5.7 %collective-permute-start.14 = (bf16[12,256,128]{2,1,0:T(8,128)(2,1)S(1)}, bf16[12,256,128]{2,1,0:T(8,128)(2,1)S(1)}, u32[]{:S(2)}, u32[]{:S(2)}) collective-permute-start(bf16[12,256,128]{2,1,0:T(8,128)(2,1)S(1)} %pad_maximum_fusion.1), channel_id=1, source_target_pairs={{0,8},{8,0},{16,24},{24,16},{32,40},{40,32},{48,56},{56,48},{64,72... | collective-permute-start | bytes 2359304 | tf_op jit(solution)/shard_map/ppermute | solution.py:38
  55.1 2.7 %collective-permute-start.7 = (bf16[12,256,128]{2,1,0:T(8,128)(2,1)S(1)}, bf16[12,256,128]{2,1,0:T(8,128)(2,1)S(1)}, u32[]{:S(2)}, u32[]{:S(2)}) collective-permute-start(bf16[12,256,128]{2,1,0:T(8,128)(2,1)S(1)} %pad_maximum_fusion), channel_id=1, source_target_pairs={{0,8},{8,0},{16,24},{24,16},{32,40},{40,32},{48,56},{56,48},{64,72... | collective-permute-start | bytes 2359304 | tf_op jit(solution)/shard_map/ppermute | solution.py:38
  57.8 1.9 %collective-permute-start.13 = (bf16[4,256,128]{2,1,0:T(8,128)(2,1)S(1)}, bf16[4,256,128]{2,1,0:T(8,128)(2,1)S(1)}, u32[]{:S(2)}, u32[]{:S(2)}) collective-permute-start(bf16[4,256,128]{2,1,0:T(8,128)(2,1)S(1)} %collective-permute-done.12.refs_10_), channel_id=1, source_target_pairs={{8,232},{24,248},{40,8},{56,24},{72,40},{88,56},{104,72},{120,88},... | collective-permute-start | bytes 786440 | tf_op jit(solution)/shard_map/ppermute | solution.py:54
  59.7 0.7 collective-permute-start.6
  60.4 4.8 %collective-permute-done.13.refs_11_ = bf16[4,256,128]{2,1,0:T(8,128)(2,1)S(1)} collective-permute-done((bf16[4,256,128]{2,1,0:T(8,128)(2,1)S(1)}, bf16[4,256,128]{2,1,0:T(8,128)(2,1)S(1)}, u32[]{:S(2)}, u32[]{:S(2)}) %collective-permute-start.13) | collective-permute-done | bytes 262176 | tf_op jit(solution)/shard_map/ppermute | solution.py:54
  65.2 1.3 %collective-permute-start.15 = (bf16[4,256,128]{2,1,0:T(8,128)(2,1)S(1)}, bf16[4,256,128]{2,1,0:T(8,128)(2,1)S(1)}, u32[]{:S(2)}, u32[]{:S(2)}) collective-permute-start(bf16[4,256,128]{2,1,0:T(8,128)(2,1)S(1)} %collective-permute-done.13.refs_11_), channel_id=1, source_target_pairs={{8,0},{24,16},{40,32},{56,48},{72,64},{88,80},{104,96},{120,112},{... | collective-permute-start | bytes 786440 | tf_op jit(solution)/shard_map/ppermute | solution.py:61
  66.5 1.5 %collective-permute-start.8 = (bf16[4,256,128]{2,1,0:T(8,128)(2,1)S(1)}, bf16[4,256,128]{2,1,0:T(8,128)(2,1)S(1)}, u32[]{:S(2)}, u32[]{:S(2)}) collective-permute-start(bf16[4,256,128]{2,1,0:T(8,128)(2,1)S(1)} %collective-permute-done.6.refs_4_), channel_id=1, source_target_pairs={{0,8},{16,24},{32,40},{48,56},{64,72},{80,88},{96,104},{112,120},{... | collective-permute-start | bytes 786440 | tf_op jit(solution)/shard_map/ppermute | solution.py:60
  68.0 2.3 %collective-permute-done.8.refs_6_ = bf16[4,256,128]{2,1,0:T(8,128)(2,1)S(1)} collective-permute-done((bf16[4,256,128]{2,1,0:T(8,128)(2,1)S(1)}, bf16[4,256,128]{2,1,0:T(8,128)(2,1)S(1)}, u32[]{:S(2)}, u32[]{:S(2)}) %collective-permute-start.8) | collective-permute-done | bytes 262176 | tf_op jit(solution)/shard_map/ppermute | solution.py:60
  70.3 0.7 copy-done.13
  71.3 0.9 copy-done.9
  72.2 23.0 %shard_map.73 = bf16[384,1024]{1,0:T(8,128)(2,1)} custom-call(s32[31]{0:T(128)} %len_ref.1, s32[31]{0:T(128)} %group_ref.1, s32[31]{0:T(128)} %order_ref.1, s32[32]{0:T(128)} %owner_ref.1, bf16[384,1024]{1,0:T(8,128)(2,1)} %q_ref.1, bf16[4,256,128]{2,1,0:T(8,128)(2,1)} %copy-done.1, bf16[4,256,128]{2,1,0:T(8,128)(2,1)} %copy-done.3, ...), custom_call_target="tpu_custom_call" | custom-call | tf_op jit(solution)/shard_map/pallas_call | solution.py:255
  (53 shorter events, 4.0 us)
Async XLA Ops:
  0.0 5.5 %copy-start.14 = (bf16[2,1,32,1024]{3,2,1,0:T(8,128)(2,1)S(1)}, bf16[2,1,32,1024]{3,2,1,0:T(8,128)(2,1)}, u32[]{:S(2)}) copy-start(bf16[2,1,32,1024]{3,2,1,0:T(8,128)(2,1)} %param.9) | copy-start | bytes 393220
  1.0 19.5 %collective-permute-start = (bf16[2,256,128]{2,1,0:T(8,128)(2,1)S(1)}, bf16[2,256,128]{2,1,0:T(8,128)(2,1)S(1)}, u32[]{:S(2)}, u32[]{:S(2)}) collective-permute-start(bf16[2,256,128]{2,1,0:T(8,128)(2,1)S(1)} %slice.9), channel_id=1, source_target_pairs={{0,8},{8,16},{16,24},{24,32},{32,40},{40,48},{48,56},{56,64},{64,7... | collective-permute-start | bytes 393224 | tf_op jit(solution)/shard_map/ppermute | solution.py:24
  20.5 1.4 %collective-permute-start.1 = (bf16[2,1,256,128]{3,2,1,0:T(8,128)(2,1)S(1)}, bf16[2,1,256,128]{3,2,1,0:T(8,128)(2,1)S(1)}, u32[]{:S(2)}, u32[]{:S(2)}) collective-permute-start(bf16[2,1,256,128]{3,2,1,0:T(8,128)(2,1)S(1)} %bitcast.13), channel_id=1, source_target_pairs={{0,8},{8,0},{16,24},{24,16},{32,40},{40,32},{48,56},{56,48},{64,72... | collective-permute-start | bytes 393224 | tf_op jit(solution)/shard_map/ppermute | solution.py:40
  22.0 4.9 %collective-permute-start.9 = (bf16[2,256,128]{2,1,0:T(8,128)(2,1)S(1)}, bf16[2,256,128]{2,1,0:T(8,128)(2,1)S(1)}, u32[]{:S(2)}, u32[]{:S(2)}) collective-permute-start(bf16[2,256,128]{2,1,0:T(8,128)(2,1)S(1)} %get-tuple-element.9), channel_id=1, source_target_pairs={{0,16},{8,24},{16,0},{24,8},{32,48},{40,56},{48,32},{56,40},{64,80... | collective-permute-start | bytes 393224 | tf_op jit(solution)/shard_map/ppermute | solution.py:38
  23.0 9.9 %collective-permute-start.2 = (bf16[2,256,128]{2,1,0:T(8,128)(2,1)S(1)}, bf16[2,256,128]{2,1,0:T(8,128)(2,1)S(1)}, u32[]{:S(2)}, u32[]{:S(2)}) collective-permute-start(bf16[2,256,128]{2,1,0:T(8,128)(2,1)S(1)} %get-tuple-element.10), channel_id=1, source_target_pairs={{0,16},{8,24},{16,0},{24,8},{32,48},{40,56},{48,32},{56,40},{64,80... | collective-permute-start | bytes 393224 | tf_op jit(solution)/shard_map/ppermute | solution.py:38
  26.9 6.1 %copy-start = (bf16[4,256,128]{2,1,0:T(8,128)(2,1)}, bf16[4,256,128]{2,1,0:T(8,128)(2,1)S(1)}, u32[]{:S(2)}) copy-start(bf16[4,256,128]{2,1,0:T(8,128)(2,1)S(1)} %maximum_select_fusion.2.refs_7_) | copy-start | bytes 786436
  26.9 9.4 %collective-permute-start.10 = (bf16[4,256,128]{2,1,0:T(8,128)(2,1)S(1)}, bf16[4,256,128]{2,1,0:T(8,128)(2,1)S(1)}, u32[]{:S(2)}, u32[]{:S(2)}) collective-permute-start(bf16[4,256,128]{2,1,0:T(8,128)(2,1)S(1)} %maximum_select_fusion.2.refs_7_), channel_id=1, source_target_pairs={{0,32},{8,232},{16,48},{24,248},{32,64},{40,8},{48,80},{56,24},{64... | collective-permute-start | bytes 786440 | tf_op jit(solution)/shard_map/ppermute | solution.py:38
  33.0 16.2 %copy-start.1 = (bf16[4,256,128]{2,1,0:T(8,128)(2,1)}, bf16[4,256,128]{2,1,0:T(8,128)(2,1)S(1)}, u32[]{:S(2)}) copy-start(bf16[4,256,128]{2,1,0:T(8,128)(2,1)S(1)} %maximum_select_fusion.1.refs_0_) | copy-start | bytes 786436
  33.0 6.4 %collective-permute-start.3 = (bf16[4,256,128]{2,1,0:T(8,128)(2,1)S(1)}, bf16[4,256,128]{2,1,0:T(8,128)(2,1)S(1)}, u32[]{:S(2)}, u32[]{:S(2)}) collective-permute-start(bf16[4,256,128]{2,1,0:T(8,128)(2,1)S(1)} %maximum_select_fusion.1.refs_0_), channel_id=1, source_target_pairs={{0,32},{8,232},{16,48},{24,248},{32,64},{40,8},{48,80},{56,24},{64... | collective-permute-start | bytes 786440 | tf_op jit(solution)/shard_map/ppermute | solution.py:38
  36.2 13.0 %copy-start.2 = (bf16[4,256,128]{2,1,0:T(8,128)(2,1)}, bf16[4,256,128]{2,1,0:T(8,128)(2,1)S(1)}, u32[]{:S(2)}) copy-start(bf16[4,256,128]{2,1,0:T(8,128)(2,1)S(1)} %collective-permute-done.10.refs_8_) | copy-start | bytes 786436
  36.2 6.4 %collective-permute-start.11 = (bf16[4,256,128]{2,1,0:T(8,128)(2,1)S(1)}, bf16[4,256,128]{2,1,0:T(8,128)(2,1)S(1)}, u32[]{:S(2)}, u32[]{:S(2)}) collective-permute-start(bf16[4,256,128]{2,1,0:T(8,128)(2,1)S(1)} %collective-permute-done.10.refs_8_), channel_id=1, source_target_pairs={{0,32},{8,232},{16,48},{24,248},{32,64},{40,8},{48,80},{56,24},{64... | collective-permute-start | bytes 786440 | tf_op jit(solution)/shard_map/ppermute | solution.py:38
  39.4 15.6 %copy-start.3 = (bf16[4,256,128]{2,1,0:T(8,128)(2,1)}, bf16[4,256,128]{2,1,0:T(8,128)(2,1)S(1)}, u32[]{:S(2)}) copy-start(bf16[4,256,128]{2,1,0:T(8,128)(2,1)S(1)} %collective-permute-done.3.refs_1_) | copy-start | bytes 786436
  39.4 6.4 %collective-permute-start.4 = (bf16[4,256,128]{2,1,0:T(8,128)(2,1)S(1)}, bf16[4,256,128]{2,1,0:T(8,128)(2,1)S(1)}, u32[]{:S(2)}, u32[]{:S(2)}) collective-permute-start(bf16[4,256,128]{2,1,0:T(8,128)(2,1)S(1)} %collective-permute-done.3.refs_1_), channel_id=1, source_target_pairs={{0,32},{8,232},{16,48},{24,248},{32,64},{40,8},{48,80},{56,24},{64... | collective-permute-start | bytes 786440 | tf_op jit(solution)/shard_map/ppermute | solution.py:38
  42.7 6.6 %copy-start.4 = (bf16[4,256,128]{2,1,0:T(8,128)(2,1)}, bf16[4,256,128]{2,1,0:T(8,128)(2,1)S(1)}, u32[]{:S(2)}) copy-start(bf16[4,256,128]{2,1,0:T(8,128)(2,1)S(1)} %collective-permute-done.11.refs_9_) | copy-start | bytes 786436
  42.7 6.4 %collective-permute-start.12 = (bf16[4,256,128]{2,1,0:T(8,128)(2,1)S(1)}, bf16[4,256,128]{2,1,0:T(8,128)(2,1)S(1)}, u32[]{:S(2)}, u32[]{:S(2)}) collective-permute-start(bf16[4,256,128]{2,1,0:T(8,128)(2,1)S(1)} %collective-permute-done.11.refs_9_), channel_id=1, source_target_pairs={{0,32},{8,232},{16,48},{24,248},{32,64},{40,8},{48,80},{56,24},{64... | collective-permute-start | bytes 786440 | tf_op jit(solution)/shard_map/ppermute | solution.py:38
  45.8 9.2 %copy-start.5 = (bf16[4,256,128]{2,1,0:T(8,128)(2,1)}, bf16[4,256,128]{2,1,0:T(8,128)(2,1)S(1)}, u32[]{:S(2)}) copy-start(bf16[4,256,128]{2,1,0:T(8,128)(2,1)S(1)} %collective-permute-done.4.refs_2_) | copy-start | bytes 786436
  45.8 9.2 %collective-permute-start.5 = (bf16[4,256,128]{2,1,0:T(8,128)(2,1)S(1)}, bf16[4,256,128]{2,1,0:T(8,128)(2,1)S(1)}, u32[]{:S(2)}, u32[]{:S(2)}) collective-permute-start(bf16[4,256,128]{2,1,0:T(8,128)(2,1)S(1)} %collective-permute-done.4.refs_2_), channel_id=1, source_target_pairs={{0,32},{8,232},{16,48},{24,248},{32,64},{40,8},{48,80},{56,24},{64... | collective-permute-start | bytes 786440 | tf_op jit(solution)/shard_map/ppermute | solution.py:38
  49.1 8.6 %copy-start.6 = (bf16[4,256,128]{2,1,0:T(8,128)(2,1)}, bf16[4,256,128]{2,1,0:T(8,128)(2,1)S(1)}, u32[]{:S(2)}) copy-start(bf16[4,256,128]{2,1,0:T(8,128)(2,1)S(1)} %collective-permute-done.12.refs_10_) | copy-start | bytes 786436
  49.2 21.0 %collective-permute-start.14 = (bf16[12,256,128]{2,1,0:T(8,128)(2,1)S(1)}, bf16[12,256,128]{2,1,0:T(8,128)(2,1)S(1)}, u32[]{:S(2)}, u32[]{:S(2)}) collective-permute-start(bf16[12,256,128]{2,1,0:T(8,128)(2,1)S(1)} %pad_maximum_fusion.1), channel_id=1, source_target_pairs={{0,8},{8,0},{16,24},{24,16},{32,40},{40,32},{48,56},{56,48},{64,72... | collective-permute-start | bytes 2359304 | tf_op jit(solution)/shard_map/ppermute | solution.py:38
  55.1 15.2 %collective-permute-start.7 = (bf16[12,256,128]{2,1,0:T(8,128)(2,1)S(1)}, bf16[12,256,128]{2,1,0:T(8,128)(2,1)S(1)}, u32[]{:S(2)}, u32[]{:S(2)}) collective-permute-start(bf16[12,256,128]{2,1,0:T(8,128)(2,1)S(1)} %pad_maximum_fusion), channel_id=1, source_target_pairs={{0,8},{8,0},{16,24},{24,16},{32,40},{40,32},{48,56},{56,48},{64,72... | collective-permute-start | bytes 2359304 | tf_op jit(solution)/shard_map/ppermute | solution.py:38
  57.8 7.4 %collective-permute-start.13 = (bf16[4,256,128]{2,1,0:T(8,128)(2,1)S(1)}, bf16[4,256,128]{2,1,0:T(8,128)(2,1)S(1)}, u32[]{:S(2)}, u32[]{:S(2)}) collective-permute-start(bf16[4,256,128]{2,1,0:T(8,128)(2,1)S(1)} %collective-permute-done.12.refs_10_), channel_id=1, source_target_pairs={{8,232},{24,248},{40,8},{56,24},{72,40},{88,56},{104,72},{120,88},... | collective-permute-start | bytes 786440 | tf_op jit(solution)/shard_map/ppermute | solution.py:54
  59.7 6.8 %collective-permute-start.6 = (bf16[4,256,128]{2,1,0:T(8,128)(2,1)S(1)}, bf16[4,256,128]{2,1,0:T(8,128)(2,1)S(1)}, u32[]{:S(2)}, u32[]{:S(2)}) collective-permute-start(bf16[4,256,128]{2,1,0:T(8,128)(2,1)S(1)} %collective-permute-done.5.refs_3_), channel_id=1, source_target_pairs={{0,32},{16,48},{32,64},{48,80},{64,96},{80,112},{96,128},{112,144}... | collective-permute-start | bytes 786440 | tf_op jit(solution)/shard_map/ppermute | solution.py:53
  65.2 2.8 %collective-permute-start.15 = (bf16[4,256,128]{2,1,0:T(8,128)(2,1)S(1)}, bf16[4,256,128]{2,1,0:T(8,128)(2,1)S(1)}, u32[]{:S(2)}, u32[]{:S(2)}) collective-permute-start(bf16[4,256,128]{2,1,0:T(8,128)(2,1)S(1)} %collective-permute-done.13.refs_11_), channel_id=1, source_target_pairs={{8,0},{24,16},{40,32},{56,48},{72,64},{88,80},{104,96},{120,112},{... | collective-permute-start | bytes 786440 | tf_op jit(solution)/shard_map/ppermute | solution.py:61
  66.5 3.8 %collective-permute-start.8 = (bf16[4,256,128]{2,1,0:T(8,128)(2,1)S(1)}, bf16[4,256,128]{2,1,0:T(8,128)(2,1)S(1)}, u32[]{:S(2)}, u32[]{:S(2)}) collective-permute-start(bf16[4,256,128]{2,1,0:T(8,128)(2,1)S(1)} %collective-permute-done.6.refs_4_), channel_id=1, source_target_pairs={{0,8},{16,24},{32,40},{48,56},{64,72},{80,88},{96,104},{112,120},{... | collective-permute-start | bytes 786440 | tf_op jit(solution)/shard_map/ppermute | solution.py:60
  (8 other events, 20.0 us)

commit v7 on v3

--- a/solution.py
+++ b/solution.py
@@ -48,9 +48,10 @@
     walked = [four]
     for _ in range(reach):
         walked.append(both(walked[-1], lambda i: i + 4 if i % 2 == 0 else i - 4))
-    mine = [jnp.concatenate([w[kv] for w in walked[1:reach]], 0) for kv in range(2)]
-    swapped = both(mine, lambda i: i ^ 1)
-    return [[w[kv] for w in walked] + [swapped[kv]] for kv in range(2)]
+    early = [jnp.concatenate([w[kv] for w in walked[1 : reach - 1]], 0) for kv in range(2)]
+    swapped = both(early, lambda i: i ^ 1)
+    late = both(walked[reach - 1], lambda i: i ^ 1)
+    return [[w[kv] for w in walked] + [swapped[kv], late[kv]] for kv in range(2)]
 
 
 def attend_kernel(
@@ -106,8 +107,15 @@
         where = position(hh, b)
         place = where // group
         for p in range(n_pieces):
-            hit = (place == p) if p < last else (place >= last)
-            at = where % group if p < last else where - last * group
+            if p <= reach:
+                hit = place == p
+                at = where % group
+            elif p == reach + 1:
+                hit = (place > reach) & (place < 2 * reach - 1)
+                at = where - (reach + 1) * group
+            else:
+                hit = place == 2 * reach - 1
+                at = where % group
 
             @pl.when(hit)
             def _():

time: 91.9 us -> 94.9 us (1.033)
  the two profiles are of different devices: /device:TPU:1 before, /device:TPU:128 now
where the time goes in v7:
time: 94.9 us; the launch traced here: 95.9 us
  waiting for transfers between devices  42.7 us (45%)
  Pallas kernels  26 us (27%)
  blocking collectives  14.8 us (16%)
  starting transfers between devices  7.02 us (7%)
  local copies, waits for them, and re-layouts  4.71 us (5%)
    ppermute x14, waiting for transfers between devices, both(): return [lax.ppermute(x[kv], 'req', route(fn)) for kv in range(2)]  34.9 us
    pallas_call x1, Pallas kernels, per_device(): pl.pallas_call(kernel, out_shape=jax.ShapeDtypeStruct((tok_rows, per_kv *...  26 us
    all_to_all x1, blocking collectives, per_device(): lax.all_to_all(prefix_kv, 'tp', split_axis=3, concat_axis=2, tiled=True)  14.8 us
    ppermute x1, waiting for transfers between devices, from_behind(): return lax.ppermute(block, axis, route)  6.45 us
    ppermute x14, starting transfers between devices, both(): return [lax.ppermute(x[kv], 'req', route(fn)) for kv in range(2)]  4.99 us
    unnamed x35, local copies, waits for them, and re-layouts  4.31 us
    ppermute x1, starting transfers between devices, from_behind(): return lax.ppermute(block, axis, route)  1.93 us
  transfers between devices with their start and end apart: 16, of which 11 were waited for; matrix products, arithmetic and copies ran while one was open for 0% of the time, Pallas kernels for 0%

profile of v7, /device:TPU:128, one launch (start us, length us, event | category | flops | bytes accessed | tf_op | source)
XLA Modules:
  0.0 95.9 jit_solution(4828232739660436053)
XLA Ops:
  0.0 1.2 %copy.14 = bf16[2,1,32,1024]{2,0,1,3:T(2,128)(2,1)S(1)} copy(bf16[2,1,32,1024]{3,2,1,0:T(8,128)(2,1)} %param.9) | data formatting | bytes 262144 | tf_op args[2]
  1.2 0.5 reshape
  1.7 14.8 %all_to_all.18 = bf16[8,2,4096]{2,1,0:T(2,128)(2,1)S(1)} all-to-all(bf16[8,2,4096]{2,1,0:T(2,128)(2,1)S(1)} %reshape), channel_id=1, replica_groups=mesh['req'=32,'tp'=8] {'tp'}, dimensions={0} | all-to-all | bytes 262144 | tf_op jit(solution)/shard_map/all_to_all | solution.py:214
  17.3 1.3 %collective-permute-done = bf16[2,1,256,128]{3,2,1,0:T(8,128)(2,1)S(1)} collective-permute-done((bf16[2,1,256,128]{3,2,1,0:T(8,128)(2,1)S(1)}, bf16[2,1,256,128]{3,2,1,0:T(8,128)(2,1)S(1)}, u32[]{:S(2)}, u32[]{:S(2)}) %collective-permute-start) | collective-permute-done | bytes 131104 | tf_op jit(solution)/shard_map/ppermute | solution.py:40
  18.7 0.7 collective-permute-start.1
  19.3 5.0 %collective-permute-done.1 = bf16[2,256,128]{2,1,0:T(8,128)(2,1)S(1)} collective-permute-done((bf16[2,256,128]{2,1,0:T(8,128)(2,1)S(1)}, bf16[2,256,128]{2,1,0:T(8,128)(2,1)S(1)}, u32[]{:S(2)}, u32[]{:S(2)}) %collective-permute-start.1) | collective-permute-done | bytes 131104 | tf_op jit(solution)/shard_map/ppermute | solution.py:38
  24.3 1.1 %collective-permute-start.2 = (bf16[4,256,128]{2,1,0:T(8,128)(2,1)S(1)}, bf16[4,256,128]{2,1,0:T(8,128)(2,1)S(1)}, u32[]{:S(2)}, u32[]{:S(2)}) collective-permute-start(bf16[4,256,128]{2,1,0:T(8,128)(2,1)S(1)} %maximum_select_fusion.1.refs_0_), channel_id=1, source_target_pairs={{0,32},{8,232},{16,48},{24,248},{32,64},{40,8},{48,80},{56,24},{64... | collective-permute-start | bytes 786440 | tf_op jit(solution)/shard_map/ppermute | solution.py:38
  25.4 0.6 collective-permute-start.8
  26.0 4.4 %collective-permute-done.8 = bf16[2,256,128]{2,1,0:T(8,128)(2,1)S(1)} collective-permute-done((bf16[2,256,128]{2,1,0:T(8,128)(2,1)S(1)}, bf16[2,256,128]{2,1,0:T(8,128)(2,1)S(1)}, u32[]{:S(2)}, u32[]{:S(2)}) %collective-permute-start.8) | collective-permute-done | bytes 131104 | tf_op jit(solution)/shard_map/ppermute | solution.py:38
  30.5 1.1 %collective-permute-start.9 = (bf16[4,256,128]{2,1,0:T(8,128)(2,1)S(1)}, bf16[4,256,128]{2,1,0:T(8,128)(2,1)S(1)}, u32[]{:S(2)}, u32[]{:S(2)}) collective-permute-start(bf16[4,256,128]{2,1,0:T(8,128)(2,1)S(1)} %maximum_select_fusion.2.refs_7_), channel_id=1, source_target_pairs={{0,32},{8,232},{16,48},{24,248},{32,64},{40,8},{48,80},{56,24},{64... | collective-permute-start | bytes 786440 | tf_op jit(solution)/shard_map/ppermute | solution.py:38
  32.0 0.6 collective-permute-start.3
  32.6 5.5 %collective-permute-done.9.refs_8_ = bf16[4,256,128]{2,1,0:T(8,128)(2,1)S(1)} collective-permute-done((bf16[4,256,128]{2,1,0:T(8,128)(2,1)S(1)}, bf16[4,256,128]{2,1,0:T(8,128)(2,1)S(1)}, u32[]{:S(2)}, u32[]{:S(2)}) %collective-permute-start.9) | collective-permute-done | bytes 262176 | tf_op jit(solution)/shard_map/ppermute | solution.py:38
  38.1 2.8 %collective-permute-done.3.refs_2_ = bf16[4,256,128]{2,1,0:T(8,128)(2,1)S(1)} collective-permute-done((bf16[4,256,128]{2,1,0:T(8,128)(2,1)S(1)}, bf16[4,256,128]{2,1,0:T(8,128)(2,1)S(1)}, u32[]{:S(2)}, u32[]{:S(2)}) %collective-permute-start.3) | collective-permute-done | bytes 262176 | tf_op jit(solution)/shard_map/ppermute | solution.py:38
  41.0 0.7 copy-done.4
  41.7 4.0 %collective-permute-done.10.refs_9_ = bf16[4,256,128]{2,1,0:T(8,128)(2,1)S(1)} collective-permute-done((bf16[4,256,128]{2,1,0:T(8,128)(2,1)S(1)}, bf16[4,256,128]{2,1,0:T(8,128)(2,1)S(1)}, u32[]{:S(2)}, u32[]{:S(2)}) %collective-permute-start.10) | collective-permute-done | bytes 262176 | tf_op jit(solution)/shard_map/ppermute | solution.py:38
  45.7 2.8 %collective-permute-done.4.refs_3_ = bf16[4,256,128]{2,1,0:T(8,128)(2,1)S(1)} collective-permute-done((bf16[4,256,128]{2,1,0:T(8,128)(2,1)S(1)}, bf16[4,256,128]{2,1,0:T(8,128)(2,1)S(1)}, u32[]{:S(2)}, u32[]{:S(2)}) %collective-permute-start.4) | collective-permute-done | bytes 262176 | tf_op jit(solution)/shard_map/ppermute | solution.py:38
  48.6 0.6 collective-permute-start.13
  49.2 1.9 %collective-permute-start.15 = (bf16[2,256,128]{2,1,0:T(8,128)(2,1)S(1)}, bf16[2,256,128]{2,1,0:T(8,128)(2,1)S(1)}, u32[]{:S(2)}, u32[]{:S(2)}) collective-permute-start(bf16[2,256,128]{2,1,0:T(8,128)(2,1)S(1)} %slice.11), channel_id=1, source_target_pairs={{0,8},{8,16},{16,24},{24,32},{32,40},{40,48},{48,56},{56,64},{64,7... | collective-permute-start | bytes 393224 | tf_op jit(solution)/shard_map/ppermute | solution.py:24
  51.1 6.5 %collective-permute-done.15.refs_14_ = bf16[2,256,128]{2,1,0:T(8,128)(2,1)S(1)} collective-permute-done((bf16[2,256,128]{2,1,0:T(8,128)(2,1)S(1)}, bf16[2,256,128]{2,1,0:T(8,128)(2,1)S(1)}, u32[]{:S(2)}, u32[]{:S(2)}) %collective-permute-start.15) | collective-permute-done | bytes 131104 | tf_op jit(solution)/shard_map/ppermute | solution.py:24
  58.0 7.2 %collective-permute-done.5.refs_4_ = bf16[4,256,128]{2,1,0:T(8,128)(2,1)S(1)} collective-permute-done((bf16[4,256,128]{2,1,0:T(8,128)(2,1)S(1)}, bf16[4,256,128]{2,1,0:T(8,128)(2,1)S(1)}, u32[]{:S(2)}, u32[]{:S(2)}) %collective-permute-start.5) | collective-permute-done | bytes 262176 | tf_op jit(solution)/shard_map/ppermute | solution.py:38
  65.2 2.8 %collective-permute-done.12.refs_11_ = bf16[4,256,128]{2,1,0:T(8,128)(2,1)S(1)} collective-permute-done((bf16[4,256,128]{2,1,0:T(8,128)(2,1)S(1)}, bf16[4,256,128]{2,1,0:T(8,128)(2,1)S(1)}, u32[]{:S(2)}, u32[]{:S(2)}) %collective-permute-start.12) | collective-permute-done | bytes 262176 | tf_op jit(solution)/shard_map/ppermute | solution.py:38
  68.0 0.6 copy-done.14
  68.9 0.8 copy-done.8
  69.7 26.0 %shard_map.73 = bf16[384,1024]{1,0:T(8,128)(2,1)} custom-call(s32[31]{0:T(128)} %len_ref.1, s32[31]{0:T(128)} %group_ref.1, s32[31]{0:T(128)} %order_ref.1, s32[32]{0:T(128)} %owner_ref.1, bf16[384,1024]{1,0:T(8,128)(2,1)} %q_ref.1, bf16[4,256,128]{2,1,0:T(8,128)(2,1)} %copy-done, bf16[4,256,128]{2,1,0:T(8,128)(2,1)} %copy-done.2, ...), custom_call_target="tpu_custom_call" | custom-call | tf_op jit(solution)/shard_map/pallas_call | solution.py:235
  (53 shorter events, 2.0 us)
Async XLA Ops:
  17.2 1.4 %collective-permute-start = (bf16[2,1,256,128]{3,2,1,0:T(8,128)(2,1)S(1)}, bf16[2,1,256,128]{3,2,1,0:T(8,128)(2,1)S(1)}, u32[]{:S(2)}, u32[]{:S(2)}) collective-permute-start(bf16[2,1,256,128]{3,2,1,0:T(8,128)(2,1)S(1)} %bitcast.13), channel_id=1, source_target_pairs={{0,8},{8,0},{16,24},{24,16},{32,40},{40,32},{48,56},{56,48},{64,72... | collective-permute-start | bytes 393224 | tf_op jit(solution)/shard_map/ppermute | solution.py:40
  18.7 5.6 %collective-permute-start.1 = (bf16[2,256,128]{2,1,0:T(8,128)(2,1)S(1)}, bf16[2,256,128]{2,1,0:T(8,128)(2,1)S(1)}, u32[]{:S(2)}, u32[]{:S(2)}) collective-permute-start(bf16[2,256,128]{2,1,0:T(8,128)(2,1)S(1)} %get-tuple-element.6), channel_id=1, source_target_pairs={{0,16},{8,24},{16,0},{24,8},{32,48},{40,56},{48,32},{56,40},{64,80... | collective-permute-start | bytes 393224 | tf_op jit(solution)/shard_map/ppermute | solution.py:38
  24.3 7.7 %collective-permute-start.2 = (bf16[4,256,128]{2,1,0:T(8,128)(2,1)S(1)}, bf16[4,256,128]{2,1,0:T(8,128)(2,1)S(1)}, u32[]{:S(2)}, u32[]{:S(2)}) collective-permute-start(bf16[4,256,128]{2,1,0:T(8,128)(2,1)S(1)} %maximum_select_fusion.1.refs_0_), channel_id=1, source_target_pairs={{0,32},{8,232},{16,48},{24,248},{32,64},{40,8},{48,80},{56,24},{64... | collective-permute-start | bytes 786440 | tf_op jit(solution)/shard_map/ppermute | solution.py:38
  25.4 5.0 %collective-permute-start.8 = (bf16[2,256,128]{2,1,0:T(8,128)(2,1)S(1)}, bf16[2,256,128]{2,1,0:T(8,128)(2,1)S(1)}, u32[]{:S(2)}, u32[]{:S(2)}) collective-permute-start(bf16[2,256,128]{2,1,0:T(8,128)(2,1)S(1)} %get-tuple-element.5), channel_id=1, source_target_pairs={{0,16},{8,24},{16,0},{24,8},{32,48},{40,56},{48,32},{56,40},{64,80... | collective-permute-start | bytes 393224 | tf_op jit(solution)/shard_map/ppermute | solution.py:38
  30.4 10.5 %copy-start.1 = (bf16[4,256,128]{2,1,0:T(8,128)(2,1)}, bf16[4,256,128]{2,1,0:T(8,128)(2,1)S(1)}, u32[]{:S(2)}) copy-start(bf16[4,256,128]{2,1,0:T(8,128)(2,1)S(1)} %maximum_select_fusion.2.refs_7_) | copy-start | bytes 786436
  30.5 7.7 %collective-permute-start.9 = (bf16[4,256,128]{2,1,0:T(8,128)(2,1)S(1)}, bf16[4,256,128]{2,1,0:T(8,128)(2,1)S(1)}, u32[]{:S(2)}, u32[]{:S(2)}) collective-permute-start(bf16[4,256,128]{2,1,0:T(8,128)(2,1)S(1)} %maximum_select_fusion.2.refs_7_), channel_id=1, source_target_pairs={{0,32},{8,232},{16,48},{24,248},{32,64},{40,8},{48,80},{56,24},{64... | collective-permute-start | bytes 786440 | tf_op jit(solution)/shard_map/ppermute | solution.py:38
  32.0 9.0 %copy-start.2 = (bf16[4,256,128]{2,1,0:T(8,128)(2,1)}, bf16[4,256,128]{2,1,0:T(8,128)(2,1)S(1)}, u32[]{:S(2)}) copy-start(bf16[4,256,128]{2,1,0:T(8,128)(2,1)S(1)} %collective-permute-done.2.refs_1_) | copy-start | bytes 786436
  32.0 8.9 %collective-permute-start.3 = (bf16[4,256,128]{2,1,0:T(8,128)(2,1)S(1)}, bf16[4,256,128]{2,1,0:T(8,128)(2,1)S(1)}, u32[]{:S(2)}, u32[]{:S(2)}) collective-permute-start(bf16[4,256,128]{2,1,0:T(8,128)(2,1)S(1)} %collective-permute-done.2.refs_1_), channel_id=1, source_target_pairs={{0,32},{8,232},{16,48},{24,248},{32,64},{40,8},{48,80},{56,24},{64... | collective-permute-start | bytes 786440 | tf_op jit(solution)/shard_map/ppermute | solution.py:38
  38.1 10.4 %copy-start.3 = (bf16[4,256,128]{2,1,0:T(8,128)(2,1)}, bf16[4,256,128]{2,1,0:T(8,128)(2,1)S(1)}, u32[]{:S(2)}) copy-start(bf16[4,256,128]{2,1,0:T(8,128)(2,1)S(1)} %collective-permute-done.9.refs_8_) | copy-start | bytes 786436
  38.1 7.6 %collective-permute-start.10 = (bf16[4,256,128]{2,1,0:T(8,128)(2,1)S(1)}, bf16[4,256,128]{2,1,0:T(8,128)(2,1)S(1)}, u32[]{:S(2)}, u32[]{:S(2)}) collective-permute-start(bf16[4,256,128]{2,1,0:T(8,128)(2,1)S(1)} %collective-permute-done.9.refs_8_), channel_id=1, source_target_pairs={{0,32},{8,232},{16,48},{24,248},{32,64},{40,8},{48,80},{56,24},{64... | collective-permute-start | bytes 786440 | tf_op jit(solution)/shard_map/ppermute | solution.py:38
  40.9 7.6 %collective-permute-start.4 = (bf16[4,256,128]{2,1,0:T(8,128)(2,1)S(1)}, bf16[4,256,128]{2,1,0:T(8,128)(2,1)S(1)}, u32[]{:S(2)}, u32[]{:S(2)}) collective-permute-start(bf16[4,256,128]{2,1,0:T(8,128)(2,1)S(1)} %collective-permute-done.3.refs_2_), channel_id=1, source_target_pairs={{0,32},{8,232},{16,48},{24,248},{32,64},{40,8},{48,80},{56,24},{64... | collective-permute-start | bytes 786440 | tf_op jit(solution)/shard_map/ppermute | solution.py:38
  41.7 7.5 %copy-start.6 = (bf16[2,384,128]{2,1,0:T(8,128)(2,1)S(1)}, bf16[2,384,128]{2,1,0:T(8,128)(2,1)}, u32[]{:S(2)}) copy-start(bf16[2,384,128]{2,1,0:T(8,128)(2,1)} %refs_15_.1) | copy-start | bytes 589828
  41.7 26.3 %collective-permute-start.6 = (bf16[8,256,128]{2,1,0:T(8,128)(2,1)S(1)}, bf16[8,256,128]{2,1,0:T(8,128)(2,1)S(1)}, u32[]{:S(2)}, u32[]{:S(2)}) collective-permute-start(bf16[8,256,128]{2,1,0:T(8,128)(2,1)S(1)} %pad_maximum_fusion), channel_id=1, source_target_pairs={{0,8},{8,0},{16,24},{24,16},{32,40},{40,32},{48,56},{56,48},{64,72... | collective-permute-start | bytes 1572872 | tf_op jit(solution)/shard_map/ppermute | solution.py:38
  45.7 11.9 %collective-permute-start.11 = (bf16[4,256,128]{2,1,0:T(8,128)(2,1)S(1)}, bf16[4,256,128]{2,1,0:T(8,128)(2,1)S(1)}, u32[]{:S(2)}, u32[]{:S(2)}) collective-permute-start(bf16[4,256,128]{2,1,0:T(8,128)(2,1)S(1)} %collective-permute-done.10.refs_9_), channel_id=1, source_target_pairs={{0,32},{8,232},{16,48},{24,248},{32,64},{40,8},{48,80},{56,24},{64... | collective-permute-start | bytes 786440 | tf_op jit(solution)/shard_map/ppermute | solution.py:38
  48.5 9.1 %copy-start.9 = (bf16[4,256,128]{2,1,0:T(8,128)(2,1)}, bf16[4,256,128]{2,1,0:T(8,128)(2,1)S(1)}, u32[]{:S(2)}) copy-start(bf16[4,256,128]{2,1,0:T(8,128)(2,1)S(1)} %collective-permute-done.4.refs_3_) | copy-start | bytes 786436
  48.5 9.2 %collective-permute-start.7 = (bf16[4,256,128]{2,1,0:T(8,128)(2,1)S(1)}, bf16[4,256,128]{2,1,0:T(8,128)(2,1)S(1)}, u32[]{:S(2)}, u32[]{:S(2)}) collective-permute-start(bf16[4,256,128]{2,1,0:T(8,128)(2,1)S(1)} %collective-permute-done.4.refs_3_), channel_id=1, source_target_pairs={{0,8},{8,0},{16,24},{24,16},{32,40},{40,32},{48,56},{56,48},{64,72... | collective-permute-start | bytes 786440 | tf_op jit(solution)/shard_map/ppermute | solution.py:38
  48.6 19.4 %collective-permute-start.13 = (bf16[8,256,128]{2,1,0:T(8,128)(2,1)S(1)}, bf16[8,256,128]{2,1,0:T(8,128)(2,1)S(1)}, u32[]{:S(2)}, u32[]{:S(2)}) collective-permute-start(bf16[8,256,128]{2,1,0:T(8,128)(2,1)S(1)} %pad_maximum_fusion.1), channel_id=1, source_target_pairs={{0,8},{8,0},{16,24},{24,16},{32,40},{40,32},{48,56},{56,48},{64,72... | collective-permute-start | bytes 1572872 | tf_op jit(solution)/shard_map/ppermute | solution.py:38
  49.2 8.4 %collective-permute-start.15 = (bf16[2,256,128]{2,1,0:T(8,128)(2,1)S(1)}, bf16[2,256,128]{2,1,0:T(8,128)(2,1)S(1)}, u32[]{:S(2)}, u32[]{:S(2)}) collective-permute-start(bf16[2,256,128]{2,1,0:T(8,128)(2,1)S(1)} %slice.11), channel_id=1, source_target_pairs={{0,8},{8,16},{16,24},{24,32},{32,40},{40,48},{48,56},{56,64},{64,7... | collective-permute-start | bytes 393224 | tf_op jit(solution)/shard_map/ppermute | solution.py:24
  57.6 10.4 %copy-start.15 = (bf16[2,256,128]{2,1,0:T(8,128)(2,1)}, bf16[2,256,128]{2,1,0:T(8,128)(2,1)S(1)}, u32[]{:S(2)}) copy-start(bf16[2,256,128]{2,1,0:T(8,128)(2,1)S(1)} %collective-permute-done.15.refs_14_) | copy-start | bytes 393220
  57.6 7.6 %collective-permute-start.5 = (bf16[4,256,128]{2,1,0:T(8,128)(2,1)S(1)}, bf16[4,256,128]{2,1,0:T(8,128)(2,1)S(1)}, u32[]{:S(2)}, u32[]{:S(2)}) collective-permute-start(bf16[4,256,128]{2,1,0:T(8,128)(2,1)S(1)} %collective-permute-done.4.refs_3_), channel_id=1, source_target_pairs={{0,32},{8,232},{16,48},{24,248},{32,64},{40,8},{48,80},{56,24},{64... | collective-permute-start | bytes 786440 | tf_op jit(solution)/shard_map/ppermute | solution.py:38
  57.6 10.4 %copy-start.10 = (bf16[4,256,128]{2,1,0:T(8,128)(2,1)}, bf16[4,256,128]{2,1,0:T(8,128)(2,1)S(1)}, u32[]{:S(2)}) copy-start(bf16[4,256,128]{2,1,0:T(8,128)(2,1)S(1)} %collective-permute-done.11.refs_10_) | copy-start | bytes 786436
  57.6 7.6 %collective-permute-start.14 = (bf16[4,256,128]{2,1,0:T(8,128)(2,1)S(1)}, bf16[4,256,128]{2,1,0:T(8,128)(2,1)S(1)}, u32[]{:S(2)}, u32[]{:S(2)}) collective-permute-start(bf16[4,256,128]{2,1,0:T(8,128)(2,1)S(1)} %collective-permute-done.11.refs_10_), channel_id=1, source_target_pairs={{0,8},{8,0},{16,24},{24,16},{32,40},{40,32},{48,56},{56,48},{64,72... | collective-permute-start | bytes 786440 | tf_op jit(solution)/shard_map/ppermute | solution.py:38
  57.7 10.3 %copy-start.11 = (bf16[4,256,128]{2,1,0:T(8,128)(2,1)}, bf16[4,256,128]{2,1,0:T(8,128)(2,1)S(1)}, u32[]{:S(2)}) copy-start(bf16[4,256,128]{2,1,0:T(8,128)(2,1)S(1)} %collective-permute-done.7.refs_6_) | copy-start | bytes 786436
  57.7 10.2 %collective-permute-start.12 = (bf16[4,256,128]{2,1,0:T(8,128)(2,1)S(1)}, bf16[4,256,128]{2,1,0:T(8,128)(2,1)S(1)}, u32[]{:S(2)}, u32[]{:S(2)}) collective-permute-start(bf16[4,256,128]{2,1,0:T(8,128)(2,1)S(1)} %collective-permute-done.11.refs_10_), channel_id=1, source_target_pairs={{0,32},{8,232},{16,48},{24,248},{32,64},{40,8},{48,80},{56,24},{64... | collective-permute-start | bytes 786440 | tf_op jit(solution)/shard_map/ppermute | solution.py:38
  (8 other events, 17.8 us)
